TPU v7x, 256 devices: a whole 4x4x8 slice. The times are simulated.
256 devices in a mesh: owner: 64 (over z, y, core), neg: 4 (over x).
Axes of the slice: x: 4, y: 4, z: 8, core: 2. Of those that a mesh axis runs over, the one named last changes fastest.
Arguments:
- nbr_ids: int32 [2048, 50], P(('owner', 'neg')), may hold values from 0 to 262143, as said below
- visit_counts: int32 [2048, 50], P(('owner', 'neg')), may hold values from 1 to 32
- self_ids: int32 [2048], P(('owner', 'neg')), may hold values from 0 to 262143, as said below
- pos_ids: int32 [2048], P(('owner', 'neg')), may hold values from 0 to 262143, as said below
- neg_ids: int32 [2048, 128], P(('owner', 'neg')), may hold values from 0 to 262143, as said below
- table: bfloat16 [262144, 1024], P('owner'), may hold values from -6 to 6
- w_pool: bfloat16 [1024, 1024], replicated, may hold values from -0.1875 to 0.1875
- b_pool: float32 [1024], replicated, may hold values from -3 to 3
- w_conv: bfloat16 [2048, 1024], replicated, may hold values from -0.125 to 0.125
- b_conv: float32 [1024], replicated, may hold values from -3 to 3
Outputs:
- query_embed: float32 [2048, 1024], P(('owner', 'neg'))
- loss: float32 [], replicated
- grad_pool_w: float32 [1024, 1024], P('owner')
- grad_pool_b: float32 [1024], replicated
- grad_conv_w: float32 [2048, 1024], P('owner')
- grad_conv_b: float32 [1024], replicated
Inputs may be any that keep to these rules, and one draw needn't show every extreme that they name: `nbr_ids`: page p belongs to owner p // 4096. Among the 400 entries of one device's rows, at most 16 belong to one owner. `neg_ids`: taken together, the self, positive and negative ids of one device's 8 queries name at most 36 pages of one owner. `self_ids`: counted with the negatives, see neg_ids. `pos_ids`: counted with the negatives, see neg_ids.
All inputs are finite; a program needn't handle non-finite values.
Results may differ from a plain program's by a relative error of at most 0.008.
Values may be sent and summed in bfloat16 or wider, within the bound.
No kernel may reach another device: no remote copies, remote signals or barrier semaphores. Data moves between devices by JAX's collectives and lax.ppermute only.
A program may use at most 128 MiB of HBM per device.

v0:
```python
import jax
import jax.numpy as jnp
from jax import lax
from jax.sharding import PartitionSpec as P

margin_value = 0.5


def silu_slope(values):
    sig = jax.nn.sigmoid(values)
    return sig * (1.0 + values * (1.0 - sig))


def forward(pooled, self_rows, w_pool, b_pool, w_conv, b_conv):
    pooled_b = pooled.astype(jnp.bfloat16)
    pre_pool = jnp.dot(pooled_b, w_pool, preferred_element_type=jnp.float32) + b_pool
    neighbour = jax.nn.silu(pre_pool).astype(jnp.bfloat16)
    joined = jnp.concatenate([self_rows, neighbour], axis=1)
    pre_conv = jnp.dot(joined, w_conv, preferred_element_type=jnp.float32) + b_conv
    hidden = jax.nn.silu(pre_conv)
    inverse = lax.rsqrt(jnp.sum(hidden * hidden, axis=1, keepdims=True) + 1e-05)
    embedding = hidden * inverse
    return (pooled_b, pre_pool, joined, pre_conv, inverse, embedding)


def margin_terms(neg_scores, pos_scores, loss_scale):
    margins = neg_scores - pos_scores[:, None] + margin_value
    loss_part = jnp.sum(jax.nn.softplus(margins)) * loss_scale
    slope_b = jax.nn.sigmoid(margins).astype(jnp.bfloat16)
    slope_total = jnp.sum(slope_b.astype(jnp.float32), axis=1, keepdims=True)
    return (loss_part, slope_b, slope_total)


def backward(d_embed, embedding, inverse, pre_conv, pre_pool, joined, pooled_b, w_conv, grad_scale):
    width = embedding.shape[1]
    contract_rows = (((0,), (0,)), ((), ()))
    radial = jnp.sum(d_embed * embedding, axis=1, keepdims=True)
    d_pre_conv = silu_slope(pre_conv) * inverse * (d_embed - embedding * radial) * grad_scale
    d_conv_b = d_pre_conv.astype(jnp.bfloat16)
    grad_conv_w = lax.dot_general(
        joined, d_conv_b, contract_rows, preferred_element_type=jnp.float32
    )
    grad_conv_b = jnp.sum(d_pre_conv, axis=0)
    d_neighbour = lax.dot_general(
        d_conv_b, w_conv[width:], (((1,), (1,)), ((), ())), preferred_element_type=jnp.float32
    )
    d_pre_pool = silu_slope(pre_pool) * d_neighbour
    d_pool_b = d_pre_pool.astype(jnp.bfloat16)
    grad_pool_w = lax.dot_general(
        pooled_b, d_pool_b, contract_rows, preferred_element_type=jnp.float32
    )
    grad_pool_b = jnp.sum(d_pre_pool, axis=0)
    return (grad_pool_w, grad_pool_b, grad_conv_w, grad_conv_b)


def bucket(page_list, owners, rows_per):
    owner_of = page_list // rows_per
    local_row = page_list - owner_of * rows_per
    one_hot = (owner_of[:, None] == jnp.arange(owners, dtype=jnp.int32)[None, :]).astype(jnp.int32)
    slot_of = jnp.sum((jnp.cumsum(one_hot, axis=0) - 1) * one_hot, axis=1)
    return (owner_of, slot_of, local_row)


def local(nbr_ids, visit_counts, self_ids, pos_ids, neg_ids, table, w_pool, b_pool, w_conv, b_conv):
    owners = lax.axis_size("owner")
    groups = lax.axis_size("neg")
    rows_per = table.shape[0]
    width = table.shape[1]
    queries, fan_count = nbr_ids.shape
    neg_count = neg_ids.shape[1]
    counts_f = visit_counts.astype(jnp.float32)
    weights = counts_f / jnp.sum(counts_f, axis=1, keepdims=True)
    flat_ids = nbr_ids.reshape(-1)
    capacity = 2 * (flat_ids.shape[0] // owners) + 4
    owner_of, slot_of, local_row = bucket(flat_ids, owners, rows_per)
    requests = jnp.zeros((owners, capacity), jnp.int32).at[owner_of, slot_of].set(local_row)
    returned = lax.all_to_all(
        table[lax.all_to_all(requests, "owner", split_axis=0, concat_axis=0, tiled=True)],
        "owner",
        split_axis=0,
        concat_axis=0,
        tiled=True,
    )
    nbr_rows = returned[owner_of, slot_of].reshape(queries, fan_count, width)
    pooled = jnp.sum(weights[:, :, None] * nbr_rows.astype(jnp.float32), axis=1)
    page_cap = 2 * (queries * (neg_count + 2) // owners) + 4
    total_queries = queries * owners * groups
    grad_scale = 1.0 / neg_count
    loss_scale = 1.0 / (total_queries * neg_count)
    page_list = jnp.concatenate([self_ids, pos_ids, neg_ids.reshape(-1)])
    page_owner, page_slot, page_row = bucket(page_list, owners, rows_per)
    page_requests = jnp.zeros((owners, page_cap), jnp.int32).at[page_owner, page_slot].set(page_row)
    page_back = lax.all_to_all(
        table[lax.all_to_all(page_requests, "owner", split_axis=0, concat_axis=0, tiled=True)],
        "owner",
        split_axis=0,
        concat_axis=0,
        tiled=True,
    )
    page_rows = page_back[page_owner, page_slot]
    self_rows = page_rows[:queries]
    pos_rows = page_rows[queries : 2 * queries]
    neg_rows = page_rows[2 * queries :].reshape(queries, neg_count, width)
    pooled_b, pre_pool, joined, pre_conv, inverse, embedding = forward(
        pooled, self_rows, w_pool, b_pool, w_conv, b_conv
    )
    embed_b = embedding.astype(jnp.bfloat16)
    neg_scores = jnp.einsum("qe,qne->qn", embed_b, neg_rows, preferred_element_type=jnp.float32)
    pos_scores = jnp.einsum("qe,qe->q", embed_b, pos_rows, preferred_element_type=jnp.float32)
    loss_part, slope_b, slope_total = margin_terms(neg_scores, pos_scores, loss_scale)
    d_embed = jnp.einsum(
        "qn,qne->qe", slope_b, neg_rows, preferred_element_type=jnp.float32
    ) - slope_total * pos_rows.astype(jnp.float32)
    pool_wgrad, pool_bgrad, conv_wgrad, conv_bgrad = backward(
        d_embed, embedding, inverse, pre_conv, pre_pool, joined, pooled_b, w_conv, grad_scale
    )
    pool_rows, conv_rows = (
        lax.psum_scatter(pool_wgrad, "owner", scatter_dimension=0, tiled=True),
        lax.psum_scatter(conv_wgrad, "owner", scatter_dimension=0, tiled=True),
    )
    grad_pool_w, grad_conv_w = lax.psum((pool_rows, conv_rows), "neg")
    loss_sum, grad_pool_b, grad_conv_b = lax.psum(
        (loss_part, pool_bgrad, conv_bgrad), ("owner", "neg")
    )
    return (embedding, loss_sum, grad_pool_w, grad_pool_b, grad_conv_w, grad_conv_b)


def solution(mesh):
    return jax.shard_map(
        local,
        mesh=mesh,
        in_specs=(
            P(("owner", "neg"), None),
            P(("owner", "neg"), None),
            P(("owner", "neg")),
            P(("owner", "neg")),
            P(("owner", "neg"), None),
            P("owner", None),
            P(),
            P(),
            P(),
            P(),
        ),
        out_specs=(P(("owner", "neg"), None), P(), P("owner", None), P(), P("owner", None), P()),
        check_vma=False,
    )
```

profile of v0, /device:TPU:6, one launch (start us, length us, event | category | flops | bytes accessed | tf_op | source)
XLA Modules:
  0.0 706.0 jit_solution(14694739714923709557)
XLA Ops:
  7.2 0.9 reshape.482
  8.9 1.2 reduce-window.16
  10.6 21.3 %scatter_fusion = s32[64,16]{0,1:T(8,128)S(1)} fusion(s32[64,16]{0,1:T(8,128)S(1)} %broadcast.319, s32[400]{0:T(512)S(1)} %bitcast.63, s32[400]{0:T(512)S(1)} %get-tuple-element.25), kind=kCustom, calls=%fused_computation.4 | custom fusion | bytes 8000 | tf_op jit(solution)/shard_map/scatter | solution.py:76
  32.6 12.1 %all-to-all-start.2 = ((s32[64,1,16]{2,1,0:T(1,128)}), s32[64,1,16]{2,1,0:T(1,128)S(1)}, u32[]{:S(2)}, u32[]{:S(2)}) async-start(s32[64,1,16]{2,1,0:T(1,128)} %copy.43), calls=%async_computation.2 | async-start | bytes 65536 | tf_op jit(solution)/shard_map/all_to_all | solution.py:78
  45.0 18.1 %reduce-window.14 = s32[64,9,128]{2,1,0:T(8,128)S(1)} reduce-window(s32[64,9,128]{2,1,0:T(8,128)S(1)} %reshape.490, s32[]{:T(128)} %constant.30.clone.1), window={size=1x1x128 pad=0_0x0_0x127_0}, to_apply=%region_0.0 | reduce-window | flops 9363456 | bytes 589828 | tf_op jit(solution)/shard_map/reduce-window
  64.5 6.5 scatter_custom_fusion.1
  71.8 10.3 %all-to-all-start = ((s32[64,1,36]{2,1,0:T(1,128)}), s32[64,1,36]{2,1,0:T(1,128)S(1)}, u32[]{:S(2)}, u32[]{:S(2)}) async-start(s32[64,1,36]{2,1,0:T(1,128)} %copy.39), calls=%async_computation | async-start | bytes 65536 | tf_op jit(solution)/shard_map/all_to_all | solution.py:94
  82.2 10.5 %gather_fusion.2 = bf16[1024,1024]{1,0:T(8,128)(2,1)} fusion(bf16[4096,1024]{1,0:T(8,128)(2,1)} %param.15, s32[1024]{0:T(1024)S(1)} %broadcast_clamp_fusion), kind=kCustom, calls=%fused_computation.2 | custom fusion | bytes 4198400 | tf_op jit(solution)/shard_map/gather | solution.py:78
  92.7 10.6 %all-to-all-start.3 = ((bf16[64,16,1024]{2,1,0:T(8,128)(2,1)}), bf16[64,16,1024]{2,1,0:T(8,128)(2,1)}, u32[]{:S(2)}, u32[]{:S(2)}) async-start(bf16[64,16,1024]{2,1,0:T(8,128)(2,1)} %bitcast.66), calls=%async_computation.3 | async-start | bytes 4194304 | tf_op jit(solution)/shard_map/all_to_all | solution.py:77
  103.4 15.5 %gather_fusion = bf16[2304,1024]{1,0:T(8,128)(2,1)} fusion(bf16[4096,1024]{1,0:T(8,128)(2,1)} %param.15, s32[3072]{0:T(1024)S(1)} %pad_clamp_fusion), kind=kCustom, calls=%fused_computation | custom fusion | bytes 9446400 | tf_op jit(solution)/shard_map/gather | solution.py:94
  118.8 7.2 %reshape.494 = bf16[64,36,1024]{2,1,0:T(8,128)(2,1)} reshape(bf16[2304,1024]{1,0:T(8,128)(2,1)} %gather_fusion) | data formatting | bytes 9437184 | tf_op jit(solution)/shard_map/gather | solution.py:94
  126.0 28.4 %all-to-all-done.3 = bf16[64,16,1024]{2,1,0:T(8,128)(2,1)} async-done(((bf16[64,16,1024]{2,1,0:T(8,128)(2,1)}), bf16[64,16,1024]{2,1,0:T(8,128)(2,1)}, u32[]{:S(2)}, u32[]{:S(2)}) %all-to-all-start.3) | async-done | bytes 2097184 | tf_op jit(solution)/shard_map/all_to_all | solution.py:77
  154.4 5.9 all-to-all-start.1
  160.5 10.8 %gather_fusion.3 = bf16[400,1024]{1,0:T(8,128)(2,1)S(1)} fusion(bf16[64,16,1024]{2,1,0:T(8,128)(2,1)} %all-to-all-done.3, s32[400]{0:T(512)S(1)} %bitcast.62), kind=kCustom, calls=%fused_computation.3 | custom fusion | bytes 1641600 | tf_op jit(solution)/shard_map/gather | solution.py:84
  171.3 1.4 reshape.492
  172.7 1.8 multiply_reduce_fusion
  175.0 104.1 %all-to-all-done.1 = bf16[64,36,1024]{2,1,0:T(8,128)(2,1)} async-done(((bf16[64,36,1024]{2,1,0:T(8,128)(2,1)}), bf16[64,36,1024]{2,1,0:T(8,128)(2,1)}, u32[]{:S(2)}, u32[]{:S(2)}) %all-to-all-start.1) | async-done | bytes 4718624 | tf_op jit(solution)/shard_map/all_to_all | solution.py:93
  279.1 7.2 %copy.40 = bf16[64,36,1024]{2,0,1:T(8,128)(2,1)} copy(bf16[64,36,1024]{2,1,0:T(8,128)(2,1)} %all-to-all-done.1) | data formatting | bytes 9437184 | tf_op jit(solution)/shard_map/all_to_all | solution.py:93
  286.3 28.6 %gather_fusion.1 = bf16[1040,1024]{1,0:T(8,128)(2,1)} fusion(bf16[64,36,1024]{2,0,1:T(8,128)(2,1)} %copy.40, s32[1040]{0:T(1024)S(1)} %get-tuple-element.17), kind=kCustom, calls=%fused_computation.1 | custom fusion | bytes 4268160 | tf_op jit(solution)/shard_map/gather | solution.py:100
  314.9 0.9 slice.53
  315.8 2.2 slice.56
  318.0 0.8 multiply_reduce_fusion.2
  318.8 0.9 fusion.9
  321.4 0.9 multiply_reduce_fusion.1
  322.4 0.8 fusion.33
  323.8 2.7 fusion.15
  326.6 4.5 fusion.14
  331.2 136.1 %reduce-scatter.3.cloned.1.call-done = f32[16,1024]{1,0:T(8,128)} async-done(((f32[1024,1024]{1,0:T(8,128)}), f32[16,1024]{1,0:T(8,128)}) %reduce-scatter.3.cloned.1.call-update) | async-done | bytes 65552 | tf_op jit(solution)/shard_map/reduce_scatter | solution.py:118
  467.4 154.9 %reduce-scatter.5.cloned.1.call-done = f32[32,1024]{1,0:T(8,128)} async-done(((f32[2048,1024]{1,0:T(8,128)}), f32[32,1024]{1,0:T(8,128)}) %reduce-scatter.5.cloned.1.call-update) | async-done | bytes 131088 | tf_op jit(solution)/shard_map/reduce_scatter | solution.py:119
  622.9 73.5 %all-reduce.2 = (f32[]{:T(128)}, f32[1024]{0:T(1024)}, f32[1024]{0:T(1024)}) all-reduce(f32[]{:T(128)S(6)} %mul.103, f32[1024]{0:T(1024)S(1)} %get-tuple-element.31, f32[1024]{0:T(1024)S(1)} %get-tuple-element.11), channel_id=1, replica_groups=mesh['owner'=64,'neg'=4] {'owner','neg'}, use_global_device_ids=true, to_apply=%region_12.13 | all-reduce | flops 2049 | bytes 16392 | tf_op jit(solution)/shard_map/psum | solution.py:122
  696.5 1.5 copy.72
  698.0 1.6 copy.73
  (77 shorter events, 7.7 us)
Async XLA Ops:
  7.2 167.4 %copy-start = (bf16[1024,1024]{1,0:T(8,128)(2,1)S(1)}, bf16[1024,1024]{1,0:T(8,128)(2,1)}, u32[]{:S(2)}) copy-start(bf16[1024,1024]{1,0:T(8,128)(2,1)} %param.16) | copy-start | bytes 6291460
  10.6 34.1 %copy-start.3 = (s32[8,128]{1,0:T(8,128)S(1)}, s32[8,128]{1,0:T(8,128)}, u32[]{:S(2)}) copy-start(s32[8,128]{1,0:T(8,128)} %param.14) | copy-start | bytes 12292
  10.6 34.1 %copy-start.7 = (s32[8]{0:T(128)S(1)}, s32[8]{0:T(128)}, u32[]{:S(2)}) copy-start(s32[8]{0:T(128)} %param.12) | copy-start | bytes 100
  10.6 34.1 %copy-start.8 = (s32[8]{0:T(128)S(1)}, s32[8]{0:T(128)}, u32[]{:S(2)}) copy-start(s32[8]{0:T(128)} %param.13) | copy-start | bytes 100
  32.6 39.2 %all-to-all-start.2 = ((s32[64,1,16]{2,1,0:T(1,128)}), s32[64,1,16]{2,1,0:T(1,128)S(1)}, u32[]{:S(2)}, u32[]{:S(2)}) async-start(s32[64,1,16]{2,1,0:T(1,128)} %copy.43), calls=%async_computation.2 | async-start | bytes 65536 | tf_op jit(solution)/shard_map/all_to_all | solution.py:78
  63.1 1.2 copy-start.10
  63.1 1.3 copy-start.9
  71.8 20.9 %all-to-all-start = ((s32[64,1,36]{2,1,0:T(1,128)}), s32[64,1,36]{2,1,0:T(1,128)S(1)}, u32[]{:S(2)}, u32[]{:S(2)}) async-start(s32[64,1,36]{2,1,0:T(1,128)} %copy.39), calls=%async_computation | async-start | bytes 65536 | tf_op jit(solution)/shard_map/all_to_all | solution.py:94
  92.7 61.7 %all-to-all-start.3 = ((bf16[64,16,1024]{2,1,0:T(8,128)(2,1)}), bf16[64,16,1024]{2,1,0:T(8,128)(2,1)}, u32[]{:S(2)}, u32[]{:S(2)}) async-start(bf16[64,16,1024]{2,1,0:T(8,128)(2,1)} %bitcast.66), calls=%async_computation.3 | async-start | bytes 4194304 | tf_op jit(solution)/shard_map/all_to_all | solution.py:77
  126.0 34.3 %copy-start.4 = (s32[8,50]{1,0:T(8,128)S(1)}, s32[8,50]{1,0:T(8,128)}, u32[]{:S(2)}) copy-start(s32[8,50]{1,0:T(8,128)} %param.11) | copy-start | bytes 4804
  154.4 124.7 %all-to-all-start.1 = ((bf16[64,36,1024]{2,1,0:T(8,128)(2,1)}), bf16[64,36,1024]{2,1,0:T(8,128)(2,1)}, u32[]{:S(2)}, u32[]{:S(2)}) async-start(bf16[64,36,1024]{2,1,0:T(8,128)(2,1)} %reshape.494), calls=%async_computation.1 | async-start | bytes 10485760 | tf_op jit(solution)/shard_map/all_to_all | solution.py:93
  160.3 307.1 %reduce-scatter.3.cloned.1.call-start = ((), (), s32[]{:S(2)}) async-start(), calls=%async_computation.6 | async-start | bytes 4259840 | tf_op jit(solution)/shard_map/reduce_scatter | solution.py:118
  171.3 3.2 copy-start.5
  314.9 3.1 copy-start.1
  314.9 3.1 copy-start.6
  319.7 2.7 copy-start.2
  326.6 295.7 %reduce-scatter.5.cloned.1.call-start = ((), (), s32[]{:S(2)}) async-start(), calls=%async_computation.7 | async-start | bytes 8519680 | tf_op jit(solution)/shard_map/reduce_scatter | solution.py:119
  331.2 365.3 %all-reduce.6.cloned.1.call-start = ((), (), s32[]{:S(2)}) async-start(), calls=%async_computation.8 | async-start | bytes 393216 | tf_op jit(solution)/shard_map/psum | solution.py:121
Sparse Core Ops, SparseCore 0:
  326.7 140.6 reduce-scatter.2
  471.6 150.6 reduce-scatter.4
  624.6 43.6 all-reduce.5
where the time goes:
time: 709 us; the launch traced here: 706 us
  waiting for transfers between devices  424 us (60%)
  local copies, waits for them, and re-layouts  120 us (17%)
  blocking collectives  73.5 us (10%)
  starting transfers between devices  39 us (6%)
  other arithmetic  25.6 us (4%)
  between operations  14.8 us (2%)
  matrix products  10.1 us (1%)
    reduce_scatter x1, waiting for transfers between devices, local(): lax.psum_scatter(conv_wgrad, 'owner', scatter_dimension=0, tiled=True)  155 us
    reduce_scatter x1, waiting for transfers between devices, local(): lax.psum_scatter(pool_wgrad, 'owner', scatter_dimension=0, tiled=True)  136 us
    all_to_all x1, waiting for transfers between devices, local(): lax.all_to_all(table[lax.all_to_all(page_requests, 'owner', split_axis=0,...  104 us
    psum x1, blocking collectives, local(): lax.psum((loss_part, pool_bgrad, conv_bgrad), ('owner', 'neg'))  73.5 us
    gather x1, local copies, waits for them, and re-layouts, local(): page_rows = page_back[page_owner, page_slot]  28.6 us
    all_to_all x1, waiting for transfers between devices, local(): lax.all_to_all(table[lax.all_to_all(requests, 'owner', split_axis=0, conc...  28.4 us
    gather x2, local copies, waits for them, and re-layouts, local(): table[lax.all_to_all(page_requests, 'owner', split_axis=0, concat_axis=0,...  22.7 us
    scatter x1, local copies, waits for them, and re-layouts, local(): jnp.zeros((owners, capacity), jnp.int32).at[owner_of, slot_of]  21.3 us
  transfers between devices with their start and end apart: 7, of which 4 were waited for; matrix products, arithmetic and copies ran while one was open for 11% of the time, Pallas kernels for 0%

commit v1 on v0

--- a/solution.py
+++ b/solution.py
@@ -31,26 +31,49 @@
     return (loss_part, slope_b, slope_total)
 
 
-def backward(d_embed, embedding, inverse, pre_conv, pre_pool, joined, pooled_b, w_conv, grad_scale):
+def backward_factors(d_embed, embedding, inverse, pre_conv, pre_pool, w_conv, grad_scale):
     width = embedding.shape[1]
-    contract_rows = (((0,), (0,)), ((), ()))
     radial = jnp.sum(d_embed * embedding, axis=1, keepdims=True)
     d_pre_conv = silu_slope(pre_conv) * inverse * (d_embed - embedding * radial) * grad_scale
     d_conv_b = d_pre_conv.astype(jnp.bfloat16)
-    grad_conv_w = lax.dot_general(
-        joined, d_conv_b, contract_rows, preferred_element_type=jnp.float32
-    )
     grad_conv_b = jnp.sum(d_pre_conv, axis=0)
     d_neighbour = lax.dot_general(
         d_conv_b, w_conv[width:], (((1,), (1,)), ((), ())), preferred_element_type=jnp.float32
     )
     d_pre_pool = silu_slope(pre_pool) * d_neighbour
     d_pool_b = d_pre_pool.astype(jnp.bfloat16)
-    grad_pool_w = lax.dot_general(
-        pooled_b, d_pool_b, contract_rows, preferred_element_type=jnp.float32
+    grad_pool_b = jnp.sum(d_pre_pool, axis=0)
+    return (d_conv_b, d_pool_b, grad_pool_b, grad_conv_b)
+
+
+def weight_grads(joined, pooled_b, d_conv_b, d_pool_b):
+    owners = lax.axis_size("owner")
+    queries = joined.shape[0]
+    conv_rows = joined.shape[1] // owners
+    pool_rows = pooled_b.shape[1] // owners
+    left = jnp.concatenate(
+        [
+            joined.reshape(queries, owners, conv_rows).transpose(1, 0, 2),
+            pooled_b.reshape(queries, owners, pool_rows).transpose(1, 0, 2),
+        ],
+        axis=2,
     )
-    grad_pool_b = jnp.sum(d_pre_pool, axis=0)
-    return (grad_pool_w, grad_pool_b, grad_conv_w, grad_conv_b)
+    left = lax.all_to_all(left, "owner", split_axis=0, concat_axis=0, tiled=True)
+    left = left.reshape(owners * queries, conv_rows + pool_rows)
+    right = lax.all_gather(
+        jnp.concatenate([d_conv_b, d_pool_b], axis=1), "owner", axis=0, tiled=True
+    )
+    contract_rows = (((0,), (0,)), ((), ()))
+    conv_width = d_conv_b.shape[1]
+    conv_part = lax.dot_general(
+        left[:, :conv_rows], right[:, :conv_width], contract_rows,
+        preferred_element_type=jnp.float32,
+    )
+    pool_part = lax.dot_general(
+        left[:, conv_rows:], right[:, conv_width:], contract_rows,
+        preferred_element_type=jnp.float32,
+    )
+    return pool_part, conv_part
 
 
 def bucket(page_list, owners, rows_per):
@@ -111,14 +134,11 @@
     d_embed = jnp.einsum(
         "qn,qne->qe", slope_b, neg_rows, preferred_element_type=jnp.float32
     ) - slope_total * pos_rows.astype(jnp.float32)
-    pool_wgrad, pool_bgrad, conv_wgrad, conv_bgrad = backward(
-        d_embed, embedding, inverse, pre_conv, pre_pool, joined, pooled_b, w_conv, grad_scale
+    d_conv_b, d_pool_b, pool_bgrad, conv_bgrad = backward_factors(
+        d_embed, embedding, inverse, pre_conv, pre_pool, w_conv, grad_scale
     )
-    pool_rows, conv_rows = (
-        lax.psum_scatter(pool_wgrad, "owner", scatter_dimension=0, tiled=True),
-        lax.psum_scatter(conv_wgrad, "owner", scatter_dimension=0, tiled=True),
-    )
-    grad_pool_w, grad_conv_w = lax.psum((pool_rows, conv_rows), "neg")
+    pool_part, conv_part = weight_grads(joined, pooled_b, d_conv_b, d_pool_b)
+    grad_pool_w, grad_conv_w = lax.psum((pool_part, conv_part), "neg")
     loss_sum, grad_pool_b, grad_conv_b = lax.psum(
         (loss_part, pool_bgrad, conv_bgrad), ("owner", "neg")
     )

time: 709 us -> 492 us (0.69)
  waiting for transfers between devices: 424 us -> 190 us
  blocking collectives: 73.5 us -> 89.9 us
    reduce_scatter x2 -> x0, waiting for transfers between devices: 291 us -> none  [the longest x1 155 us: local(): lax.psum_scatter(conv_wgrad, 'owner', scatter_dimension=0, tiled=True)]
    all_gather x0 -> x1, waiting for transfers between devices: none -> 57.6 us  [weight_grads(): lax.all_gather(jnp.concatenate([d_conv_b, d_pool_b], axis=1), 'owner', ax...]
    all_to_all x0 -> x1, blocking collectives: none -> 15.1 us  [weight_grads(): lax.all_to_all(left, 'owner', split_axis=0, concat_axis=0, tiled=True)]
  transfers between devices with their start and end apart: 7 -> 6, of which waited for: 4 -> 3; matrix products, arithmetic and copies ran while one was open for 11% -> 15% of each run, Pallas kernels for 0% -> 0%
where the time goes in v1:
time: 492 us; the launch traced here: 489 us
  waiting for transfers between devices  190 us (39%)
  local copies, waits for them, and re-layouts  121 us (25%)
  blocking collectives  89.9 us (18%)
  starting transfers between devices  39.1 us (8%)
  other arithmetic  26.3 us (5%)
  between operations  15.1 us (3%)
  matrix products  7.26 us (1%)
    all_to_all x1, waiting for transfers between devices, local(): lax.all_to_all(table[lax.all_to_all(page_requests, 'owner', split_axis=0,...  104 us
    psum x1, blocking collectives, local(): lax.psum((loss_part, pool_bgrad, conv_bgrad), ('owner', 'neg'))  74.8 us
    all_gather x1, waiting for transfers between devices, weight_grads(): lax.all_gather(jnp.concatenate([d_conv_b, d_pool_b], axis=1), 'owner', ax...  57.6 us
    gather x1, local copies, waits for them, and re-layouts, local(): page_rows = page_back[page_owner, page_slot]  28.6 us
    all_to_all x1, waiting for transfers between devices, local(): lax.all_to_all(table[lax.all_to_all(requests, 'owner', split_axis=0, conc...  28.4 us
    gather x2, local copies, waits for them, and re-layouts, local(): table[lax.all_to_all(page_requests, 'owner', split_axis=0, concat_axis=0,...  22.7 us
    scatter x1, local copies, waits for them, and re-layouts, local(): jnp.zeros((owners, capacity), jnp.int32).at[owner_of, slot_of]  21.3 us
    another operation x8, other arithmetic  19.7 us
  transfers between devices with their start and end apart: 6, of which 3 were waited for; matrix products, arithmetic and copies ran while one was open for 15% of the time, Pallas kernels for 0%

profile of v1, /device:TPU:6, one launch (start us, length us, event | category | flops | bytes accessed | tf_op | source)
XLA Modules:
  0.0 488.5 jit_solution(18082749127227649497)
XLA Ops:
  7.2 0.9 reshape.491
  8.9 1.2 reduce-window.16
  10.6 21.3 %scatter_fusion = s32[64,16]{0,1:T(8,128)S(1)} fusion(s32[64,16]{0,1:T(8,128)S(1)} %broadcast.319, s32[400]{0:T(512)S(1)} %bitcast.63, s32[400]{0:T(512)S(1)} %get-tuple-element.27), kind=kCustom, calls=%fused_computation.4 | custom fusion | bytes 8000 | tf_op jit(solution)/shard_map/scatter | solution.py:99
  32.6 12.1 %all-to-all-start.2 = ((s32[64,1,16]{2,1,0:T(1,128)}), s32[64,1,16]{2,1,0:T(1,128)S(1)}, u32[]{:S(2)}, u32[]{:S(2)}) async-start(s32[64,1,16]{2,1,0:T(1,128)} %copy.46), calls=%async_computation.2 | async-start | bytes 65536 | tf_op jit(solution)/shard_map/all_to_all | solution.py:101
  45.0 18.1 %reduce-window.14 = s32[64,9,128]{2,1,0:T(8,128)S(1)} reduce-window(s32[64,9,128]{2,1,0:T(8,128)S(1)} %reshape.501, s32[]{:T(128)} %constant.30.clone.1), window={size=1x1x128 pad=0_0x0_0x127_0}, to_apply=%region_0.0 | reduce-window | flops 9363456 | bytes 589828 | tf_op jit(solution)/shard_map/reduce-window
  64.5 6.5 %scatter_custom_fusion.1 = s32[2304]{0:T(1024)S(1)} fusion(s32[1040]{0:T(1024)S(1)} %broadcast_select_fusion, s32[1040]{0:T(1024)S(1)} %get-tuple-element.24, s32[]{:T(128)} %constant.30.clone.1), kind=kCustom, calls=%fused_computation.79 | custom fusion | bytes 9220
  71.8 10.3 %all-to-all-start = ((s32[64,1,36]{2,1,0:T(1,128)}), s32[64,1,36]{2,1,0:T(1,128)S(1)}, u32[]{:S(2)}, u32[]{:S(2)}) async-start(s32[64,1,36]{2,1,0:T(1,128)} %copy.42), calls=%async_computation | async-start | bytes 65536 | tf_op jit(solution)/shard_map/all_to_all | solution.py:117
  82.2 10.5 %gather_fusion.2 = bf16[1024,1024]{1,0:T(8,128)(2,1)} fusion(bf16[4096,1024]{1,0:T(8,128)(2,1)} %param.15, s32[1024]{0:T(1024)S(1)} %broadcast_clamp_fusion), kind=kCustom, calls=%fused_computation.2 | custom fusion | bytes 4198400 | tf_op jit(solution)/shard_map/gather | solution.py:101
  92.7 10.6 %all-to-all-start.3 = ((bf16[64,16,1024]{2,1,0:T(8,128)(2,1)}), bf16[64,16,1024]{2,1,0:T(8,128)(2,1)}, u32[]{:S(2)}, u32[]{:S(2)}) async-start(bf16[64,16,1024]{2,1,0:T(8,128)(2,1)} %bitcast.66), calls=%async_computation.3 | async-start | bytes 4194304 | tf_op jit(solution)/shard_map/all_to_all | solution.py:100
  103.4 15.5 %gather_fusion = bf16[2304,1024]{1,0:T(8,128)(2,1)} fusion(bf16[4096,1024]{1,0:T(8,128)(2,1)} %param.15, s32[3072]{0:T(1024)S(1)} %pad_clamp_fusion), kind=kCustom, calls=%fused_computation | custom fusion | bytes 9446400 | tf_op jit(solution)/shard_map/gather | solution.py:117
  118.8 7.2 %reshape.505 = bf16[64,36,1024]{2,1,0:T(8,128)(2,1)} reshape(bf16[2304,1024]{1,0:T(8,128)(2,1)} %gather_fusion) | data formatting | bytes 9437184 | tf_op jit(solution)/shard_map/gather | solution.py:117
  126.0 28.4 %all-to-all-done.3 = bf16[64,16,1024]{2,1,0:T(8,128)(2,1)} async-done(((bf16[64,16,1024]{2,1,0:T(8,128)(2,1)}), bf16[64,16,1024]{2,1,0:T(8,128)(2,1)}, u32[]{:S(2)}, u32[]{:S(2)}) %all-to-all-start.3) | async-done | bytes 2097184 | tf_op jit(solution)/shard_map/all_to_all | solution.py:100
  154.4 5.9 %all-to-all-start.1 = ((bf16[64,36,1024]{2,1,0:T(8,128)(2,1)}), bf16[64,36,1024]{2,1,0:T(8,128)(2,1)}, u32[]{:S(2)}, u32[]{:S(2)}) async-start(bf16[64,36,1024]{2,1,0:T(8,128)(2,1)} %reshape.505), calls=%async_computation.1 | async-start | bytes 10485760 | tf_op jit(solution)/shard_map/all_to_all | solution.py:116
  160.5 10.8 %gather_fusion.3 = bf16[400,1024]{1,0:T(8,128)(2,1)S(1)} fusion(bf16[64,16,1024]{2,1,0:T(8,128)(2,1)} %all-to-all-done.3, s32[400]{0:T(512)S(1)} %bitcast.62), kind=kCustom, calls=%fused_computation.3 | custom fusion | bytes 1641600 | tf_op jit(solution)/shard_map/gather | solution.py:107
  171.3 1.4 reshape.503
  172.8 1.8 multiply_reduce_fusion
  175.0 104.1 %all-to-all-done.1 = bf16[64,36,1024]{2,1,0:T(8,128)(2,1)} async-done(((bf16[64,36,1024]{2,1,0:T(8,128)(2,1)}), bf16[64,36,1024]{2,1,0:T(8,128)(2,1)}, u32[]{:S(2)}, u32[]{:S(2)}) %all-to-all-start.1) | async-done | bytes 4718624 | tf_op jit(solution)/shard_map/all_to_all | solution.py:116
  279.1 7.2 %copy.43 = bf16[64,36,1024]{2,0,1:T(8,128)(2,1)} copy(bf16[64,36,1024]{2,1,0:T(8,128)(2,1)} %all-to-all-done.1) | data formatting | bytes 9437184 | tf_op jit(solution)/shard_map/all_to_all | solution.py:116
  286.3 28.6 %gather_fusion.1 = bf16[1040,1024]{1,0:T(8,128)(2,1)} fusion(bf16[64,36,1024]{2,0,1:T(8,128)(2,1)} %copy.43, s32[1040]{0:T(1024)S(1)} %get-tuple-element.17), kind=kCustom, calls=%fused_computation.1 | custom fusion | bytes 4268160 | tf_op jit(solution)/shard_map/gather | solution.py:123
  315.7 1.9 slice.72
  317.6 0.9 copy-done.1
  318.5 0.8 multiply_reduce_fusion.2
  319.3 0.9 fusion.15
  321.9 0.9 multiply_reduce_fusion.1
  322.8 0.8 fusion.30
  325.9 15.1 %all_to_all.39 = bf16[64,2,192]{2,1,0:T(2,128)(2,1)S(1)} all-to-all(bf16[64,2,192]{2,1,0:T(2,128)(2,1)S(1)} %reshape.556), channel_id=1, replica_groups=mesh['owner'=64,'neg'=4] {'owner'}, dimensions={0} | all-to-all | bytes 98304 | tf_op jit(solution)/shard_map/all_to_all | solution.py:61
  341.1 57.6 %all-gather.2.cloned.1.call-done = bf16[512,2048]{1,0:T(8,128)(2,1)} async-done(((bf16[8,2048]{1,0:T(8,128)(2,1)}), bf16[512,2048]{1,0:T(8,128)(2,1)}) %all-gather.2.cloned.1.call-update) | async-done | bytes 2097168 | tf_op jit(solution)/shard_map/all_gather | solution.py:63
  398.8 2.2 fusion.5
  401.0 2.2 fusion.7
  403.9 74.8 %all-reduce.2 = (f32[]{:T(128)}, f32[1024]{0:T(1024)}, f32[1024]{0:T(1024)}) all-reduce(f32[]{:T(128)S(6)} %mul.103, f32[1024]{0:T(1024)S(1)} %get-tuple-element.23, f32[1024]{0:T(1024)S(1)} %get-tuple-element.11), channel_id=1, replica_groups=mesh['owner'=64,'neg'=4] {'owner','neg'}, use_global_device_ids=true, to_apply=%region_12.13 | all-reduce | flops 2049 | bytes 16392 | tf_op jit(solution)/shard_map/psum | solution.py:142
  478.6 1.5 copy.76
  480.1 1.6 copy.77
  (83 shorter events, 10.0 us)
Async XLA Ops:
  7.2 167.4 %copy-start = (bf16[1024,1024]{1,0:T(8,128)(2,1)S(1)}, bf16[1024,1024]{1,0:T(8,128)(2,1)}, u32[]{:S(2)}) copy-start(bf16[1024,1024]{1,0:T(8,128)(2,1)} %param.16) | copy-start | bytes 6291460
  10.6 34.1 %copy-start.3 = (s32[8,128]{1,0:T(8,128)S(1)}, s32[8,128]{1,0:T(8,128)}, u32[]{:S(2)}) copy-start(s32[8,128]{1,0:T(8,128)} %param.14) | copy-start | bytes 12292
  10.6 34.1 %copy-start.7 = (s32[8]{0:T(128)S(1)}, s32[8]{0:T(128)}, u32[]{:S(2)}) copy-start(s32[8]{0:T(128)} %param.12) | copy-start | bytes 100
  10.6 34.1 %copy-start.8 = (s32[8]{0:T(128)S(1)}, s32[8]{0:T(128)}, u32[]{:S(2)}) copy-start(s32[8]{0:T(128)} %param.13) | copy-start | bytes 100
  32.6 39.2 %all-to-all-start.2 = ((s32[64,1,16]{2,1,0:T(1,128)}), s32[64,1,16]{2,1,0:T(1,128)S(1)}, u32[]{:S(2)}, u32[]{:S(2)}) async-start(s32[64,1,16]{2,1,0:T(1,128)} %copy.46), calls=%async_computation.2 | async-start | bytes 65536 | tf_op jit(solution)/shard_map/all_to_all | solution.py:101
  63.1 1.2 copy-start.10
  63.1 1.3 copy-start.9
  71.8 20.9 %all-to-all-start = ((s32[64,1,36]{2,1,0:T(1,128)}), s32[64,1,36]{2,1,0:T(1,128)S(1)}, u32[]{:S(2)}, u32[]{:S(2)}) async-start(s32[64,1,36]{2,1,0:T(1,128)} %copy.42), calls=%async_computation | async-start | bytes 65536 | tf_op jit(solution)/shard_map/all_to_all | solution.py:117
  92.7 61.7 %all-to-all-start.3 = ((bf16[64,16,1024]{2,1,0:T(8,128)(2,1)}), bf16[64,16,1024]{2,1,0:T(8,128)(2,1)}, u32[]{:S(2)}, u32[]{:S(2)}) async-start(bf16[64,16,1024]{2,1,0:T(8,128)(2,1)} %bitcast.66), calls=%async_computation.3 | async-start | bytes 4194304 | tf_op jit(solution)/shard_map/all_to_all | solution.py:100
  126.0 34.3 %copy-start.4 = (s32[8,50]{1,0:T(8,128)S(1)}, s32[8,50]{1,0:T(8,128)}, u32[]{:S(2)}) copy-start(s32[8,50]{1,0:T(8,128)} %param.11) | copy-start | bytes 4804
  154.4 124.7 %all-to-all-start.1 = ((bf16[64,36,1024]{2,1,0:T(8,128)(2,1)}), bf16[64,36,1024]{2,1,0:T(8,128)(2,1)}, u32[]{:S(2)}, u32[]{:S(2)}) async-start(bf16[64,36,1024]{2,1,0:T(8,128)(2,1)} %reshape.505), calls=%async_computation.1 | async-start | bytes 10485760 | tf_op jit(solution)/shard_map/all_to_all | solution.py:116
  160.3 238.5 %all-gather.2.cloned.1.call-start = ((), (), s32[]{:S(2)}) async-start(), calls=%async_computation.5 | async-start | bytes 2129920 | tf_op jit(solution)/shard_map/all_gather | solution.py:63
  171.3 3.2 copy-start.5
  286.3 31.3 %copy-start.6 = (f32[1024]{0:T(1024)S(1)}, f32[1024]{0:T(1024)}, u32[]{:S(2)}) copy-start(f32[1024]{0:T(1024)} %param.19) | copy-start | bytes 12292
  315.6 2.8 copy-start.1
  320.2 2.7 copy-start.2
  325.0 153.7 %all-reduce.6.cloned.1.call-start = ((), (), s32[]{:S(2)}) async-start(), calls=%async_computation.6 | async-start | bytes 393216 | tf_op jit(solution)/shard_map/psum | solution.py:141
Sparse Core Ops, SparseCore 0:
  325.1 73.6 all-gather.1
  403.3 42.9 all-reduce.5

commit v2 on v1

--- a/solution.py
+++ b/solution.py
@@ -46,7 +46,7 @@
     return (d_conv_b, d_pool_b, grad_pool_b, grad_conv_b)
 
 
-def weight_grads(joined, pooled_b, d_conv_b, d_pool_b):
+def weight_grads(joined, pooled_b, d_conv_b, d_pool_b, stats):
     owners = lax.axis_size("owner")
     queries = joined.shape[0]
     conv_rows = joined.shape[1] // owners
@@ -60,8 +60,17 @@
     )
     left = lax.all_to_all(left, "owner", split_axis=0, concat_axis=0, tiled=True)
     left = left.reshape(owners * queries, conv_rows + pool_rows)
-    right = lax.all_gather(
-        jnp.concatenate([d_conv_b, d_pool_b], axis=1), "owner", axis=0, tiled=True
+    stats_hi = stats.astype(jnp.bfloat16)
+    stats_lo = (stats - stats_hi.astype(jnp.float32)).astype(jnp.bfloat16)
+    payload = jnp.concatenate([d_conv_b, d_pool_b], axis=1)
+    payload = jnp.concatenate([payload, stats_hi, stats_lo], axis=0)
+    gathered = lax.all_gather(payload, "owner", axis=0)
+    right = gathered[:, :queries].reshape(owners * queries, payload.shape[1])
+    stat_rows = stats.shape[0]
+    stats_sum = jnp.sum(
+        gathered[:, queries : queries + stat_rows].astype(jnp.float32)
+        + gathered[:, queries + stat_rows :].astype(jnp.float32),
+        axis=0,
     )
     contract_rows = (((0,), (0,)), ((), ()))
     conv_width = d_conv_b.shape[1]
@@ -73,15 +82,24 @@
         left[:, conv_rows:], right[:, conv_width:], contract_rows,
         preferred_element_type=jnp.float32,
     )
-    return pool_part, conv_part
+    return pool_part, conv_part, stats_sum
 
 
-def bucket(page_list, owners, rows_per):
+def bucket(page_list, owners, rows_per, capacity):
+    count = page_list.shape[0]
     owner_of = page_list // rows_per
     local_row = page_list - owner_of * rows_per
-    one_hot = (owner_of[:, None] == jnp.arange(owners, dtype=jnp.int32)[None, :]).astype(jnp.int32)
-    slot_of = jnp.sum((jnp.cumsum(one_hot, axis=0) - 1) * one_hot, axis=1)
-    return (owner_of, slot_of, local_row)
+    one_hot = (owner_of[:, None] == jnp.arange(owners, dtype=jnp.int32)[None, :]).astype(jnp.bfloat16)
+    positions = jnp.arange(count, dtype=jnp.int32)
+    earlier = (positions[:, None] > positions[None, :]).astype(jnp.bfloat16)
+    before = jnp.dot(earlier, one_hot, preferred_element_type=jnp.float32)
+    slot_of = jnp.sum(before * one_hot.astype(jnp.float32), axis=1).astype(jnp.int32)
+    flat = owner_of * capacity + slot_of
+    select = (flat[:, None] == jnp.arange(owners * capacity, dtype=jnp.int32)[None, :]).astype(jnp.bfloat16)
+    parts = jnp.stack([local_row // 64, local_row % 64]).astype(jnp.bfloat16)
+    placed = jnp.dot(parts, select, preferred_element_type=jnp.float32).astype(jnp.int32)
+    requests = (placed[0] * 64 + placed[1]).reshape(owners, capacity)
+    return (owner_of, slot_of, requests)
 
 
 def local(nbr_ids, visit_counts, self_ids, pos_ids, neg_ids, table, w_pool, b_pool, w_conv, b_conv):
@@ -95,53 +113,68 @@
     weights = counts_f / jnp.sum(counts_f, axis=1, keepdims=True)
     flat_ids = nbr_ids.reshape(-1)
     capacity = 2 * (flat_ids.shape[0] // owners) + 4
-    owner_of, slot_of, local_row = bucket(flat_ids, owners, rows_per)
-    requests = jnp.zeros((owners, capacity), jnp.int32).at[owner_of, slot_of].set(local_row)
-    returned = lax.all_to_all(
-        table[lax.all_to_all(requests, "owner", split_axis=0, concat_axis=0, tiled=True)],
-        "owner",
-        split_axis=0,
-        concat_axis=0,
-        tiled=True,
-    )
-    nbr_rows = returned[owner_of, slot_of].reshape(queries, fan_count, width)
-    pooled = jnp.sum(weights[:, :, None] * nbr_rows.astype(jnp.float32), axis=1)
+    owner_of, slot_of, requests = bucket(flat_ids, owners, rows_per, capacity)
     page_cap = 2 * (queries * (neg_count + 2) // owners) + 4
     total_queries = queries * owners * groups
     grad_scale = 1.0 / neg_count
     loss_scale = 1.0 / (total_queries * neg_count)
     page_list = jnp.concatenate([self_ids, pos_ids, neg_ids.reshape(-1)])
-    page_owner, page_slot, page_row = bucket(page_list, owners, rows_per)
-    page_requests = jnp.zeros((owners, page_cap), jnp.int32).at[page_owner, page_slot].set(page_row)
-    page_back = lax.all_to_all(
-        table[lax.all_to_all(page_requests, "owner", split_axis=0, concat_axis=0, tiled=True)],
-        "owner",
-        split_axis=0,
-        concat_axis=0,
-        tiled=True,
+    page_owner, page_slot, page_requests = bucket(page_list, owners, rows_per, page_cap)
+    slots = capacity + page_cap
+    all_requests = jnp.concatenate([requests, page_requests], axis=1)
+    served = lax.all_to_all(all_requests, "owner", split_axis=0, concat_axis=0, tiled=True)
+    returned = lax.all_to_all(table[served], "owner", split_axis=0, concat_axis=0, tiled=True)
+    nbr_rows = returned[:, :capacity].reshape(owners * capacity, width)
+    page_rows = returned[:, capacity:].reshape(owners * page_cap, width)
+    nbr_flat = (owner_of * capacity + slot_of).reshape(queries, fan_count)
+    nbr_slots = jnp.arange(owners * capacity, dtype=jnp.int32)
+    pool_weights = jnp.sum(
+        jnp.where(nbr_flat[:, :, None] == nbr_slots[None, None, :], weights[:, :, None], 0.0), axis=1
     )
-    page_rows = page_back[page_owner, page_slot]
-    self_rows = page_rows[:queries]
-    pos_rows = page_rows[queries : 2 * queries]
-    neg_rows = page_rows[2 * queries :].reshape(queries, neg_count, width)
+    pooled = jnp.dot(
+        pool_weights, nbr_rows.astype(jnp.float32), precision=lax.Precision.HIGHEST,
+        preferred_element_type=jnp.float32,
+    )
+    page_flat = page_owner * page_cap + page_slot
+    page_slots = jnp.arange(owners * page_cap, dtype=jnp.int32)
+    self_flat = page_flat[:queries]
+    pos_flat = page_flat[queries : 2 * queries]
+    neg_flat = page_flat[2 * queries :].reshape(queries, neg_count)
+    pick = (jnp.stack([self_flat, pos_flat])[:, :, None] == page_slots[None, None, :]).astype(jnp.bfloat16)
+    picked = jnp.einsum("aqs,se->aqe", pick, page_rows, preferred_element_type=jnp.float32)
+    self_rows = picked[0].astype(jnp.bfloat16)
+    pos_rows = picked[1].astype(jnp.bfloat16)
     pooled_b, pre_pool, joined, pre_conv, inverse, embedding = forward(
         pooled, self_rows, w_pool, b_pool, w_conv, b_conv
     )
     embed_b = embedding.astype(jnp.bfloat16)
-    neg_scores = jnp.einsum("qe,qne->qn", embed_b, neg_rows, preferred_element_type=jnp.float32)
+    slot_scores = lax.dot_general(
+        embed_b, page_rows, (((1,), (1,)), ((), ())), preferred_element_type=jnp.float32
+    )
+    neg_scores = jnp.take_along_axis(slot_scores, neg_flat, axis=1)
     pos_scores = jnp.einsum("qe,qe->q", embed_b, pos_rows, preferred_element_type=jnp.float32)
     loss_part, slope_b, slope_total = margin_terms(neg_scores, pos_scores, loss_scale)
-    d_embed = jnp.einsum(
-        "qn,qne->qe", slope_b, neg_rows, preferred_element_type=jnp.float32
+    slope_slots = jnp.sum(
+        jnp.where(
+            neg_flat[:, :, None] == page_slots[None, None, :],
+            slope_b.astype(jnp.float32)[:, :, None],
+            0.0,
+        ),
+        axis=1,
+    ).astype(jnp.bfloat16)
+    d_embed = jnp.dot(
+        slope_slots, page_rows, preferred_element_type=jnp.float32
     ) - slope_total * pos_rows.astype(jnp.float32)
     d_conv_b, d_pool_b, pool_bgrad, conv_bgrad = backward_factors(
         d_embed, embedding, inverse, pre_conv, pre_pool, w_conv, grad_scale
     )
-    pool_part, conv_part = weight_grads(joined, pooled_b, d_conv_b, d_pool_b)
-    grad_pool_w, grad_conv_w = lax.psum((pool_part, conv_part), "neg")
-    loss_sum, grad_pool_b, grad_conv_b = lax.psum(
-        (loss_part, pool_bgrad, conv_bgrad), ("owner", "neg")
-    )
+    loss_row = jnp.zeros((2 * width,), jnp.float32).at[0].set(loss_part)
+    stats = jnp.stack([jnp.concatenate([conv_bgrad, pool_bgrad]), loss_row])
+    pool_part, conv_part, stats_sum = weight_grads(joined, pooled_b, d_conv_b, d_pool_b, stats)
+    grad_pool_w, grad_conv_w, stats_all = lax.psum((pool_part, conv_part, stats_sum), "neg")
+    grad_conv_b = stats_all[0, :width]
+    grad_pool_b = stats_all[0, width:]
+    loss_sum = stats_all[1, 0]
     return (embedding, loss_sum, grad_pool_w, grad_pool_b, grad_conv_w, grad_conv_b)
 
 

time: 492 us -> 431 us (0.88)
  waiting for transfers between devices: 190 us -> 265 us
  local copies, waits for them, and re-layouts: 121 us -> 68.6 us
  blocking collectives: 89.9 us -> 51 us
  starting transfers between devices: 39.1 us -> 6.1 us
  other arithmetic: 26.3 us -> 7.62 us
  matrix products: 7.26 us -> 15.6 us
    psum x1, blocking collectives: 74.8 us -> 13.9 us  [local(): lax.psum((pool_part, conv_part, stats_sum), 'neg')]
    psum x1, waiting for transfers between devices: 0.01 us -> 43 us  [local(): lax.psum((pool_part, conv_part, stats_sum), 'neg')]
    gather x5 -> x3, local copies, waits for them, and re-layouts: 72.6 us -> 36.3 us  [the longest x2 29.6 us: local(): table[served]]
    all_to_all x4 -> x1, starting transfers between devices: 38.8 us -> 5.84 us  [local(): lax.all_to_all(table[served], 'owner', split_axis=0, concat_axis=0, tiled...]
    all_to_all x4 -> x1, waiting for transfers between devices: 132 us -> 163 us  [local(): lax.all_to_all(table[served], 'owner', split_axis=0, concat_axis=0, tiled...]
    all_to_all x0 -> x1, blocking collectives: none -> 21.5 us  [local(): lax.all_to_all(all_requests, 'owner', split_axis=0, concat_axis=0, tiled=...]
    scatter x1 -> x0, local copies, waits for them, and re-layouts: 21.3 us -> none  [local(): jnp.zeros((owners, capacity), jnp.int32).at[owner_of, slot_of]]
    another operation x8 -> x5, other arithmetic: 19.7 us -> 0.12 us
  transfers between devices with their start and end apart: 6 -> 3, of which waited for: 3 -> 3; matrix products, arithmetic and copies ran while one was open for 15% -> 1% of each run, Pallas kernels for 0% -> 0%
where the time goes in v2:
time: 431 us; the launch traced here: 429 us
  waiting for transfers between devices  265 us (61%)
  local copies, waits for them, and re-layouts  68.6 us (16%)
  blocking collectives  51 us (12%)
  matrix products  15.6 us (4%)
  between operations  15.1 us (4%)
  other arithmetic  7.62 us (2%)
  starting transfers between devices  6.1 us (1%)
    all_to_all x1, waiting for transfers between devices, local(): lax.all_to_all(table[served], 'owner', split_axis=0, concat_axis=0, tiled...  163 us
    all_gather x1, waiting for transfers between devices, weight_grads(): gathered = lax.all_gather(payload, 'owner', axis=0)  59.5 us
    psum x1, waiting for transfers between devices, local(): lax.psum((pool_part, conv_part, stats_sum), 'neg')  43 us
    gather x2, local copies, waits for them, and re-layouts, local(): table[served]  29.6 us
    all_to_all x1, blocking collectives, local(): lax.all_to_all(all_requests, 'owner', split_axis=0, concat_axis=0, tiled=...  21.5 us
    all_to_all x1, blocking collectives, weight_grads(): lax.all_to_all(left, 'owner', split_axis=0, concat_axis=0, tiled=True)  15.6 us
    reshape x2, local copies, waits for them, and re-layouts, local(): page_rows = returned[:, capacity:].reshape(owners * page_cap, width)  14.4 us
    psum x1, blocking collectives, local(): lax.psum((pool_part, conv_part, stats_sum), 'neg')  13.9 us
  transfers between devices with their start and end apart: 3, of which 3 were waited for; matrix products, arithmetic and copies ran while one was open for 1% of the time, Pallas kernels for 0%

profile of v2, /device:TPU:6, one launch (start us, length us, event | category | flops | bytes accessed | tf_op | source)
XLA Modules:
  0.0 429.1 jit_solution(17860637634227320779)
XLA Ops:
  7.2 0.9 reshape.936
  8.1 0.8 reshape.935
  9.7 0.8 concatenate.104
  10.6 0.8 concatenate.100
  12.0 1.9 fusion.3
  14.2 21.5 %all_to_all.22 = s32[64,1,52]{2,1,0:T(1,128)S(1)} all-to-all(s32[64,1,52]{2,1,0:T(1,128)S(1)} %bitcast.76), channel_id=1, replica_groups=mesh['owner'=64,'neg'=4] {'owner'}, dimensions={0} | all-to-all | bytes 26624 | tf_op jit(solution)/shard_map/all_to_all | solution.py:125
  35.8 19.8 %gather_fusion = bf16[3328,1024]{1,0:T(8,128)(2,1)} fusion(bf16[4096,1024]{1,0:T(8,128)(2,1)} %param.17, s32[4096]{0:T(1024)S(1)} %pad_clamp_fusion), kind=kCustom, calls=%fused_computation | custom fusion | bytes 13644800 | tf_op jit(solution)/shard_map/gather | solution.py:126
  55.6 9.8 %reshape.945 = bf16[64,52,1024]{2,1,0:T(8,128)(2,1)} reshape(bf16[3328,1024]{1,0:T(8,128)(2,1)} %gather_fusion) | data formatting | bytes 13631488 | tf_op jit(solution)/shard_map/gather | solution.py:126
  65.4 5.8 %all-to-all-start.1 = ((bf16[64,52,1024]{2,1,0:T(8,128)(2,1)}), bf16[64,52,1024]{2,1,0:T(8,128)(2,1)}, u32[]{:S(2)}, u32[]{:S(2)}) async-start(bf16[64,52,1024]{2,1,0:T(8,128)(2,1)} %reshape.945), calls=%async_computation.1 | async-start | bytes 14680064 | tf_op jit(solution)/shard_map/all_to_all | solution.py:126
  72.5 162.5 %all-to-all-done.1 = bf16[64,52,1024]{2,1,0:T(8,128)(2,1)} async-done(((bf16[64,52,1024]{2,1,0:T(8,128)(2,1)}), bf16[64,52,1024]{2,1,0:T(8,128)(2,1)}, u32[]{:S(2)}, u32[]{:S(2)}) %all-to-all-start.1) | async-done | bytes 6815776 | tf_op jit(solution)/shard_map/all_to_all | solution.py:126
  235.0 5.4 %slice.109 = bf16[64,36,1024]{2,1,0:T(8,128)(2,1)} slice(bf16[64,52,1024]{2,1,0:T(8,128)(2,1)} %all-to-all-done.1), slice={[0:64], [16:52], [0:1024]} | slice | bytes 9437184 | tf_op jit(solution)/shard_map/slice | solution.py:128
  240.4 7.2 %reshape.937 = bf16[2304,1024]{1,0:T(8,128)(2,1)} reshape(bf16[64,36,1024]{2,1,0:T(8,128)(2,1)} %slice.109) | data formatting | bytes 9437184 | tf_op jit(solution)/shard_map/reshape | solution.py:128
  247.6 7.2 %reshape.963 = bf16[2304,1024,1]{1,0,2:T(8,128)(2,1)} reshape(bf16[64,36,1024]{2,1,0:T(8,128)(2,1)} %slice.109) | data formatting | bytes 9437184 | tf_op jit(solution)/shard_map/reshape | solution.py:128
  254.8 3.2 convolution_convert_fusion
  258.1 1.9 slice.111
  260.0 0.9 convolution_convert_fusion.1
  261.4 0.8 multiply_reduce_fusion.1
  262.4 1.3 fusion.32
  263.7 6.7 %gather_fusion.1 = f32[1024]{0:T(1024)S(1)} fusion(f32[8,2304]{1,0:T(8,128)S(1)} %fusion.32, s32[1024]{0:T(1024)S(1)} %fusion.46), kind=kCustom, calls=%fused_computation.1 | custom fusion | bytes 16384 | tf_op jit(solution)/shard_map/jit(take_along_axis)/gather | solution.py:154
  270.5 0.7 fusion.65
  271.9 1.8 select_reduce_fusion
  273.7 3.2 multiply_reduce_fusion
  279.1 15.6 %all_to_all.23 = bf16[64,2,192]{2,1,0:T(2,128)(2,1)S(1)} all-to-all(bf16[64,2,192]{2,1,0:T(2,128)(2,1)S(1)} %reshape.976), channel_id=1, replica_groups=mesh['owner'=64,'neg'=4] {'owner'}, dimensions={0} | all-to-all | bytes 98304 | tf_op jit(solution)/shard_map/all_to_all | solution.py:61
  294.8 59.5 %all-gather.4.cloned.1.call-done = bf16[64,12,2048]{2,1,0:T(8,128)(2,1)} async-done(((bf16[1,12,2048]{2,1,0:T(8,128)(2,1)}), bf16[64,12,2048]{2,1,0:T(8,128)(2,1)}) %all-gather.4.cloned.1.call-update) | async-done | bytes 3145744 | tf_op jit(solution)/shard_map/all_gather | solution.py:67
  354.3 1.7 slice_bitcast_fusion
  356.0 1.0 fusion.16
  357.0 1.0 fusion.14
  358.0 3.2 add_reduce_fusion
  361.2 13.9 %psum.21 = f32[2,2048]{1,0:T(2,128)S(1)} all-reduce(f32[2,2048]{1,0:T(2,128)S(1)} %add_reduce_fusion), channel_id=1, replica_groups=mesh['owner'=64,'neg'=4] {'neg'}, use_global_device_ids=true, to_apply=%region_12.13 | all-reduce | flops 4096 | bytes 32768 | tf_op jit(solution)/shard_map/psum | solution.py:174
  376.2 43.0 %all-reduce.4.cloned.1.call-done = (f32[16,1024]{1,0:T(8,128)}, f32[32,1024]{1,0:T(8,128)}) async-done(((f32[16,1024]{1,0:T(8,128)}, f32[32,1024]{1,0:T(8,128)}), (f32[16,1024]{1,0:T(8,128)}, f32[32,1024]{1,0:T(8,128)})) %all-reduce.4.cloned.1.call-update) | async-done | bytes 196624 | tf_op jit(solution)/shard_map/psum | solution.py:174
  419.2 1.5 copy.30
  420.7 1.6 copy.31
  (74 shorter events, 7.1 us)
Async XLA Ops:
  7.2 253.8 %copy-start = (bf16[1024,1024]{1,0:T(8,128)(2,1)S(1)}, bf16[1024,1024]{1,0:T(8,128)(2,1)}, u32[]{:S(2)}) copy-start(bf16[1024,1024]{1,0:T(8,128)(2,1)} %param.18) | copy-start | bytes 6291460
  65.4 6.2 %copy-start.5 = (s32[8,50]{1,0:T(8,128)S(1)}, s32[8,50]{1,0:T(8,128)}, u32[]{:S(2)}) copy-start(s32[8,50]{1,0:T(8,128)} %param.13) | copy-start | bytes 4804
  65.4 6.5 %copy-start.4 = (s32[8,50]{1,0:T(8,128)S(1)}, s32[8,50]{1,0:T(8,128)}, u32[]{:S(2)}) copy-start(s32[8,50]{1,0:T(8,128)} %param.12) | copy-start | bytes 4804
  65.4 169.6 %all-to-all-start.1 = ((bf16[64,52,1024]{2,1,0:T(8,128)(2,1)}), bf16[64,52,1024]{2,1,0:T(8,128)(2,1)}, u32[]{:S(2)}, u32[]{:S(2)}) async-start(bf16[64,52,1024]{2,1,0:T(8,128)(2,1)} %reshape.945), calls=%async_computation.1 | async-start | bytes 14680064 | tf_op jit(solution)/shard_map/all_to_all | solution.py:126
  71.3 283.0 %all-gather.4.cloned.1.call-start = ((), (), s32[]{:S(2)}) async-start(), calls=%async_computation.3 | async-start | bytes 4259840 | tf_op jit(solution)/shard_map/all_gather | solution.py:67
  254.8 7.6 %slice-start = ((s8[4718592]{0:T(1024)(128)(4,1)}), s8[4194304]{0:T(1024)(128)(4,1)S(1)}, s32[]{:S(2)}) async-start(s8[4718592]{0:T(1024)(128)(4,1)} %bitcast.69), calls=%async_computation.5 | async-start | bytes 8388608
  258.1 2.9 copy-start.6
  258.1 3.3 copy-start.1
  258.1 3.3 copy-start.7
  258.1 4.3 %slice-start.1 = ((s8[4718592]{0:T(1024)(128)(4,1)}), s8[524288]{0:T(1024)(128)(4,1)S(1)}, s32[]{:S(2)}) async-start(s8[4718592]{0:T(1024)(128)(4,1)} %bitcast.69), calls=%async_computation.6 | async-start | bytes 1048576
  262.4 14.4 %copy-start.3 = (f32[8,1024]{1,0:T(8,128)}, f32[8,1024]{1,0:T(8,128)S(1)}, u32[]{:S(2)}) copy-start(f32[8,1024]{1,0:T(8,128)S(1)} %get-tuple-element.48) | copy-start | bytes 98308
  271.9 5.1 %copy-start.2 = (bf16[2048,1024]{1,0:T(8,128)(2,1)S(1)}, bf16[2048,1024]{1,0:T(8,128)(2,1)}, u32[]{:S(2)}) copy-start(bf16[2048,1024]{1,0:T(8,128)(2,1)} %param.20) | copy-start | bytes 12582916
  278.3 140.8 %all-reduce.4.cloned.1.call-start = ((), (), s32[]{:S(2)}) async-start(), calls=%async_computation.4 | async-start | bytes 393216 | tf_op jit(solution)/shard_map/psum | solution.py:174
Sparse Core Ops, SparseCore 0:
  278.5 75.7 all-gather.3
  375.7 43.3 all-reduce.3

commit v3 on v2

--- a/solution.py
+++ b/solution.py
@@ -113,17 +113,22 @@
     weights = counts_f / jnp.sum(counts_f, axis=1, keepdims=True)
     flat_ids = nbr_ids.reshape(-1)
     capacity = 2 * (flat_ids.shape[0] // owners) + 4
-    owner_of, slot_of, requests = bucket(flat_ids, owners, rows_per, capacity)
     page_cap = 2 * (queries * (neg_count + 2) // owners) + 4
+    capacity = -(-capacity // 8) * 8
+    page_cap = -(-page_cap // 8) * 8
     total_queries = queries * owners * groups
     grad_scale = 1.0 / neg_count
     loss_scale = 1.0 / (total_queries * neg_count)
+    owner_of, slot_of, requests = bucket(flat_ids, owners, rows_per, capacity)
     page_list = jnp.concatenate([self_ids, pos_ids, neg_ids.reshape(-1)])
     page_owner, page_slot, page_requests = bucket(page_list, owners, rows_per, page_cap)
     slots = capacity + page_cap
     all_requests = jnp.concatenate([requests, page_requests], axis=1)
     served = lax.all_to_all(all_requests, "owner", split_axis=0, concat_axis=0, tiled=True)
-    returned = lax.all_to_all(table[served], "owner", split_axis=0, concat_axis=0, tiled=True)
+    returned = lax.all_to_all(
+        table[served.reshape(-1)].reshape(owners, slots, width),
+        "owner", split_axis=0, concat_axis=0, tiled=True,
+    )
     nbr_rows = returned[:, :capacity].reshape(owners * capacity, width)
     page_rows = returned[:, capacity:].reshape(owners * page_cap, width)
     nbr_flat = (owner_of * capacity + slot_of).reshape(queries, fan_count)
@@ -171,7 +176,14 @@
     loss_row = jnp.zeros((2 * width,), jnp.float32).at[0].set(loss_part)
     stats = jnp.stack([jnp.concatenate([conv_bgrad, pool_bgrad]), loss_row])
     pool_part, conv_part, stats_sum = weight_grads(joined, pooled_b, d_conv_b, d_pool_b, stats)
-    grad_pool_w, grad_conv_w, stats_all = lax.psum((pool_part, conv_part, stats_sum), "neg")
+    pool_rows = pool_part.shape[0]
+    conv_rows = conv_part.shape[0]
+    summed = lax.psum(
+        jnp.concatenate([pool_part, conv_part, stats_sum.reshape(-1, width)], axis=0), "neg"
+    )
+    grad_pool_w = summed[:pool_rows]
+    grad_conv_w = summed[pool_rows : pool_rows + conv_rows]
+    stats_all = summed[pool_rows + conv_rows :].reshape(stats_sum.shape)
     grad_conv_b = stats_all[0, :width]
     grad_pool_b = stats_all[0, width:]
     loss_sum = stats_all[1, 0]

time: 431 us -> 392 us (0.910)
  local copies, waits for them, and re-layouts: 68.6 us -> 45.3 us
  blocking collectives: 51 us -> 37.2 us
    reshape x2 -> x3, local copies, waits for them, and re-layouts: 14.4 us -> 0.15 us  [the longest x1 0.1 us: local(): served.reshape(-1)]
    psum x1 -> x0, blocking collectives: 13.9 us -> none  [local(): lax.psum((pool_part, conv_part, stats_sum), 'neg')]
    gather x2 -> x1, local copies, waits for them, and re-layouts: 29.6 us -> 20.8 us  [local(): table[served.reshape(-1)].reshape(owners, slots, width)]
  transfers between devices with their start and end apart: 3 -> 3, of which waited for: 3 -> 3; matrix products, arithmetic and copies ran while one was open for 1% -> 0% of each run, Pallas kernels for 0% -> 0%
where the time goes in v3:
time: 392 us; the launch traced here: 390 us
  waiting for transfers between devices  265 us (68%)
  local copies, waits for them, and re-layouts  45.3 us (12%)
  blocking collectives  37.2 us (9%)
  between operations  15.1 us (4%)
  matrix products  12.4 us (3%)
  other arithmetic  9.32 us (2%)
  starting transfers between devices  6.1 us (2%)
    all_to_all x1, waiting for transfers between devices, local(): lax.all_to_all(table[served.reshape(-1)].reshape(owners, slots, width), '...  163 us
    all_gather x1, waiting for transfers between devices, weight_grads(): gathered = lax.all_gather(payload, 'owner', axis=0)  59.5 us
    psum x1, waiting for transfers between devices, local(): lax.psum(jnp.concatenate([pool_part, conv_part, stats_sum.reshape(-1, wid...  42.8 us
    all_to_all x1, blocking collectives, local(): lax.all_to_all(all_requests, 'owner', split_axis=0, concat_axis=0, tiled=...  21.5 us
    gather x1, local copies, waits for them, and re-layouts, local(): table[served.reshape(-1)].reshape(owners, slots, width)  20.8 us
    all_to_all x1, blocking collectives, weight_grads(): lax.all_to_all(left, 'owner', split_axis=0, concat_axis=0, tiled=True)  15.6 us
  transfers between devices with their start and end apart: 3, of which 3 were waited for; matrix products, arithmetic and copies ran while one was open for 0% of the time, Pallas kernels for 0%

profile of v3, /device:TPU:6, one launch (start us, length us, event | category | flops | bytes accessed | tf_op | source)
XLA Modules:
  0.0 390.2 jit_solution(14158465473803235317)
XLA Ops:
  7.2 0.9 reshape.949
  8.1 0.8 reshape.948
  9.7 0.8 concatenate.107
  10.6 0.8 concatenate.103
  11.4 0.6 fusion.8
  12.0 2.0 fusion.3
  14.3 21.5 %all_to_all.19 = s32[64,1,56]{2,1,0:T(1,128)S(1)} all-to-all(s32[64,1,56]{2,1,0:T(1,128)S(1)} %bitcast.79), channel_id=1, replica_groups=mesh['owner'=64,'neg'=4] {'owner'}, dimensions={0} | all-to-all | bytes 28672 | tf_op jit(solution)/shard_map/all_to_all | solution.py:127
  36.4 0.7 reduce.19
  37.3 20.8 %gather_fusion = bf16[3584,1024]{1,0:T(8,128)(2,1)} fusion(bf16[4096,1024]{1,0:T(8,128)(2,1)} %param.17, s32[4096]{0:T(1024)S(1)} %pad_clamp_fusion), kind=kCustom, calls=%fused_computation | custom fusion | bytes 14694400 | tf_op jit(solution)/shard_map/gather | solution.py:129
  58.1 5.8 %all-to-all-start.1 = ((bf16[64,56,1024]{2,1,0:T(8,128)(2,1)}), bf16[64,56,1024]{2,1,0:T(8,128)(2,1)}, u32[]{:S(2)}, u32[]{:S(2)}) async-start(bf16[64,56,1024]{2,1,0:T(8,128)(2,1)} %bitcast.73), calls=%async_computation.1 | async-start | bytes 14680064 | tf_op jit(solution)/shard_map/all_to_all | solution.py:128
  65.2 162.5 %all-to-all-done.1 = bf16[64,56,1024]{2,1,0:T(8,128)(2,1)} async-done(((bf16[64,56,1024]{2,1,0:T(8,128)(2,1)}), bf16[64,56,1024]{2,1,0:T(8,128)(2,1)}, u32[]{:S(2)}, u32[]{:S(2)}) %all-to-all-start.1) | async-done | bytes 7340064 | tf_op jit(solution)/shard_map/all_to_all | solution.py:128
  227.7 3.1 slice.121
  230.8 0.8 convolution_convert_fusion
  231.7 2.8 slice.123
  234.5 0.9 convolution_convert_fusion.1
  235.8 0.8 multiply_reduce_fusion.1
  236.8 1.5 fusion.33
  238.3 6.7 %gather_fusion.1 = f32[1024]{0:T(1024)S(1)} fusion(f32[8,2560]{1,0:T(8,128)S(1)} %fusion.33, s32[1024]{0:T(1024)S(1)} %fusion.47), kind=kCustom, calls=%fused_computation.1 | custom fusion | bytes 16384 | tf_op jit(solution)/shard_map/jit(take_along_axis)/gather | solution.py:159
  245.0 0.7 fusion.66
  246.4 2.0 select_reduce_fusion
  248.4 3.4 multiply_reduce_fusion
  251.9 0.7 fusion.68
  252.6 0.7 maximum_bitcast_fusion
  254.1 15.6 %all_to_all.20 = bf16[64,2,192]{2,1,0:T(2,128)(2,1)S(1)} all-to-all(bf16[64,2,192]{2,1,0:T(2,128)(2,1)S(1)} %reshape.999), channel_id=1, replica_groups=mesh['owner'=64,'neg'=4] {'owner'}, dimensions={0} | all-to-all | bytes 98304 | tf_op jit(solution)/shard_map/all_to_all | solution.py:61
  269.8 59.5 %all-gather.4.cloned.1.call-done = bf16[64,12,2048]{2,1,0:T(8,128)(2,1)} async-done(((bf16[1,12,2048]{2,1,0:T(8,128)(2,1)}), bf16[64,12,2048]{2,1,0:T(8,128)(2,1)}) %all-gather.4.cloned.1.call-update) | async-done | bytes 3145744 | tf_op jit(solution)/shard_map/all_gather | solution.py:67
  329.3 1.7 slice_bitcast_fusion
  331.7 3.2 add_reduce_fusion
  334.9 0.7 pad_maximum_fusion
  335.6 42.8 %all-reduce.3.cloned.1.call-done = f32[52,1024]{1,0:T(8,128)} async-done(((f32[52,1024]{1,0:T(8,128)}), f32[52,1024]{1,0:T(8,128)}) %all-reduce.3.cloned.1.call-update) | async-done | bytes 213008 | tf_op jit(solution)/shard_map/psum | solution.py:181
  378.5 0.8 slice.133
  380.4 1.5 slice.135
  381.8 1.6 slice.137
  (73 shorter events, 6.4 us)
Async XLA Ops:
  7.2 228.2 %copy-start = (bf16[1024,1024]{1,0:T(8,128)(2,1)S(1)}, bf16[1024,1024]{1,0:T(8,128)(2,1)}, u32[]{:S(2)}) copy-start(bf16[1024,1024]{1,0:T(8,128)(2,1)} %param.18) | copy-start | bytes 6291460
  58.1 6.2 %copy-start.6 = (s32[8,50]{1,0:T(8,128)S(1)}, s32[8,50]{1,0:T(8,128)}, u32[]{:S(2)}) copy-start(s32[8,50]{1,0:T(8,128)} %param.13) | copy-start | bytes 4804
  58.1 6.5 %copy-start.5 = (s32[8,50]{1,0:T(8,128)S(1)}, s32[8,50]{1,0:T(8,128)}, u32[]{:S(2)}) copy-start(s32[8,50]{1,0:T(8,128)} %param.12) | copy-start | bytes 4804
  58.1 169.6 %all-to-all-start.1 = ((bf16[64,56,1024]{2,1,0:T(8,128)(2,1)}), bf16[64,56,1024]{2,1,0:T(8,128)(2,1)}, u32[]{:S(2)}, u32[]{:S(2)}) async-start(bf16[64,56,1024]{2,1,0:T(8,128)(2,1)} %bitcast.73), calls=%async_computation.1 | async-start | bytes 14680064 | tf_op jit(solution)/shard_map/all_to_all | solution.py:128
  64.0 265.3 %all-gather.4.cloned.1.call-start = ((), (), s32[]{:S(2)}) async-start(), calls=%async_computation.4 | async-start | bytes 4259840 | tf_op jit(solution)/shard_map/all_gather | solution.py:67
  230.8 6.0 %copy-start.1 = (bf16[64,40,1024]{2,1,0:T(8,128)(2,1)}, bf16[64,40,1024]{2,1,0:T(8,128)(2,1)S(1)}, u32[]{:S(2)}) copy-start(bf16[64,40,1024]{2,1,0:T(8,128)(2,1)S(1)} %slice.121) | copy-start | bytes 15728644
  231.6 3.8 copy-start.7
  231.6 4.2 %copy-start.2 = (bf16[2048,1024]{1,0:T(8,128)(2,1)S(1)}, bf16[2048,1024]{1,0:T(8,128)(2,1)}, u32[]{:S(2)}) copy-start(bf16[2048,1024]{1,0:T(8,128)(2,1)} %param.20) | copy-start | bytes 12582916
  231.7 4.2 %copy-start.8 = (f32[1024]{0:T(1024)S(1)}, f32[1024]{0:T(1024)}, u32[]{:S(2)}) copy-start(f32[1024]{0:T(1024)} %param.21) | copy-start | bytes 12292
  236.8 15.0 %copy-start.4 = (f32[8,1024]{1,0:T(8,128)}, f32[8,1024]{1,0:T(8,128)S(1)}, u32[]{:S(2)}) copy-start(f32[8,1024]{1,0:T(8,128)S(1)} %get-tuple-element.25) | copy-start | bytes 98308
  246.4 5.5 %copy-start.3 = (bf16[2048,1024]{1,0:T(8,128)(2,1)S(1)}, bf16[2048,1024]{1,0:T(8,128)(2,1)}, u32[]{:S(2)}) copy-start(bf16[2048,1024]{1,0:T(8,128)(2,1)} %param.20) | copy-start | bytes 12582916
  253.3 125.2 %all-reduce.3.cloned.1.call-start = ((), (), s32[]{:S(2)}) async-start(), calls=%async_computation.3 | async-start | bytes 458752 | tf_op jit(solution)/shard_map/psum | solution.py:181
Sparse Core Ops, SparseCore 0:
  253.4 75.7 all-gather.3
  335.8 42.6 all-reduce.2

commit v4 on v3

--- a/solution.py
+++ b/solution.py
@@ -1,9 +1,10 @@
 import jax
 import jax.numpy as jnp
 from jax import lax
-from jax.sharding import PartitionSpec as P
+from jax.sharding import Mesh, PartitionSpec as P
 
 margin_value = 0.5
+OWNER = ("oz", "oy", "oc")
 
 
 def silu_slope(values):
@@ -47,7 +48,7 @@
 
 
 def weight_grads(joined, pooled_b, d_conv_b, d_pool_b, stats):
-    owners = lax.axis_size("owner")
+    owners = lax.axis_size(OWNER)
     queries = joined.shape[0]
     conv_rows = joined.shape[1] // owners
     pool_rows = pooled_b.shape[1] // owners
@@ -58,13 +59,16 @@
         ],
         axis=2,
     )
-    left = lax.all_to_all(left, "owner", split_axis=0, concat_axis=0, tiled=True)
+    left = lax.all_to_all(left, OWNER, split_axis=0, concat_axis=0, tiled=True)
     left = left.reshape(owners * queries, conv_rows + pool_rows)
     stats_hi = stats.astype(jnp.bfloat16)
     stats_lo = (stats - stats_hi.astype(jnp.float32)).astype(jnp.bfloat16)
     payload = jnp.concatenate([d_conv_b, d_pool_b], axis=1)
     payload = jnp.concatenate([payload, stats_hi, stats_lo], axis=0)
-    gathered = lax.all_gather(payload, "owner", axis=0)
+    gathered = payload
+    for axis in OWNER[::-1]:
+        gathered = lax.all_gather(gathered, axis, axis=0)
+    gathered = gathered.reshape((owners,) + payload.shape)
     right = gathered[:, :queries].reshape(owners * queries, payload.shape[1])
     stat_rows = stats.shape[0]
     stats_sum = jnp.sum(
@@ -103,7 +107,7 @@
 
 
 def local(nbr_ids, visit_counts, self_ids, pos_ids, neg_ids, table, w_pool, b_pool, w_conv, b_conv):
-    owners = lax.axis_size("owner")
+    owners = lax.axis_size(OWNER)
     groups = lax.axis_size("neg")
     rows_per = table.shape[0]
     width = table.shape[1]
@@ -124,10 +128,10 @@
     page_owner, page_slot, page_requests = bucket(page_list, owners, rows_per, page_cap)
     slots = capacity + page_cap
     all_requests = jnp.concatenate([requests, page_requests], axis=1)
-    served = lax.all_to_all(all_requests, "owner", split_axis=0, concat_axis=0, tiled=True)
+    served = lax.all_to_all(all_requests, OWNER, split_axis=0, concat_axis=0, tiled=True)
     returned = lax.all_to_all(
         table[served.reshape(-1)].reshape(owners, slots, width),
-        "owner", split_axis=0, concat_axis=0, tiled=True,
+        OWNER, split_axis=0, concat_axis=0, tiled=True,
     )
     nbr_rows = returned[:, :capacity].reshape(owners * capacity, width)
     page_rows = returned[:, capacity:].reshape(owners * page_cap, width)
@@ -191,21 +195,29 @@
 
 
 def solution(mesh):
+    owners, groups = mesh.devices.shape
+    cores = 2
+    rows_y = 4 if owners % (cores * 4) == 0 else 1
+    fine = Mesh(
+        mesh.devices.reshape(owners // (cores * rows_y), rows_y, cores, groups),
+        OWNER + ("neg",),
+    )
+    spread = OWNER + ("neg",)
     return jax.shard_map(
         local,
-        mesh=mesh,
+        mesh=fine,
         in_specs=(
-            P(("owner", "neg"), None),
-            P(("owner", "neg"), None),
-            P(("owner", "neg")),
-            P(("owner", "neg")),
-            P(("owner", "neg"), None),
-            P("owner", None),
+            P(spread, None),
+            P(spread, None),
+            P(spread),
+            P(spread),
+            P(spread, None),
+            P(OWNER, None),
             P(),
             P(),
             P(),
             P(),
         ),
-        out_specs=(P(("owner", "neg"), None), P(), P("owner", None), P(), P("owner", None), P()),
+        out_specs=(P(spread, None), P(), P(OWNER, None), P(), P(OWNER, None), P()),
         check_vma=False,
     )

time: 392 us -> 385 us (0.982)
  waiting for transfers between devices: 265 us -> 232 us
  blocking collectives: 37.2 us -> 51.9 us
  local copies, waits for them, and re-layouts: 45.3 us -> 58.4 us
    all_gather x1, waiting for transfers between devices: 59.5 us -> 25.8 us  [weight_grads(): gathered = lax.all_gather(gathered, axis, axis=0)]
    all_gather x0 -> x2, blocking collectives: none -> 15.3 us  [weight_grads(): gathered = lax.all_gather(gathered, axis, axis=0)]
    all_gather x0 -> x2, local copies, waits for them, and re-layouts: none -> 7.49 us  [weight_grads(): gathered = lax.all_gather(gathered, axis, axis=0)]
    reshape x1, local copies, waits for them, and re-layouts: 1.73 us -> 5.74 us  [weight_grads(): gathered = gathered.reshape((owners,) + payload.shape)]
where the time goes in v4:
time: 385 us; the launch traced here: 383 us
  waiting for transfers between devices  232 us (60%)
  local copies, waits for them, and re-layouts  58.4 us (15%)
  blocking collectives  51.9 us (13%)
  between operations  15.1 us (4%)
  matrix products  12.4 us (3%)
  other arithmetic  7.01 us (2%)
  starting transfers between devices  6.1 us (2%)
    all_to_all x1, waiting for transfers between devices, local(): lax.all_to_all(table[served.reshape(-1)].reshape(owners, slots, width), O...  163 us
    psum x1, waiting for transfers between devices, local(): lax.psum(jnp.concatenate([pool_part, conv_part, stats_sum.reshape(-1, wid...  44 us
    all_gather x1, waiting for transfers between devices, weight_grads(): gathered = lax.all_gather(gathered, axis, axis=0)  25.8 us
    all_to_all x1, blocking collectives, local(): lax.all_to_all(all_requests, OWNER, split_axis=0, concat_axis=0, tiled=True)  21.5 us
    gather x1, local copies, waits for them, and re-layouts, local(): table[served.reshape(-1)].reshape(owners, slots, width)  20.8 us
    all_gather x2, blocking collectives, weight_grads(): gathered = lax.all_gather(gathered, axis, axis=0)  15.3 us
    all_to_all x1, blocking collectives, weight_grads(): left = lax.all_to_all(left, OWNER, split_axis=0, concat_axis=0, tiled=True)  15.1 us
  transfers between devices with their start and end apart: 3, of which 3 were waited for; matrix products, arithmetic and copies ran while one was open for 0% of the time, Pallas kernels for 0%

profile of v4, /device:TPU:6, one launch (start us, length us, event | category | flops | bytes accessed | tf_op | source)
XLA Modules:
  0.0 383.2 jit_solution(2959173300135636853)
XLA Ops:
  7.2 0.9 reshape.952
  8.1 0.8 reshape.951
  9.7 0.8 concatenate.107
  10.6 0.8 concatenate.103
  12.0 2.0 fusion.3
  14.3 21.5 %all_to_all.19 = s32[64,1,56]{2,1,0:T(1,128)S(1)} all-to-all(s32[64,1,56]{2,1,0:T(1,128)S(1)} %bitcast.86), channel_id=1, replica_groups=mesh['oz'=8,'oy'=4,'oc'=2,'neg'=4] {'oz','oy','oc'}, dimensions={0} | all-to-all | bytes 28672 | tf_op jit(solution)/shard_map/all_to_all | solution.py:131
  37.3 20.8 %gather_fusion = bf16[3584,1024]{1,0:T(8,128)(2,1)} fusion(bf16[4096,1024]{1,0:T(8,128)(2,1)} %param.17, s32[4096]{0:T(1024)S(1)} %pad_clamp_fusion), kind=kCustom, calls=%fused_computation | custom fusion | bytes 14694400 | tf_op jit(solution)/shard_map/gather | solution.py:133
  58.1 5.8 %all-to-all-start.1 = ((bf16[64,56,1024]{2,1,0:T(8,128)(2,1)}), bf16[64,56,1024]{2,1,0:T(8,128)(2,1)}, u32[]{:S(2)}, u32[]{:S(2)}) async-start(bf16[64,56,1024]{2,1,0:T(8,128)(2,1)} %bitcast.77), calls=%async_computation.1 | async-start | bytes 14680064 | tf_op jit(solution)/shard_map/all_to_all | solution.py:132
  65.2 162.5 %all-to-all-done.1 = bf16[64,56,1024]{2,1,0:T(8,128)(2,1)} async-done(((bf16[64,56,1024]{2,1,0:T(8,128)(2,1)}), bf16[64,56,1024]{2,1,0:T(8,128)(2,1)}, u32[]{:S(2)}, u32[]{:S(2)}) %all-to-all-start.1) | async-done | bytes 7340064 | tf_op jit(solution)/shard_map/all_to_all | solution.py:132
  227.7 3.1 slice.121
  230.8 0.8 convolution_convert_fusion
  231.7 2.8 slice.123
  234.5 0.9 convolution_convert_fusion.1
  235.8 0.8 multiply_reduce_fusion.1
  236.8 1.5 fusion.33
  238.3 6.7 %gather_fusion.1 = f32[1024]{0:T(1024)S(1)} fusion(f32[8,2560]{1,0:T(8,128)S(1)} %fusion.33, s32[1024]{0:T(1024)S(1)} %fusion.47), kind=kCustom, calls=%fused_computation.1 | custom fusion | bytes 16384 | tf_op jit(solution)/shard_map/jit(take_along_axis)/gather | solution.py:163
  245.0 0.7 fusion.66
  246.4 2.0 select_reduce_fusion
  248.4 3.4 multiply_reduce_fusion
  252.6 1.9 all-gather.3
  254.5 13.4 %all-gather.1 = bf16[8,12,2048]{2,1,0:T(8,128)(2,1)S(1)} all-gather(bf16[2,12,2048]{2,1,0:T(8,128)(2,1)S(1)} %all-gather.3), channel_id=3, replica_groups=mesh['oz'=8,'oy'=4,'oc'=2,'neg'=4] {'oy'}, dimensions={0}, use_global_device_ids=true | all-gather | bytes 491520 | tf_op jit(solution)/shard_map/all_gather | solution.py:70
  267.9 1.1 copy.33
  269.9 15.1 %all_to_all.20 = bf16[64,2,192]{2,1,0:T(2,128)(2,1)S(1)} all-to-all(bf16[64,2,192]{2,1,0:T(2,128)(2,1)S(1)} %reshape.1006), channel_id=1, replica_groups=mesh['oz'=8,'oy'=4,'oc'=2,'neg'=4] {'oz','oy','oc'}, dimensions={0} | all-to-all | bytes 98304 | tf_op jit(solution)/shard_map/all_to_all | solution.py:62
  285.1 25.8 %all-gather.6.cloned.1.call-done = bf16[32,2,12,2048]{3,1,2,0:T(2,128)(2,1)} async-done(((bf16[4,2,12,2048]{3,1,2,0:T(2,128)(2,1)}), bf16[32,2,12,2048]{3,1,2,0:T(2,128)(2,1)}) %all-gather.6.cloned.1.call-update) | async-done | bytes 3145744 | tf_op jit(solution)/shard_map/all_gather | solution.py:70
  310.8 6.3 %copy.34 = bf16[32,2,12,2048]{3,1,0,2:T(2,128)(2,1)} copy(bf16[32,2,12,2048]{3,1,2,0:T(2,128)(2,1)} %all-gather.6.cloned.1.call-done) | data formatting | bytes 6291456 | tf_op jit(solution)/shard_map/all_gather | solution.py:70
  317.2 5.7 %reshape.961 = bf16[64,12,2048]{2,0,1:T(8,128)(2,1)} reshape(bf16[32,2,12,2048]{3,1,0,2:T(2,128)(2,1)} %copy.34) | data formatting | bytes 6291456 | tf_op jit(solution)/shard_map/reshape | solution.py:71
  322.9 1.5 add_reduce_fusion
  324.8 1.2 copy.42
  327.4 44.0 %all-reduce.3.cloned.1.call-done = f32[52,1024]{1,0:T(8,128)} async-done(((f32[52,1024]{1,0:T(8,128)}), f32[52,1024]{1,0:T(8,128)}) %all-reduce.3.cloned.1.call-update) | async-done | bytes 213008 | tf_op jit(solution)/shard_map/psum | solution.py:185
  371.4 0.8 slice.133
  373.3 1.5 slice.135
  374.8 1.6 slice.137
  (80 shorter events, 9.5 us)
Async XLA Ops:
  7.2 228.2 %copy-start = (bf16[1024,1024]{1,0:T(8,128)(2,1)S(1)}, bf16[1024,1024]{1,0:T(8,128)(2,1)}, u32[]{:S(2)}) copy-start(bf16[1024,1024]{1,0:T(8,128)(2,1)} %param.18) | copy-start | bytes 6291460
  58.1 6.2 %copy-start.6 = (s32[8,50]{1,0:T(8,128)S(1)}, s32[8,50]{1,0:T(8,128)}, u32[]{:S(2)}) copy-start(s32[8,50]{1,0:T(8,128)} %param.13) | copy-start | bytes 4804
  58.1 6.5 %copy-start.5 = (s32[8,50]{1,0:T(8,128)S(1)}, s32[8,50]{1,0:T(8,128)}, u32[]{:S(2)}) copy-start(s32[8,50]{1,0:T(8,128)} %param.12) | copy-start | bytes 4804
  58.1 169.6 %all-to-all-start.1 = ((bf16[64,56,1024]{2,1,0:T(8,128)(2,1)}), bf16[64,56,1024]{2,1,0:T(8,128)(2,1)}, u32[]{:S(2)}, u32[]{:S(2)}) async-start(bf16[64,56,1024]{2,1,0:T(8,128)(2,1)} %bitcast.77), calls=%async_computation.1 | async-start | bytes 14680064 | tf_op jit(solution)/shard_map/all_to_all | solution.py:132
  64.0 246.9 %all-gather.6.cloned.1.call-start = ((), (), s32[]{:S(2)}) async-start(), calls=%async_computation.4 | async-start | bytes 3538944 | tf_op jit(solution)/shard_map/all_gather | solution.py:70
  230.8 6.0 %copy-start.1 = (bf16[64,40,1024]{2,1,0:T(8,128)(2,1)}, bf16[64,40,1024]{2,1,0:T(8,128)(2,1)S(1)}, u32[]{:S(2)}) copy-start(bf16[64,40,1024]{2,1,0:T(8,128)(2,1)S(1)} %slice.121) | copy-start | bytes 15728644
  231.6 3.8 copy-start.7
  231.6 4.2 %copy-start.2 = (bf16[2048,1024]{1,0:T(8,128)(2,1)S(1)}, bf16[2048,1024]{1,0:T(8,128)(2,1)}, u32[]{:S(2)}) copy-start(bf16[2048,1024]{1,0:T(8,128)(2,1)} %param.20) | copy-start | bytes 12582916
  231.7 4.2 %copy-start.8 = (f32[1024]{0:T(1024)S(1)}, f32[1024]{0:T(1024)}, u32[]{:S(2)}) copy-start(f32[1024]{0:T(1024)} %param.21) | copy-start | bytes 12292
  236.8 15.0 %copy-start.4 = (f32[8,1024]{1,0:T(8,128)}, f32[8,1024]{1,0:T(8,128)S(1)}, u32[]{:S(2)}) copy-start(f32[8,1024]{1,0:T(8,128)S(1)} %get-tuple-element.25) | copy-start | bytes 98308
  246.4 5.5 %copy-start.3 = (bf16[2048,1024]{1,0:T(8,128)(2,1)S(1)}, bf16[2048,1024]{1,0:T(8,128)(2,1)}, u32[]{:S(2)}) copy-start(bf16[2048,1024]{1,0:T(8,128)(2,1)} %param.20) | copy-start | bytes 12582916
  269.1 102.3 %all-reduce.3.cloned.1.call-start = ((), (), s32[]{:S(2)}) async-start(), calls=%async_computation.3 | async-start | bytes 458752 | tf_op jit(solution)/shard_map/psum | solution.py:185
  322.9 1.9 slice-start
Sparse Core Ops, SparseCore 0:
  269.2 41.5 all-gather.5
  327.5 43.8 all-reduce.2

commit v5 on v4

--- a/solution.py
+++ b/solution.py
@@ -87,6 +87,15 @@
         preferred_element_type=jnp.float32,
     )
     return pool_part, conv_part, stats_sum
+
+
+def pair_sum(values, groups):
+    step = 1
+    while step < groups:
+        partner = lax.ppermute(values, "neg", [(i, i ^ step) for i in range(groups)])
+        values = values + partner
+        step *= 2
+    return values
 
 
 def bucket(page_list, owners, rows_per, capacity):
@@ -182,8 +191,8 @@
     pool_part, conv_part, stats_sum = weight_grads(joined, pooled_b, d_conv_b, d_pool_b, stats)
     pool_rows = pool_part.shape[0]
     conv_rows = conv_part.shape[0]
-    summed = lax.psum(
-        jnp.concatenate([pool_part, conv_part, stats_sum.reshape(-1, width)], axis=0), "neg"
+    summed = pair_sum(
+        jnp.concatenate([pool_part, conv_part, stats_sum.reshape(-1, width)], axis=0), groups
     )
     grad_pool_w = summed[:pool_rows]
     grad_conv_w = summed[pool_rows : pool_rows + conv_rows]

time: 385 us -> 352 us (0.914)
  waiting for transfers between devices: 232 us -> 201 us
    psum x1 -> x0, waiting for transfers between devices: 44 us -> none  [local(): lax.psum(jnp.concatenate([pool_part, conv_part, stats_sum.reshape(-1, wid...]
    ppermute x0 -> x2, waiting for transfers between devices: none -> 13.1 us  [pair_sum(): lax.ppermute(values, 'neg', [(i, i ^ step) for i in range(groups)])]
  transfers between devices with their start and end apart: 3 -> 4, of which waited for: 3 -> 4; matrix products, arithmetic and copies ran while one was open for 0% -> 0% of each run, Pallas kernels for 0% -> 0%
where the time goes in v5:
time: 352 us
  waiting for transfers between devices  201 us (57%)
  local copies, waits for them, and re-layouts  55.9 us (16%)
  blocking collectives  51.9 us (15%)
  between operations  15.1 us (4%)
  matrix products  12.4 us (4%)
  starting transfers between devices  8.45 us (2%)
  other arithmetic  6.38 us (2%)
    all_to_all x1, waiting for transfers between devices, local(): lax.all_to_all(table[served.reshape(-1)].reshape(owners, slots, width), O...  163 us
    all_gather x1, waiting for transfers between devices, weight_grads(): gathered = lax.all_gather(gathered, axis, axis=0)  25.8 us
    all_to_all x1, blocking collectives, local(): lax.all_to_all(all_requests, OWNER, split_axis=0, concat_axis=0, tiled=True)  21.5 us
    gather x1, local copies, waits for them, and re-layouts, local(): table[served.reshape(-1)].reshape(owners, slots, width)  20.8 us
    all_gather x2, blocking collectives, weight_grads(): gathered = lax.all_gather(gathered, axis, axis=0)  15.3 us
    all_to_all x1, blocking collectives, weight_grads(): left = lax.all_to_all(left, OWNER, split_axis=0, concat_axis=0, tiled=True)  15 us
    ppermute x2, waiting for transfers between devices, pair_sum(): lax.ppermute(values, 'neg', [(i, i ^ step) for i in range(groups)])  13.1 us
    all_gather x2, local copies, waits for them, and re-layouts, weight_grads(): gathered = lax.all_gather(gathered, axis, axis=0)  7.49 us
  transfers between devices with their start and end apart: 4, of which 4 were waited for; matrix products, arithmetic and copies ran while one was open for 0% of the time, Pallas kernels for 0%

profile of v5, /device:TPU:6, one launch (start us, length us, event | category | flops | bytes accessed | tf_op | source)
XLA Modules:
  0.0 351.5 jit_solution(4909479911728006914)
XLA Ops:
  7.2 0.9 reshape.952
  8.1 0.8 reshape.951
  9.7 0.8 concatenate.107
  10.6 0.8 concatenate.103
  12.0 2.0 fusion.3
  14.3 21.5 %all_to_all.19 = s32[64,1,56]{2,1,0:T(1,128)S(1)} all-to-all(s32[64,1,56]{2,1,0:T(1,128)S(1)} %bitcast.86), channel_id=1, replica_groups=mesh['oz'=8,'oy'=4,'oc'=2,'neg'=4] {'oz','oy','oc'}, dimensions={0} | all-to-all | bytes 28672 | tf_op jit(solution)/shard_map/all_to_all | solution.py:140
  37.3 20.8 %gather_fusion = bf16[3584,1024]{1,0:T(8,128)(2,1)} fusion(bf16[4096,1024]{1,0:T(8,128)(2,1)} %param.17, s32[4096]{0:T(1024)S(1)} %pad_clamp_fusion), kind=kCustom, calls=%fused_computation | custom fusion | bytes 14694400 | tf_op jit(solution)/shard_map/gather | solution.py:142
  58.1 5.8 %all-to-all-start.1 = ((bf16[64,56,1024]{2,1,0:T(8,128)(2,1)}), bf16[64,56,1024]{2,1,0:T(8,128)(2,1)}, u32[]{:S(2)}, u32[]{:S(2)}) async-start(bf16[64,56,1024]{2,1,0:T(8,128)(2,1)} %bitcast.77), calls=%async_computation.1 | async-start | bytes 14680064 | tf_op jit(solution)/shard_map/all_to_all | solution.py:141
  65.2 162.5 %all-to-all-done.1 = bf16[64,56,1024]{2,1,0:T(8,128)(2,1)} async-done(((bf16[64,56,1024]{2,1,0:T(8,128)(2,1)}), bf16[64,56,1024]{2,1,0:T(8,128)(2,1)}, u32[]{:S(2)}, u32[]{:S(2)}) %all-to-all-start.1) | async-done | bytes 7340064 | tf_op jit(solution)/shard_map/all_to_all | solution.py:141
  227.7 3.1 slice.121
  230.8 0.8 convolution_convert_fusion
  231.7 2.8 slice.123
  234.5 0.9 convolution_convert_fusion.1
  235.8 0.8 multiply_reduce_fusion.1
  236.8 1.5 fusion.33
  238.3 6.7 %gather_fusion.1 = f32[1024]{0:T(1024)S(1)} fusion(f32[8,2560]{1,0:T(8,128)S(1)} %fusion.33, s32[1024]{0:T(1024)S(1)} %fusion.47), kind=kCustom, calls=%fused_computation.1 | custom fusion | bytes 16384 | tf_op jit(solution)/shard_map/jit(take_along_axis)/gather | solution.py:172
  245.0 0.7 fusion.67
  246.4 2.0 select_reduce_fusion
  248.4 3.4 multiply_reduce_fusion
  252.7 1.9 all-gather.3
  254.6 13.4 %all-gather.1 = bf16[8,12,2048]{2,1,0:T(8,128)(2,1)S(1)} all-gather(bf16[2,12,2048]{2,1,0:T(8,128)(2,1)S(1)} %all-gather.3), channel_id=3, replica_groups=mesh['oz'=8,'oy'=4,'oc'=2,'neg'=4] {'oy'}, dimensions={0}, use_global_device_ids=true | all-gather | bytes 491520 | tf_op jit(solution)/shard_map/all_gather | solution.py:70
  267.9 1.1 copy.33
  269.8 15.0 %all_to_all.20 = bf16[64,2,192]{2,1,0:T(2,128)(2,1)S(1)} all-to-all(bf16[64,2,192]{2,1,0:T(2,128)(2,1)S(1)} %reshape.1006), channel_id=1, replica_groups=mesh['oz'=8,'oy'=4,'oc'=2,'neg'=4] {'oz','oy','oc'}, dimensions={0} | all-to-all | bytes 98304 | tf_op jit(solution)/shard_map/all_to_all | solution.py:62
  285.0 25.8 %all-gather.6.cloned.1.call-done = bf16[32,2,12,2048]{3,1,2,0:T(2,128)(2,1)} async-done(((bf16[4,2,12,2048]{3,1,2,0:T(2,128)(2,1)}), bf16[32,2,12,2048]{3,1,2,0:T(2,128)(2,1)}) %all-gather.6.cloned.1.call-update) | async-done | bytes 3145744 | tf_op jit(solution)/shard_map/all_gather | solution.py:70
  310.8 6.3 %copy.34 = bf16[32,2,12,2048]{3,1,0,2:T(2,128)(2,1)} copy(bf16[32,2,12,2048]{3,1,2,0:T(2,128)(2,1)} %all-gather.6.cloned.1.call-done) | data formatting | bytes 6291456 | tf_op jit(solution)/shard_map/all_gather | solution.py:70
  317.2 5.7 %reshape.961 = bf16[64,12,2048]{2,0,1:T(8,128)(2,1)} reshape(bf16[32,2,12,2048]{3,1,0,2:T(2,128)(2,1)} %copy.34) | data formatting | bytes 6291456 | tf_op jit(solution)/shard_map/reshape | solution.py:71
  322.9 1.5 add_reduce_fusion
  324.8 1.2 copy.42
  326.7 0.9 collective-permute-start
  327.6 6.5 %collective-permute-done = f32[52,1024]{1,0:T(8,128)S(1)} collective-permute-done((f32[52,1024]{1,0:T(8,128)S(1)}, f32[52,1024]{1,0:T(8,128)S(1)}, u32[]{:S(2)}, u32[]{:S(2)}) %collective-permute-start) | collective-permute-done | bytes 213024 | tf_op jit(solution)/shard_map/ppermute | solution.py:95
  334.1 1.5 collective-permute-start.1
  335.6 6.6 %collective-permute-done.1 = f32[52,1024]{1,0:T(8,128)S(1)} collective-permute-done((f32[52,1024]{1,0:T(8,128)S(1)}, f32[52,1024]{1,0:T(8,128)S(1)}, u32[]{:S(2)}, u32[]{:S(2)}) %collective-permute-start.1) | collective-permute-done | bytes 213024 | tf_op jit(solution)/shard_map/ppermute | solution.py:95
  (83 shorter events, 10.1 us)
Async XLA Ops:
  7.2 228.2 %copy-start = (bf16[1024,1024]{1,0:T(8,128)(2,1)S(1)}, bf16[1024,1024]{1,0:T(8,128)(2,1)}, u32[]{:S(2)}) copy-start(bf16[1024,1024]{1,0:T(8,128)(2,1)} %param.18) | copy-start | bytes 6291460
  58.1 6.2 %copy-start.6 = (s32[8,50]{1,0:T(8,128)S(1)}, s32[8,50]{1,0:T(8,128)}, u32[]{:S(2)}) copy-start(s32[8,50]{1,0:T(8,128)} %param.13) | copy-start | bytes 4804
  58.1 6.5 %copy-start.5 = (s32[8,50]{1,0:T(8,128)S(1)}, s32[8,50]{1,0:T(8,128)}, u32[]{:S(2)}) copy-start(s32[8,50]{1,0:T(8,128)} %param.12) | copy-start | bytes 4804
  58.1 169.6 %all-to-all-start.1 = ((bf16[64,56,1024]{2,1,0:T(8,128)(2,1)}), bf16[64,56,1024]{2,1,0:T(8,128)(2,1)}, u32[]{:S(2)}, u32[]{:S(2)}) async-start(bf16[64,56,1024]{2,1,0:T(8,128)(2,1)} %bitcast.77), calls=%async_computation.1 | async-start | bytes 14680064 | tf_op jit(solution)/shard_map/all_to_all | solution.py:141
  64.0 246.9 %all-gather.6.cloned.1.call-start = ((), (), s32[]{:S(2)}) async-start(), calls=%async_computation.3 | async-start | bytes 3538944 | tf_op jit(solution)/shard_map/all_gather | solution.py:70
  230.8 6.0 %copy-start.1 = (bf16[64,40,1024]{2,1,0:T(8,128)(2,1)}, bf16[64,40,1024]{2,1,0:T(8,128)(2,1)S(1)}, u32[]{:S(2)}) copy-start(bf16[64,40,1024]{2,1,0:T(8,128)(2,1)S(1)} %slice.121) | copy-start | bytes 15728644
  231.6 3.8 %copy-start.7 = (f32[1024]{0:T(1024)S(1)}, f32[1024]{0:T(1024)}, u32[]{:S(2)}) copy-start(f32[1024]{0:T(1024)} %param.19) | copy-start | bytes 12292
  231.6 4.2 %copy-start.2 = (bf16[2048,1024]{1,0:T(8,128)(2,1)S(1)}, bf16[2048,1024]{1,0:T(8,128)(2,1)}, u32[]{:S(2)}) copy-start(bf16[2048,1024]{1,0:T(8,128)(2,1)} %param.20) | copy-start | bytes 12582916
  231.7 4.2 %copy-start.8 = (f32[1024]{0:T(1024)S(1)}, f32[1024]{0:T(1024)}, u32[]{:S(2)}) copy-start(f32[1024]{0:T(1024)} %param.21) | copy-start | bytes 12292
  236.8 15.0 %copy-start.4 = (f32[8,1024]{1,0:T(8,128)}, f32[8,1024]{1,0:T(8,128)S(1)}, u32[]{:S(2)}) copy-start(f32[8,1024]{1,0:T(8,128)S(1)} %get-tuple-element.25) | copy-start | bytes 98308
  246.4 5.5 %copy-start.3 = (bf16[2048,1024]{1,0:T(8,128)(2,1)S(1)}, bf16[2048,1024]{1,0:T(8,128)(2,1)}, u32[]{:S(2)}) copy-start(bf16[2048,1024]{1,0:T(8,128)(2,1)} %param.20) | copy-start | bytes 12582916
  322.9 1.9 slice-start
  326.7 7.4 %collective-permute-start = (f32[52,1024]{1,0:T(8,128)S(1)}, f32[52,1024]{1,0:T(8,128)S(1)}, u32[]{:S(2)}, u32[]{:S(2)}) collective-permute-start(f32[52,1024]{1,0:T(8,128)S(1)} %pad_maximum_fusion), channel_id=1, source_target_pairs={{0,1},{1,0},{2,3},{3,2},{4,5},{5,4},{6,7},{7,6},{8,9},{9,8},{10,11... | collective-permute-start | bytes 638984 | tf_op jit(solution)/shard_map/ppermute | solution.py:95
  334.1 8.0 %collective-permute-start.1 = (f32[52,1024]{1,0:T(8,128)S(1)}, f32[52,1024]{1,0:T(8,128)S(1)}, u32[]{:S(2)}, u32[]{:S(2)}) collective-permute-start(f32[52,1024]{1,0:T(8,128)S(1)} %fusion.64), channel_id=1, source_target_pairs={{0,2},{1,3},{2,0},{3,1},{4,6},{5,7},{6,4},{7,5},{8,10},{9,11},{10,... | collective-permute-start | bytes 638984 | tf_op jit(solution)/shard_map/ppermute | solution.py:95
Sparse Core Ops, SparseCore 0:
  269.2 41.5 all-gather.5

commit v6 on v5

--- a/solution.py
+++ b/solution.py
@@ -142,46 +142,44 @@
         table[served.reshape(-1)].reshape(owners, slots, width),
         OWNER, split_axis=0, concat_axis=0, tiled=True,
     )
-    nbr_rows = returned[:, :capacity].reshape(owners * capacity, width)
-    page_rows = returned[:, capacity:].reshape(owners * page_cap, width)
-    nbr_flat = (owner_of * capacity + slot_of).reshape(queries, fan_count)
-    nbr_slots = jnp.arange(owners * capacity, dtype=jnp.int32)
-    pool_weights = jnp.sum(
-        jnp.where(nbr_flat[:, :, None] == nbr_slots[None, None, :], weights[:, :, None], 0.0), axis=1
-    )
-    pooled = jnp.dot(
-        pool_weights, nbr_rows.astype(jnp.float32), precision=lax.Precision.HIGHEST,
-        preferred_element_type=jnp.float32,
-    )
-    page_flat = page_owner * page_cap + page_slot
-    page_slots = jnp.arange(owners * page_cap, dtype=jnp.int32)
+    rows = returned.reshape(owners * slots, width)
+    slot_ids = jnp.arange(owners * slots, dtype=jnp.int32)
+    nbr_flat = (owner_of * slots + slot_of).reshape(queries, fan_count)
+    page_flat = page_owner * slots + capacity + page_slot
     self_flat = page_flat[:queries]
     pos_flat = page_flat[queries : 2 * queries]
     neg_flat = page_flat[2 * queries :].reshape(queries, neg_count)
-    pick = (jnp.stack([self_flat, pos_flat])[:, :, None] == page_slots[None, None, :]).astype(jnp.bfloat16)
-    picked = jnp.einsum("aqs,se->aqe", pick, page_rows, preferred_element_type=jnp.float32)
-    self_rows = picked[0].astype(jnp.bfloat16)
-    pos_rows = picked[1].astype(jnp.bfloat16)
+    pool_weights = jnp.sum(
+        jnp.where(nbr_flat[:, :, None] == slot_ids[None, None, :], weights[:, :, None], 0.0), axis=1
+    )
+    part_1 = pool_weights.astype(jnp.bfloat16)
+    rest_1 = pool_weights - part_1.astype(jnp.float32)
+    part_2 = rest_1.astype(jnp.bfloat16)
+    part_3 = (rest_1 - part_2.astype(jnp.float32)).astype(jnp.bfloat16)
+    pick = (jnp.concatenate([self_flat, pos_flat])[:, None] == slot_ids[None, :]).astype(jnp.bfloat16)
+    picked = jnp.dot(
+        jnp.concatenate([part_1, part_2, part_3, pick], axis=0), rows,
+        preferred_element_type=jnp.float32,
+    )
+    pooled = (picked[:queries] + picked[queries : 2 * queries]) + picked[2 * queries : 3 * queries]
+    self_rows = picked[3 * queries : 4 * queries].astype(jnp.bfloat16)
+    pos_rows = picked[4 * queries :].astype(jnp.bfloat16)
     pooled_b, pre_pool, joined, pre_conv, inverse, embedding = forward(
         pooled, self_rows, w_pool, b_pool, w_conv, b_conv
     )
     embed_b = embedding.astype(jnp.bfloat16)
     slot_scores = lax.dot_general(
-        embed_b, page_rows, (((1,), (1,)), ((), ())), preferred_element_type=jnp.float32
-    )
-    neg_scores = jnp.take_along_axis(slot_scores, neg_flat, axis=1)
+        embed_b, rows, (((1,), (1,)), ((), ())), preferred_element_type=jnp.float32
+    )
+    neg_match = neg_flat[:, :, None] == slot_ids[None, None, :]
+    neg_scores = jnp.sum(jnp.where(neg_match, slot_scores[:, None, :], 0.0), axis=2)
     pos_scores = jnp.einsum("qe,qe->q", embed_b, pos_rows, preferred_element_type=jnp.float32)
     loss_part, slope_b, slope_total = margin_terms(neg_scores, pos_scores, loss_scale)
     slope_slots = jnp.sum(
-        jnp.where(
-            neg_flat[:, :, None] == page_slots[None, None, :],
-            slope_b.astype(jnp.float32)[:, :, None],
-            0.0,
-        ),
-        axis=1,
+        jnp.where(neg_match, slope_b.astype(jnp.float32)[:, :, None], 0.0), axis=1
     ).astype(jnp.bfloat16)
     d_embed = jnp.dot(
-        slope_slots, page_rows, preferred_element_type=jnp.float32
+        slope_slots, rows, preferred_element_type=jnp.float32
     ) - slope_total * pos_rows.astype(jnp.float32)
     d_conv_b, d_pool_b, pool_bgrad, conv_bgrad = backward_factors(
         d_embed, embedding, inverse, pre_conv, pre_pool, w_conv, grad_scale

time: 352 us -> 352 us (level)
  local copies, waits for them, and re-layouts: 55.9 us -> 44.5 us
  matrix products: 12.4 us -> 20 us
  other arithmetic: 6.38 us -> 11 us
    dot_general x4 -> x3, matrix products: 6.6 us -> 14 us  [the longest x1 5.09 us: local(): lax.dot_general(embed_b, rows, (((1,), (1,)), ((), ())), preferred_elemen...]
    gather x1 -> x0, local copies, waits for them, and re-layouts: 6.73 us -> none  [local(): neg_scores = jnp.take_along_axis(slot_scores, neg_flat, axis=1)]
    slice x2 -> x1, local copies, waits for them, and re-layouts: 5.87 us -> 0.01 us  [local(): self_rows = picked[3 * queries:4 * queries].astype(jnp.bfloat16)]
    reduce_sum x2 -> x3, other arithmetic: 2.21 us -> 6.99 us  [the longest x1 3.26 us: local(): jnp.sum(jnp.where(neg_match, slope_b.astype(jnp.float32)[:, :, None], 0.0...]
  transfers between devices with their start and end apart: 4 -> 4, of which waited for: 4 -> 4; matrix products, arithmetic and copies ran while one was open for 0% -> 1% of each run, Pallas kernels for 0% -> 0%
where the time goes in v6:
time: 352 us; the launch traced here: 351 us
  waiting for transfers between devices  200 us (57%)
  blocking collectives  51.9 us (15%)
  local copies, waits for them, and re-layouts  44.5 us (13%)
  matrix products  20 us (6%)
  between operations  15.1 us (4%)
  other arithmetic  11 us (3%)
  starting transfers between devices  8.46 us (2%)
    all_to_all x1, waiting for transfers between devices, local(): lax.all_to_all(table[served.reshape(-1)].reshape(owners, slots, width), O...  161 us
    all_gather x1, waiting for transfers between devices, weight_grads(): gathered = lax.all_gather(gathered, axis, axis=0)  25.8 us
    all_to_all x1, blocking collectives, local(): lax.all_to_all(all_requests, OWNER, split_axis=0, concat_axis=0, tiled=True)  21.5 us
    gather x1, local copies, waits for them, and re-layouts, local(): table[served.reshape(-1)].reshape(owners, slots, width)  20.8 us
    all_gather x2, blocking collectives, weight_grads(): gathered = lax.all_gather(gathered, axis, axis=0)  15.3 us
    all_to_all x1, blocking collectives, weight_grads(): left = lax.all_to_all(left, OWNER, split_axis=0, concat_axis=0, tiled=True)  15 us
    ppermute x2, waiting for transfers between devices, pair_sum(): lax.ppermute(values, 'neg', [(i, i ^ step) for i in range(groups)])  13 us
    all_gather x2, local copies, waits for them, and re-layouts, weight_grads(): gathered = lax.all_gather(gathered, axis, axis=0)  7.49 us
  transfers between devices with their start and end apart: 4, of which 4 were waited for; matrix products, arithmetic and copies ran while one was open for 1% of the time, Pallas kernels for 0%

profile of v6, /device:TPU:6, one launch (start us, length us, event | category | flops | bytes accessed | tf_op | source)
XLA Modules:
  0.0 350.9 jit_solution(2132949499186267657)
XLA Ops:
  7.2 0.9 reshape.890
  8.1 0.8 reshape.892
  8.9 0.8 concatenate.109
  10.3 0.8 concatenate.115
  11.2 2.0 fusion.3
  14.3 21.5 %all_to_all.19 = s32[64,1,56]{2,1,0:T(1,128)S(1)} all-to-all(s32[64,1,56]{2,1,0:T(1,128)S(1)} %bitcast.43), channel_id=1, replica_groups=mesh['oz'=8,'oy'=4,'oc'=2,'neg'=4] {'oz','oy','oc'}, dimensions={0} | all-to-all | bytes 28672 | tf_op jit(solution)/shard_map/all_to_all | solution.py:140
  36.4 0.7 reduce.15
  37.3 20.8 %gather_fusion = bf16[3584,1024]{1,0:T(8,128)(2,1)} fusion(bf16[4096,1024]{1,0:T(8,128)(2,1)} %param.17, s32[4096]{0:T(1024)S(1)} %pad_clamp_fusion), kind=kCustom, calls=%fused_computation | custom fusion | bytes 14694400 | tf_op jit(solution)/shard_map/gather | solution.py:142
  58.1 5.8 %all-to-all-start.1 = ((bf16[64,56,1024]{2,1,0:T(8,128)(2,1)}), bf16[64,56,1024]{2,1,0:T(8,128)(2,1)}, u32[]{:S(2)}, u32[]{:S(2)}) async-start(bf16[64,56,1024]{2,1,0:T(8,128)(2,1)} %bitcast.35), calls=%async_computation.1 | async-start | bytes 14680064 | tf_op jit(solution)/shard_map/all_to_all | solution.py:141
  64.8 1.7 select_reduce_fusion.2
  66.6 161.1 %all-to-all-done.1 = bf16[64,56,1024]{2,1,0:T(8,128)(2,1)} async-done(((bf16[64,56,1024]{2,1,0:T(8,128)(2,1)}), bf16[64,56,1024]{2,1,0:T(8,128)(2,1)}, u32[]{:S(2)}, u32[]{:S(2)}) %all-to-all-start.1) | async-done | bytes 7340064 | tf_op jit(solution)/shard_map/all_to_all | solution.py:141
  227.7 4.6 %fusion.77 = (bf16[40,1024]{1,0:T(8,128)(2,1)S(1)}, f32[40,1024]{1,0:T(8,128)S(1)}) fusion(bf16[3584,1024]{1,0:T(8,128)(2,1)} %bitcast.7, bf16[16,3584]{1,0:T(8,128)(2,1)S(1)} %fusion.28, bf16[8,3584]{1,0:T(8,128)(2,1)S(1)} %get-tuple-element.31, bf16[8,3584]{1,0:T(8,128)(2,1)S(1)} %get-tuple-element.32, bf16[8,3584]{1,0:T(8,128)(2,1)S(1)} %get-tuple-element.30), kind=kOutput, calls=%fused_computation.164 | convolution fusion | flops 294789120 | bytes 7872512 | tf_op jit(solution)/shard_map/dot_general | solution.py:160
  232.8 0.8 multiply_reduce_fusion.1
  233.8 5.1 %fusion.43 = f32[8,3584]{1,0:T(8,128)S(1)} fusion(bf16[3584,1024]{1,0:T(8,128)(2,1)} %bitcast.7, f32[8,1024]{1,0:T(8,128)S(1)} %get-tuple-element.25), kind=kOutput, calls=%fused_computation.99 | convolution fusion | flops 58728448 | bytes 7487488 | tf_op jit(solution)/shard_map/dot_general | solution.py:171
  238.9 2.1 select_reduce_fusion.1
  241.6 3.3 select_reduce_fusion
  244.9 4.3 %multiply_reduce_fusion = (f32[8]{0:T(128)S(1)}, f32[8,1024]{1,0:T(8,128)S(1)}) fusion(f32[8,1024]{1,0:T(8,128)S(1)} %get-tuple-element.25, bf16[40,1024]{1,0:T(8,128)(2,1)S(1)} %get-tuple-element.40, f32[8]{0:T(128)S(1)} %get-tuple-element.22, bf16[8,3584]{1,0:T(8,128)(2,1)S(1)} %select_reduce_fusion, bf16[3584,1024]{1,0:T(8,128)(2,1)} %bitcast.7), kind=kOutput, calls=%fused_computation.68 | convolution fusion | flops 58761208 | bytes 7479360 | tf_op jit(solution)/shard_map/dot_general | solution.py:181
  249.2 0.9 fusion.75
  250.9 1.9 all-gather.3
  252.8 13.4 %all-gather.1 = bf16[8,12,2048]{2,1,0:T(8,128)(2,1)S(1)} all-gather(bf16[2,12,2048]{2,1,0:T(8,128)(2,1)S(1)} %all-gather.3), channel_id=3, replica_groups=mesh['oz'=8,'oy'=4,'oc'=2,'neg'=4] {'oy'}, dimensions={0}, use_global_device_ids=true | all-gather | bytes 491520 | tf_op jit(solution)/shard_map/all_gather | solution.py:70
  266.1 1.1 copy.33
  268.0 15.0 %all_to_all.20 = bf16[64,2,192]{2,1,0:T(2,128)(2,1)S(1)} all-to-all(bf16[64,2,192]{2,1,0:T(2,128)(2,1)S(1)} %reshape.937), channel_id=1, replica_groups=mesh['oz'=8,'oy'=4,'oc'=2,'neg'=4] {'oz','oy','oc'}, dimensions={0} | all-to-all | bytes 98304 | tf_op jit(solution)/shard_map/all_to_all | solution.py:62
  283.2 25.8 %all-gather.6.cloned.1.call-done = bf16[32,2,12,2048]{3,1,2,0:T(2,128)(2,1)} async-done(((bf16[4,2,12,2048]{3,1,2,0:T(2,128)(2,1)}), bf16[32,2,12,2048]{3,1,2,0:T(2,128)(2,1)}) %all-gather.6.cloned.1.call-update) | async-done | bytes 3145744 | tf_op jit(solution)/shard_map/all_gather | solution.py:70
  309.0 6.3 %copy.34 = bf16[32,2,12,2048]{3,1,0,2:T(2,128)(2,1)} copy(bf16[32,2,12,2048]{3,1,2,0:T(2,128)(2,1)} %all-gather.6.cloned.1.call-done) | data formatting | bytes 6291456 | tf_op jit(solution)/shard_map/all_gather | solution.py:70
  315.4 5.7 %reshape.899 = bf16[64,12,2048]{2,0,1:T(8,128)(2,1)} reshape(bf16[32,2,12,2048]{3,1,0,2:T(2,128)(2,1)} %copy.34) | data formatting | bytes 6291456 | tf_op jit(solution)/shard_map/reshape | solution.py:71
  321.1 1.7 slice.123
  322.8 1.2 copy.42
  324.7 1.4 add_reduce_fusion
  326.1 0.9 collective-permute-start
  327.0 6.5 %collective-permute-done = f32[52,1024]{1,0:T(8,128)S(1)} collective-permute-done((f32[52,1024]{1,0:T(8,128)S(1)}, f32[52,1024]{1,0:T(8,128)S(1)}, u32[]{:S(2)}, u32[]{:S(2)}) %collective-permute-start) | collective-permute-done | bytes 213024 | tf_op jit(solution)/shard_map/ppermute | solution.py:95
  333.6 1.5 collective-permute-start.1
  335.0 6.6 %collective-permute-done.1 = f32[52,1024]{1,0:T(8,128)S(1)} collective-permute-done((f32[52,1024]{1,0:T(8,128)S(1)}, f32[52,1024]{1,0:T(8,128)S(1)}, u32[]{:S(2)}, u32[]{:S(2)}) %collective-permute-start.1) | collective-permute-done | bytes 213024 | tf_op jit(solution)/shard_map/ppermute | solution.py:95
  (76 shorter events, 8.8 us)
Async XLA Ops:
  7.2 225.2 %copy-start = (bf16[1024,1024]{1,0:T(8,128)(2,1)S(1)}, bf16[1024,1024]{1,0:T(8,128)(2,1)}, u32[]{:S(2)}) copy-start(bf16[1024,1024]{1,0:T(8,128)(2,1)} %param.18) | copy-start | bytes 6291460
  58.1 6.2 %copy-start.3 = (s32[8,50]{1,0:T(8,128)S(1)}, s32[8,50]{1,0:T(8,128)}, u32[]{:S(2)}) copy-start(s32[8,50]{1,0:T(8,128)} %param.12) | copy-start | bytes 4804
  58.1 6.3 %copy-start.4 = (s32[8,50]{1,0:T(8,128)S(1)}, s32[8,50]{1,0:T(8,128)}, u32[]{:S(2)}) copy-start(s32[8,50]{1,0:T(8,128)} %param.13) | copy-start | bytes 4804
  58.1 169.6 %all-to-all-start.1 = ((bf16[64,56,1024]{2,1,0:T(8,128)(2,1)}), bf16[64,56,1024]{2,1,0:T(8,128)(2,1)}, u32[]{:S(2)}, u32[]{:S(2)}) async-start(bf16[64,56,1024]{2,1,0:T(8,128)(2,1)} %bitcast.35), calls=%async_computation.1 | async-start | bytes 14680064 | tf_op jit(solution)/shard_map/all_to_all | solution.py:141
  64.0 168.4 %copy-start.5 = (f32[1024]{0:T(1024)S(1)}, f32[1024]{0:T(1024)}, u32[]{:S(2)}) copy-start(f32[1024]{0:T(1024)} %param.19) | copy-start | bytes 12292
  64.0 168.8 %copy-start.6 = (f32[1024]{0:T(1024)S(1)}, f32[1024]{0:T(1024)}, u32[]{:S(2)}) copy-start(f32[1024]{0:T(1024)} %param.21) | copy-start | bytes 12292
  64.0 245.0 %all-gather.6.cloned.1.call-start = ((), (), s32[]{:S(2)}) async-start(), calls=%async_computation.3 | async-start | bytes 3538944 | tf_op jit(solution)/shard_map/all_gather | solution.py:70
  227.7 5.1 %copy-start.1 = (bf16[2048,1024]{1,0:T(8,128)(2,1)S(1)}, bf16[2048,1024]{1,0:T(8,128)(2,1)}, u32[]{:S(2)}) copy-start(bf16[2048,1024]{1,0:T(8,128)(2,1)} %param.20) | copy-start | bytes 12582916
  233.8 15.4 %copy-start.2 = (f32[8,1024]{1,0:T(8,128)}, f32[8,1024]{1,0:T(8,128)S(1)}, u32[]{:S(2)}) copy-start(f32[8,1024]{1,0:T(8,128)S(1)} %get-tuple-element.25) | copy-start | bytes 98308
  326.1 7.4 %collective-permute-start = (f32[52,1024]{1,0:T(8,128)S(1)}, f32[52,1024]{1,0:T(8,128)S(1)}, u32[]{:S(2)}, u32[]{:S(2)}) collective-permute-start(f32[52,1024]{1,0:T(8,128)S(1)} %pad_maximum_fusion), channel_id=1, source_target_pairs={{0,1},{1,0},{2,3},{3,2},{4,5},{5,4},{6,7},{7,6},{8,9},{9,8},{10,11... | collective-permute-start | bytes 638984 | tf_op jit(solution)/shard_map/ppermute | solution.py:95
  333.6 8.0 %collective-permute-start.1 = (f32[52,1024]{1,0:T(8,128)S(1)}, f32[52,1024]{1,0:T(8,128)S(1)}, u32[]{:S(2)}, u32[]{:S(2)}) collective-permute-start(f32[52,1024]{1,0:T(8,128)S(1)} %fusion.69), channel_id=1, source_target_pairs={{0,2},{1,3},{2,0},{3,1},{4,6},{5,7},{6,4},{7,5},{8,10},{9,11},{10,... | collective-permute-start | bytes 638984 | tf_op jit(solution)/shard_map/ppermute | solution.py:95
Sparse Core Ops, SparseCore 0:
  267.4 41.5 all-gather.5

commit v7 on v5

--- a/solution.py
+++ b/solution.py
@@ -65,9 +65,8 @@
     stats_lo = (stats - stats_hi.astype(jnp.float32)).astype(jnp.bfloat16)
     payload = jnp.concatenate([d_conv_b, d_pool_b], axis=1)
     payload = jnp.concatenate([payload, stats_hi, stats_lo], axis=0)
-    gathered = payload
-    for axis in OWNER[::-1]:
-        gathered = lax.all_gather(gathered, axis, axis=0)
+    gathered = lax.all_gather(payload, OWNER[2], axis=0)
+    gathered = lax.all_gather(gathered, OWNER[:2], axis=0)
     gathered = gathered.reshape((owners,) + payload.shape)
     right = gathered[:, :queries].reshape(owners * queries, payload.shape[1])
     stat_rows = stats.shape[0]

time: 352 us -> 365 us (1.037)
  waiting for transfers between devices: 201 us -> 239 us
  local copies, waits for them, and re-layouts: 55.9 us -> 42.8 us
  blocking collectives: 51.9 us -> 39.2 us
    all_gather x1, waiting for transfers between devices: 25.8 us -> 62.1 us  [weight_grads(): gathered = lax.all_gather(gathered, OWNER[:2], axis=0)]
    all_gather x2 -> x1, blocking collectives: 15.3 us -> 2.03 us  [weight_grads(): gathered = lax.all_gather(payload, OWNER[2], axis=0)]
    all_gather x2 -> x0, local copies, waits for them, and re-layouts: 7.49 us -> none  [weight_grads(): gathered = lax.all_gather(gathered, axis, axis=0)]
    reshape x1, local copies, waits for them, and re-layouts: 5.74 us -> 1.73 us  [weight_grads(): right = gathered[:, :queries].reshape(owners * queries, payload.shape[1])]
where the time goes in v7:
time: 365 us; the launch traced here: 364 us
  waiting for transfers between devices  239 us (65%)
  local copies, waits for them, and re-layouts  42.8 us (12%)
  blocking collectives  39.2 us (11%)
  between operations  15.1 us (4%)
  matrix products  12.4 us (3%)
  other arithmetic  8.06 us (2%)
  starting transfers between devices  7.09 us (2%)
    all_to_all x1, waiting for transfers between devices, local(): lax.all_to_all(table[served.reshape(-1)].reshape(owners, slots, width), O...  163 us
    all_gather x1, waiting for transfers between devices, weight_grads(): gathered = lax.all_gather(gathered, OWNER[:2], axis=0)  62.1 us
    all_to_all x1, blocking collectives, local(): lax.all_to_all(all_requests, OWNER, split_axis=0, concat_axis=0, tiled=True)  21.5 us
    gather x1, local copies, waits for them, and re-layouts, local(): table[served.reshape(-1)].reshape(owners, slots, width)  20.8 us
    all_to_all x1, blocking collectives, weight_grads(): left = lax.all_to_all(left, OWNER, split_axis=0, concat_axis=0, tiled=True)  15.6 us
    ppermute x2, waiting for transfers between devices, pair_sum(): lax.ppermute(values, 'neg', [(i, i ^ step) for i in range(groups)])  14.9 us
  transfers between devices with their start and end apart: 4, of which 4 were waited for; matrix products, arithmetic and copies ran while one was open for 0% of the time, Pallas kernels for 0%

profile of v7, /device:TPU:6, one launch (start us, length us, event | category | flops | bytes accessed | tf_op | source)
XLA Modules:
  0.0 364.2 jit_solution(8500312684695146535)
XLA Ops:
  7.2 0.9 reshape.952
  8.1 0.8 reshape.951
  9.7 0.8 concatenate.107
  10.6 0.8 concatenate.103
  11.4 0.6 fusion.8
  12.0 2.0 fusion.3
  14.3 21.5 %all_to_all.19 = s32[64,1,56]{2,1,0:T(1,128)S(1)} all-to-all(s32[64,1,56]{2,1,0:T(1,128)S(1)} %bitcast.79), channel_id=1, replica_groups=mesh['oz'=8,'oy'=4,'oc'=2,'neg'=4] {'oz','oy','oc'}, dimensions={0} | all-to-all | bytes 28672 | tf_op jit(solution)/shard_map/all_to_all | solution.py:139
  36.4 0.7 reduce.19
  37.3 20.8 %gather_fusion = bf16[3584,1024]{1,0:T(8,128)(2,1)} fusion(bf16[4096,1024]{1,0:T(8,128)(2,1)} %param.17, s32[4096]{0:T(1024)S(1)} %pad_clamp_fusion), kind=kCustom, calls=%fused_computation | custom fusion | bytes 14694400 | tf_op jit(solution)/shard_map/gather | solution.py:141
  58.1 5.8 %all-to-all-start.1 = ((bf16[64,56,1024]{2,1,0:T(8,128)(2,1)}), bf16[64,56,1024]{2,1,0:T(8,128)(2,1)}, u32[]{:S(2)}, u32[]{:S(2)}) async-start(bf16[64,56,1024]{2,1,0:T(8,128)(2,1)} %bitcast.73), calls=%async_computation.1 | async-start | bytes 14680064 | tf_op jit(solution)/shard_map/all_to_all | solution.py:140
  65.2 162.5 %all-to-all-done.1 = bf16[64,56,1024]{2,1,0:T(8,128)(2,1)} async-done(((bf16[64,56,1024]{2,1,0:T(8,128)(2,1)}), bf16[64,56,1024]{2,1,0:T(8,128)(2,1)}, u32[]{:S(2)}, u32[]{:S(2)}) %all-to-all-start.1) | async-done | bytes 7340064 | tf_op jit(solution)/shard_map/all_to_all | solution.py:140
  227.7 3.1 slice.121
  230.8 0.8 convolution_convert_fusion
  231.7 2.8 slice.123
  234.5 0.9 convolution_convert_fusion.1
  235.8 0.8 multiply_reduce_fusion.1
  236.8 1.5 fusion.33
  238.3 6.7 %gather_fusion.1 = f32[1024]{0:T(1024)S(1)} fusion(f32[8,2560]{1,0:T(8,128)S(1)} %fusion.33, s32[1024]{0:T(1024)S(1)} %fusion.47), kind=kCustom, calls=%fused_computation.1 | custom fusion | bytes 16384 | tf_op jit(solution)/shard_map/jit(take_along_axis)/gather | solution.py:171
  245.0 0.7 fusion.67
  246.4 2.0 select_reduce_fusion
  248.4 3.4 multiply_reduce_fusion
  251.9 0.7 fusion.69
  252.7 2.0 all-gather.2
  255.4 15.6 %all_to_all.20 = bf16[64,2,192]{2,1,0:T(2,128)(2,1)S(1)} all-to-all(bf16[64,2,192]{2,1,0:T(2,128)(2,1)S(1)} %reshape.1005), channel_id=1, replica_groups=mesh['oz'=8,'oy'=4,'oc'=2,'neg'=4] {'oz','oy','oc'}, dimensions={0} | all-to-all | bytes 98304 | tf_op jit(solution)/shard_map/all_to_all | solution.py:62
  271.2 62.1 %all-gather.5.cloned.1.call-done = bf16[64,12,2048]{2,1,0:T(8,128)(2,1)} async-done(((bf16[2,12,2048]{2,1,0:T(8,128)(2,1)}), bf16[64,12,2048]{2,1,0:T(8,128)(2,1)}) %all-gather.5.cloned.1.call-update) | async-done | bytes 3145744 | tf_op jit(solution)/shard_map/all_gather | solution.py:69
  333.2 1.7 slice_bitcast_fusion
  335.7 3.2 add_reduce_fusion
  338.9 0.9 collective-permute-start
  339.9 7.3 %collective-permute-done = f32[52,1024]{1,0:T(8,128)S(1)} collective-permute-done((f32[52,1024]{1,0:T(8,128)S(1)}, f32[52,1024]{1,0:T(8,128)S(1)}, u32[]{:S(2)}, u32[]{:S(2)}) %collective-permute-start) | collective-permute-done | bytes 213024 | tf_op jit(solution)/shard_map/ppermute | solution.py:94
  347.3 7.5 %collective-permute-done.1 = f32[52,1024]{1,0:T(8,128)S(1)} collective-permute-done((f32[52,1024]{1,0:T(8,128)S(1)}, f32[52,1024]{1,0:T(8,128)S(1)}, u32[]{:S(2)}, u32[]{:S(2)}) %collective-permute-start.1) | collective-permute-done | bytes 213024 | tf_op jit(solution)/shard_map/ppermute | solution.py:94
  356.0 0.6 slice.135
  356.7 0.7 slice.137
  (77 shorter events, 6.6 us)
Async XLA Ops:
  7.2 228.2 %copy-start = (bf16[1024,1024]{1,0:T(8,128)(2,1)S(1)}, bf16[1024,1024]{1,0:T(8,128)(2,1)}, u32[]{:S(2)}) copy-start(bf16[1024,1024]{1,0:T(8,128)(2,1)} %param.18) | copy-start | bytes 6291460
  58.1 6.2 %copy-start.6 = (s32[8,50]{1,0:T(8,128)S(1)}, s32[8,50]{1,0:T(8,128)}, u32[]{:S(2)}) copy-start(s32[8,50]{1,0:T(8,128)} %param.13) | copy-start | bytes 4804
  58.1 6.5 %copy-start.5 = (s32[8,50]{1,0:T(8,128)S(1)}, s32[8,50]{1,0:T(8,128)}, u32[]{:S(2)}) copy-start(s32[8,50]{1,0:T(8,128)} %param.12) | copy-start | bytes 4804
  58.1 169.6 %all-to-all-start.1 = ((bf16[64,56,1024]{2,1,0:T(8,128)(2,1)}), bf16[64,56,1024]{2,1,0:T(8,128)(2,1)}, u32[]{:S(2)}, u32[]{:S(2)}) async-start(bf16[64,56,1024]{2,1,0:T(8,128)(2,1)} %bitcast.73), calls=%async_computation.1 | async-start | bytes 14680064 | tf_op jit(solution)/shard_map/all_to_all | solution.py:140
  64.0 269.3 %all-gather.5.cloned.1.call-start = ((), (), s32[]{:S(2)}) async-start(), calls=%async_computation.3 | async-start | bytes 4325376 | tf_op jit(solution)/shard_map/all_gather | solution.py:69
  230.8 6.0 %copy-start.1 = (bf16[64,40,1024]{2,1,0:T(8,128)(2,1)}, bf16[64,40,1024]{2,1,0:T(8,128)(2,1)S(1)}, u32[]{:S(2)}) copy-start(bf16[64,40,1024]{2,1,0:T(8,128)(2,1)S(1)} %slice.121) | copy-start | bytes 15728644
  231.6 3.8 %copy-start.7 = (f32[1024]{0:T(1024)S(1)}, f32[1024]{0:T(1024)}, u32[]{:S(2)}) copy-start(f32[1024]{0:T(1024)} %param.19) | copy-start | bytes 12292
  231.6 4.2 %copy-start.2 = (bf16[2048,1024]{1,0:T(8,128)(2,1)S(1)}, bf16[2048,1024]{1,0:T(8,128)(2,1)}, u32[]{:S(2)}) copy-start(bf16[2048,1024]{1,0:T(8,128)(2,1)} %param.20) | copy-start | bytes 12582916
  231.7 4.2 %copy-start.8 = (f32[1024]{0:T(1024)S(1)}, f32[1024]{0:T(1024)}, u32[]{:S(2)}) copy-start(f32[1024]{0:T(1024)} %param.21) | copy-start | bytes 12292
  236.8 15.0 %copy-start.4 = (f32[8,1024]{1,0:T(8,128)}, f32[8,1024]{1,0:T(8,128)S(1)}, u32[]{:S(2)}) copy-start(f32[8,1024]{1,0:T(8,128)S(1)} %get-tuple-element.25) | copy-start | bytes 98308
  246.4 5.5 %copy-start.3 = (bf16[2048,1024]{1,0:T(8,128)(2,1)S(1)}, bf16[2048,1024]{1,0:T(8,128)(2,1)}, u32[]{:S(2)}) copy-start(bf16[2048,1024]{1,0:T(8,128)(2,1)} %param.20) | copy-start | bytes 12582916
  338.9 8.3 %collective-permute-start = (f32[52,1024]{1,0:T(8,128)S(1)}, f32[52,1024]{1,0:T(8,128)S(1)}, u32[]{:S(2)}, u32[]{:S(2)}) collective-permute-start(f32[52,1024]{1,0:T(8,128)S(1)} %pad_maximum_fusion), channel_id=1, source_target_pairs={{0,1},{1,0},{2,3},{3,2},{4,5},{5,4},{6,7},{7,6},{8,9},{9,8},{10,11... | collective-permute-start | bytes 638984 | tf_op jit(solution)/shard_map/ppermute | solution.py:94
  347.2 7.6 %collective-permute-start.1 = (f32[52,1024]{1,0:T(8,128)S(1)}, f32[52,1024]{1,0:T(8,128)S(1)}, u32[]{:S(2)}, u32[]{:S(2)}) collective-permute-start(f32[52,1024]{1,0:T(8,128)S(1)} %fusion.64), channel_id=1, source_target_pairs={{0,2},{1,3},{2,0},{3,1},{4,6},{5,7},{6,4},{7,5},{8,10},{9,11},{10,... | collective-permute-start | bytes 638984 | tf_op jit(solution)/shard_map/ppermute | solution.py:94
Sparse Core Ops, SparseCore 0:
  254.8 78.3 all-gather.4

commit v8 on v7

--- a/solution.py
+++ b/solution.py
@@ -60,20 +60,21 @@
         axis=2,
     )
     left = lax.all_to_all(left, OWNER, split_axis=0, concat_axis=0, tiled=True)
-    left = left.reshape(owners * queries, conv_rows + pool_rows)
     stats_hi = stats.astype(jnp.bfloat16)
     stats_lo = (stats - stats_hi.astype(jnp.float32)).astype(jnp.bfloat16)
     payload = jnp.concatenate([d_conv_b, d_pool_b], axis=1)
     payload = jnp.concatenate([payload, stats_hi, stats_lo], axis=0)
     gathered = lax.all_gather(payload, OWNER[2], axis=0)
-    gathered = lax.all_gather(gathered, OWNER[:2], axis=0)
-    gathered = gathered.reshape((owners,) + payload.shape)
-    right = gathered[:, :queries].reshape(owners * queries, payload.shape[1])
+    gathered = lax.all_gather(gathered, OWNER[1], axis=0)
+    ring = ring_gather(gathered, OWNER[0], lax.axis_size(OWNER[0]))
+    here = lax.axis_index(OWNER[0])
+    left = jnp.roll(left.reshape((ring.shape[0], -1) + left.shape[1:]), -here, axis=0)
+    left = left.reshape(owners * queries, conv_rows + pool_rows)
+    right = ring[:, :, :, :queries].reshape(owners * queries, payload.shape[1])
     stat_rows = stats.shape[0]
+    stat_parts = jnp.roll(ring[:, :, :, queries:], here, axis=0).astype(jnp.float32)
     stats_sum = jnp.sum(
-        gathered[:, queries : queries + stat_rows].astype(jnp.float32)
-        + gathered[:, queries + stat_rows :].astype(jnp.float32),
-        axis=0,
+        stat_parts[:, :, :, :stat_rows] + stat_parts[:, :, :, stat_rows:], axis=(0, 1, 2)
     )
     contract_rows = (((0,), (0,)), ((), ()))
     conv_width = d_conv_b.shape[1]
@@ -86,6 +87,18 @@
         preferred_element_type=jnp.float32,
     )
     return pool_part, conv_part, stats_sum
+
+
+def ring_gather(block, axis, size):
+    ahead, behind = [], []
+    forward_part, backward_part = block, block
+    for step in range(1, size // 2 + 1):
+        forward_part = lax.ppermute(forward_part, axis, [(i, (i + 1) % size) for i in range(size)])
+        behind.append(forward_part)
+        if 2 * step < size:
+            backward_part = lax.ppermute(backward_part, axis, [(i, (i - 1) % size) for i in range(size)])
+            ahead.append(backward_part)
+    return jnp.stack([block] + ahead + behind[::-1])
 
 
 def pair_sum(values, groups):

time: 365 us -> 352 us (0.964)
  waiting for transfers between devices: 239 us -> 221 us
  between operations: 15.1 us -> 1.75 us
  starting transfers between devices: 7.09 us -> 18.6 us
  local copies, waits for them, and re-layouts: 42.8 us -> 53.4 us
    all_gather x1 -> x0, waiting for transfers between devices: 62.1 us -> none  [weight_grads(): gathered = lax.all_gather(gathered, OWNER[:2], axis=0)]
    ppermute x0 -> x7, waiting for transfers between devices: none -> 35.3 us  [the longest x4 25 us: ring_gather(): lax.ppermute(forward_part, axis, [(i, (i + 1) % size) for i in range(size)])]
    all_to_all x1 -> x0, blocking collectives: 15.6 us -> none  [weight_grads(): left = lax.all_to_all(left, OWNER, split_axis=0, concat_axis=0, tiled=True)]
    all_gather x0 -> x1, blocking collectives: none -> 13.4 us  [weight_grads(): gathered = lax.all_gather(gathered, OWNER[1], axis=0)]
    all_to_all x0 -> x1, waiting for transfers between devices: none -> 8.98 us  [weight_grads(): left = lax.all_to_all(left, OWNER, split_axis=0, concat_axis=0, tiled=True)]
    unnamed x20 -> x27, local copies, waits for them, and re-layouts: 0.33 us -> 7.9 us
    ppermute x0 -> x7, starting transfers between devices: none -> 6.16 us  [the longest x4 4.1 us: ring_gather(): lax.ppermute(forward_part, axis, [(i, (i + 1) % size) for i in range(size)])]
    all_to_all x0 -> x1, starting transfers between devices: none -> 5.43 us  [weight_grads(): left = lax.all_to_all(left, OWNER, split_axis=0, concat_axis=0, tiled=True)]
  transfers between devices with their start and end apart: 4 -> 11, of which waited for: 4 -> 7; matrix products, arithmetic and copies ran while one was open for 0% -> 2% of each run, Pallas kernels for 0% -> 0%
where the time goes in v8:
time: 352 us; the launch traced here: 351 us
  waiting for transfers between devices  221 us (63%)
  local copies, waits for them, and re-layouts  53.4 us (15%)
  blocking collectives  36.9 us (10%)
  starting transfers between devices  18.6 us (5%)
  matrix products  12.4 us (4%)
  other arithmetic  6.87 us (2%)
    all_to_all x1, waiting for transfers between devices, local(): lax.all_to_all(table[served.reshape(-1)].reshape(owners, slots, width), O...  163 us
    ppermute x4, waiting for transfers between devices, ring_gather(): lax.ppermute(forward_part, axis, [(i, (i + 1) % size) for i in range(size)])  25 us
    all_to_all x1, blocking collectives, local(): lax.all_to_all(all_requests, OWNER, split_axis=0, concat_axis=0, tiled=True)  21.5 us
    gather x1, local copies, waits for them, and re-layouts, local(): table[served.reshape(-1)].reshape(owners, slots, width)  20.8 us
    ppermute x2, waiting for transfers between devices, pair_sum(): lax.ppermute(values, 'neg', [(i, i ^ step) for i in range(groups)])  14.6 us
    all_gather x1, blocking collectives, weight_grads(): gathered = lax.all_gather(gathered, OWNER[1], axis=0)  13.4 us
    ppermute x3, waiting for transfers between devices, ring_gather(): lax.ppermute(backward_part, axis, [(i, (i - 1) % size) for i in range(siz...  10.2 us
    all_to_all x1, waiting for transfers between devices, weight_grads(): left = lax.all_to_all(left, OWNER, split_axis=0, concat_axis=0, tiled=True)  8.98 us
  transfers between devices with their start and end apart: 11, of which 7 were waited for; matrix products, arithmetic and copies ran while one was open for 2% of the time, Pallas kernels for 0%

profile of v8, /device:TPU:6, one launch (start us, length us, event | category | flops | bytes accessed | tf_op | source)
XLA Modules:
  0.0 351.3 jit_solution(9340036942730123489)
XLA Ops:
  0.6 0.9 reshape.952
  4.7 2.0 fusion.3
  7.8 21.5 %all_to_all.19 = s32[64,1,56]{2,1,0:T(1,128)S(1)} all-to-all(s32[64,1,56]{2,1,0:T(1,128)S(1)} %bitcast.101), channel_id=1, replica_groups=mesh['oz'=8,'oy'=4,'oc'=2,'neg'=4] {'oz','oy','oc'}, dimensions={0} | all-to-all | bytes 28672 | tf_op jit(solution)/shard_map/all_to_all | solution.py:152
  30.7 20.8 %gather_fusion = bf16[3584,1024]{1,0:T(8,128)(2,1)} fusion(bf16[4096,1024]{1,0:T(8,128)(2,1)} %param.17, s32[4096]{0:T(1024)S(1)} %pad_clamp_fusion), kind=kCustom, calls=%fused_computation | custom fusion | bytes 14694400 | tf_op jit(solution)/shard_map/gather | solution.py:154
  51.6 6.0 %all-to-all-start.1 = ((bf16[64,56,1024]{2,1,0:T(8,128)(2,1)}), bf16[64,56,1024]{2,1,0:T(8,128)(2,1)}, u32[]{:S(2)}, u32[]{:S(2)}) async-start(bf16[64,56,1024]{2,1,0:T(8,128)(2,1)} %bitcast.89), calls=%async_computation.1 | async-start | bytes 14680064 | tf_op jit(solution)/shard_map/all_to_all | solution.py:153
  58.6 162.5 %all-to-all-done.1 = bf16[64,56,1024]{2,1,0:T(8,128)(2,1)} async-done(((bf16[64,56,1024]{2,1,0:T(8,128)(2,1)}), bf16[64,56,1024]{2,1,0:T(8,128)(2,1)}, u32[]{:S(2)}, u32[]{:S(2)}) %all-to-all-start.1) | async-done | bytes 7340064 | tf_op jit(solution)/shard_map/all_to_all | solution.py:153
  221.1 3.1 slice.125
  225.1 2.8 slice.127
  227.9 0.9 convolution_convert_fusion.1
  230.3 1.5 fusion.37
  231.7 6.7 %gather_fusion.1 = f32[1024]{0:T(1024)S(1)} fusion(f32[8,2560]{1,0:T(8,128)S(1)} %fusion.37, s32[1024]{0:T(1024)S(1)} %fusion.51), kind=kCustom, calls=%fused_computation.1 | custom fusion | bytes 16384 | tf_op jit(solution)/shard_map/jit(take_along_axis)/gather | solution.py:184
  239.2 2.0 select_reduce_fusion
  241.2 3.4 multiply_reduce_fusion
  246.1 1.9 all-gather.2
  248.0 13.4 %all-gather.1 = bf16[8,12,2048]{2,1,0:T(8,128)(2,1)S(1)} all-gather(bf16[2,12,2048]{2,1,0:T(8,128)(2,1)S(1)} %all-gather.2), channel_id=3, replica_groups=mesh['oz'=8,'oy'=4,'oc'=2,'neg'=4] {'oy'}, dimensions={0}, use_global_device_ids=true | all-gather | bytes 491520 | tf_op jit(solution)/shard_map/all_gather | solution.py:68
  261.4 2.0 collective-permute-start.3
  264.8 5.4 %all-to-all-start.2 = ((bf16[64,2,192]{2,1,0:T(2,128)(2,1)}), bf16[64,2,192]{2,1,0:T(2,128)(2,1)S(1)}, u32[]{:S(2)}, u32[]{:S(2)}) async-start(bf16[64,2,192]{2,1,0:T(2,128)(2,1)} %reshape.1005), calls=%async_computation.2 | async-start | bytes 131072 | tf_op jit(solution)/shard_map/all_to_all | solution.py:62
  271.0 9.0 %all-to-all-done.2 = bf16[64,2,192]{2,1,0:T(2,128)(2,1)S(1)} async-done(((bf16[64,2,192]{2,1,0:T(2,128)(2,1)}), bf16[64,2,192]{2,1,0:T(2,128)(2,1)S(1)}, u32[]{:S(2)}, u32[]{:S(2)}) %all-to-all-start.2) | async-done | bytes 49184 | tf_op jit(solution)/shard_map/all_to_all | solution.py:62
  280.7 1.6 collective-permute-start.4
  282.4 1.9 bitcast_dynamic-update-slice_fusion.6
  284.2 10.2 %collective-permute-done.1 = bf16[4,2,12,2048]{3,2,1,0:T(8,128)(2,1)S(1)} collective-permute-done((bf16[4,2,12,2048]{3,2,1,0:T(8,128)(2,1)}, bf16[4,2,12,2048]{3,2,1,0:T(8,128)(2,1)S(1)}, u32[]{:S(2)}, u32[]{:S(2)}) %collective-permute-start.1) | collective-permute-done | bytes 393248 | tf_op jit(solution)/shard_map/ppermute | solution.py:99
  294.5 1.6 collective-permute-start.2
  296.5 0.9 bitcast_dynamic-update-slice_fusion.5
  297.4 12.7 %collective-permute-done.5 = bf16[4,2,12,2048]{3,2,1,0:T(8,128)(2,1)S(1)} collective-permute-done((bf16[4,2,12,2048]{3,2,1,0:T(8,128)(2,1)S(1)}, bf16[4,2,12,2048]{3,2,1,0:T(8,128)(2,1)S(1)}, u32[]{:S(2)}, u32[]{:S(2)}) %collective-permute-start.5) | collective-permute-done | bytes 393248 | tf_op jit(solution)/shard_map/ppermute | solution.py:96
  310.1 0.8 bitcast_dynamic-update-slice_fusion.4
  311.0 12.3 %collective-permute-done.6 = bf16[4,2,12,2048]{3,2,1,0:T(8,128)(2,1)S(1)} collective-permute-done((bf16[4,2,12,2048]{3,2,1,0:T(8,128)(2,1)S(1)}, bf16[4,2,12,2048]{3,2,1,0:T(8,128)(2,1)S(1)}, u32[]{:S(2)}, u32[]{:S(2)}) %collective-permute-start.6) | collective-permute-done | bytes 393248 | tf_op jit(solution)/shard_map/ppermute | solution.py:96
  326.6 1.7 slice.131
  329.0 2.1 slice.135
  331.2 1.2 fusion.15
  333.2 0.9 collective-permute-start.7
  334.1 7.0 %collective-permute-done.7 = f32[52,1024]{1,0:T(8,128)S(1)} collective-permute-done((f32[52,1024]{1,0:T(8,128)S(1)}, f32[52,1024]{1,0:T(8,128)S(1)}, u32[]{:S(2)}, u32[]{:S(2)}) %collective-permute-start.7) | collective-permute-done | bytes 213024 | tf_op jit(solution)/shard_map/ppermute | solution.py:107
  341.3 7.5 %collective-permute-done.8 = f32[52,1024]{1,0:T(8,128)S(1)} collective-permute-done((f32[52,1024]{1,0:T(8,128)S(1)}, f32[52,1024]{1,0:T(8,128)S(1)}, u32[]{:S(2)}, u32[]{:S(2)}) %collective-permute-start.8) | collective-permute-done | bytes 213024 | tf_op jit(solution)/shard_map/ppermute | solution.py:107
  (101 shorter events, 20.8 us)
Async XLA Ops:
  0.6 228.2 %copy-start = (bf16[1024,1024]{1,0:T(8,128)(2,1)S(1)}, bf16[1024,1024]{1,0:T(8,128)(2,1)}, u32[]{:S(2)}) copy-start(bf16[1024,1024]{1,0:T(8,128)(2,1)} %param.18) | copy-start | bytes 6291460
  51.6 6.2 %copy-start.5 = (s32[8,50]{1,0:T(8,128)S(1)}, s32[8,50]{1,0:T(8,128)}, u32[]{:S(2)}) copy-start(s32[8,50]{1,0:T(8,128)} %param.12) | copy-start | bytes 4804
  51.6 6.3 %copy-start.6 = (s32[8,50]{1,0:T(8,128)S(1)}, s32[8,50]{1,0:T(8,128)}, u32[]{:S(2)}) copy-start(s32[8,50]{1,0:T(8,128)} %param.13) | copy-start | bytes 4804
  51.6 169.6 %all-to-all-start.1 = ((bf16[64,56,1024]{2,1,0:T(8,128)(2,1)}), bf16[64,56,1024]{2,1,0:T(8,128)(2,1)}, u32[]{:S(2)}, u32[]{:S(2)}) async-start(bf16[64,56,1024]{2,1,0:T(8,128)(2,1)} %bitcast.89), calls=%async_computation.1 | async-start | bytes 14680064 | tf_op jit(solution)/shard_map/all_to_all | solution.py:153
  224.2 6.0 %copy-start.1 = (bf16[64,40,1024]{2,1,0:T(8,128)(2,1)}, bf16[64,40,1024]{2,1,0:T(8,128)(2,1)S(1)}, u32[]{:S(2)}) copy-start(bf16[64,40,1024]{2,1,0:T(8,128)(2,1)S(1)} %slice.125) | copy-start | bytes 15728644
  225.1 3.8 %copy-start.7 = (f32[1024]{0:T(1024)S(1)}, f32[1024]{0:T(1024)}, u32[]{:S(2)}) copy-start(f32[1024]{0:T(1024)} %param.19) | copy-start | bytes 12292
  225.1 4.2 %copy-start.2 = (bf16[2048,1024]{1,0:T(8,128)(2,1)S(1)}, bf16[2048,1024]{1,0:T(8,128)(2,1)}, u32[]{:S(2)}) copy-start(bf16[2048,1024]{1,0:T(8,128)(2,1)} %param.20) | copy-start | bytes 12582916
  225.1 4.2 %copy-start.8 = (f32[1024]{0:T(1024)S(1)}, f32[1024]{0:T(1024)}, u32[]{:S(2)}) copy-start(f32[1024]{0:T(1024)} %param.21) | copy-start | bytes 12292
  230.3 14.3 %copy-start.4 = (f32[8,1024]{1,0:T(8,128)}, f32[8,1024]{1,0:T(8,128)S(1)}, u32[]{:S(2)}) copy-start(f32[8,1024]{1,0:T(8,128)S(1)} %get-tuple-element.25) | copy-start | bytes 98308
  238.5 6.2 %copy-start.3 = (bf16[2048,1024]{1,0:T(8,128)(2,1)S(1)}, bf16[2048,1024]{1,0:T(8,128)(2,1)}, u32[]{:S(2)}) copy-start(bf16[2048,1024]{1,0:T(8,128)(2,1)} %param.20) | copy-start | bytes 12582916
  261.4 18.8 %collective-permute-start = (bf16[4,2,12,2048]{3,2,1,0:T(8,128)(2,1)S(1)}, bf16[4,2,12,2048]{3,2,1,0:T(8,128)(2,1)}, u32[]{:S(2)}, u32[]{:S(2)}) collective-permute-start(bf16[4,2,12,2048]{3,2,1,0:T(8,128)(2,1)S(1)} %bitcast.93), channel_id=1, source_target_pairs={{0,224},{32,0},{64,32},{96,64},{128,96},{160,128},{192,160},{224,1... | collective-permute-start | bytes 1179656 | tf_op jit(solution)/shard_map/ppermute | solution.py:99
  261.4 19.3 %collective-permute-start.3 = (bf16[4,2,12,2048]{3,2,1,0:T(8,128)(2,1)S(1)}, bf16[4,2,12,2048]{3,2,1,0:T(8,128)(2,1)S(1)}, u32[]{:S(2)}, u32[]{:S(2)}) collective-permute-start(bf16[4,2,12,2048]{3,2,1,0:T(8,128)(2,1)S(1)} %bitcast.94), channel_id=1, source_target_pairs={{0,32},{32,64},{64,96},{96,128},{128,160},{160,192},{192,224},{224... | collective-permute-start | bytes 1179656 | tf_op jit(solution)/shard_map/ppermute | solution.py:96
  264.8 15.2 %all-to-all-start.2 = ((bf16[64,2,192]{2,1,0:T(2,128)(2,1)}), bf16[64,2,192]{2,1,0:T(2,128)(2,1)S(1)}, u32[]{:S(2)}, u32[]{:S(2)}) async-start(bf16[64,2,192]{2,1,0:T(2,128)(2,1)} %reshape.1005), calls=%async_computation.2 | async-start | bytes 131072 | tf_op jit(solution)/shard_map/all_to_all | solution.py:62
  280.2 14.2 %collective-permute-start.1 = (bf16[4,2,12,2048]{3,2,1,0:T(8,128)(2,1)}, bf16[4,2,12,2048]{3,2,1,0:T(8,128)(2,1)S(1)}, u32[]{:S(2)}, u32[]{:S(2)}) collective-permute-start(bf16[4,2,12,2048]{3,2,1,0:T(8,128)(2,1)} %collective-permute-done), channel_id=1, source_target_pairs={{0,224},{32,0},{64,32},{96,64},{128,96},{160,128},{192,160},{224,1... | collective-permute-start | bytes 1179656 | tf_op jit(solution)/shard_map/ppermute | solution.py:99
  280.7 15.4 %collective-permute-start.4 = (bf16[4,2,12,2048]{3,2,1,0:T(8,128)(2,1)S(1)}, bf16[4,2,12,2048]{3,2,1,0:T(8,128)(2,1)S(1)}, u32[]{:S(2)}, u32[]{:S(2)}) collective-permute-start(bf16[4,2,12,2048]{3,2,1,0:T(8,128)(2,1)S(1)} %collective-permute-done.3), channel_id=1, source_target_pairs={{0,32},{32,64},{64,96},{96,128},{128,160},{160,192},{192,224},{224... | collective-permute-start | bytes 1179656 | tf_op jit(solution)/shard_map/ppermute | solution.py:96
  294.5 15.6 %collective-permute-start.2 = (bf16[4,2,12,2048]{3,2,1,0:T(8,128)(2,1)S(1)}, bf16[4,2,12,2048]{3,2,1,0:T(8,128)(2,1)S(1)}, u32[]{:S(2)}, u32[]{:S(2)}) collective-permute-start(bf16[4,2,12,2048]{3,2,1,0:T(8,128)(2,1)S(1)} %collective-permute-done.1), channel_id=1, source_target_pairs={{0,224},{32,0},{64,32},{96,64},{128,96},{160,128},{192,160},{224,1... | collective-permute-start | bytes 1179656 | tf_op jit(solution)/shard_map/ppermute | solution.py:99
  296.1 14.0 %collective-permute-start.5 = (bf16[4,2,12,2048]{3,2,1,0:T(8,128)(2,1)S(1)}, bf16[4,2,12,2048]{3,2,1,0:T(8,128)(2,1)S(1)}, u32[]{:S(2)}, u32[]{:S(2)}) collective-permute-start(bf16[4,2,12,2048]{3,2,1,0:T(8,128)(2,1)S(1)} %collective-permute-done.4), channel_id=1, source_target_pairs={{0,32},{32,64},{64,96},{96,128},{128,160},{160,192},{192,224},{224... | collective-permute-start | bytes 1179656 | tf_op jit(solution)/shard_map/ppermute | solution.py:96
  310.1 13.2 %collective-permute-start.6 = (bf16[4,2,12,2048]{3,2,1,0:T(8,128)(2,1)S(1)}, bf16[4,2,12,2048]{3,2,1,0:T(8,128)(2,1)S(1)}, u32[]{:S(2)}, u32[]{:S(2)}) collective-permute-start(bf16[4,2,12,2048]{3,2,1,0:T(8,128)(2,1)S(1)} %collective-permute-done.5), channel_id=1, source_target_pairs={{0,32},{32,64},{64,96},{96,128},{128,160},{160,192},{192,224},{224... | collective-permute-start | bytes 1179656 | tf_op jit(solution)/shard_map/ppermute | solution.py:96
  333.2 8.0 %collective-permute-start.7 = (f32[52,1024]{1,0:T(8,128)S(1)}, f32[52,1024]{1,0:T(8,128)S(1)}, u32[]{:S(2)}, u32[]{:S(2)}) collective-permute-start(f32[52,1024]{1,0:T(8,128)S(1)} %pad_maximum_fusion), channel_id=1, source_target_pairs={{0,1},{1,0},{2,3},{3,2},{4,5},{5,4},{6,7},{7,6},{8,9},{9,8},{10,11... | collective-permute-start | bytes 638984 | tf_op jit(solution)/shard_map/ppermute | solution.py:107
  341.2 7.6 %collective-permute-start.8 = (f32[52,1024]{1,0:T(8,128)S(1)}, f32[52,1024]{1,0:T(8,128)S(1)}, u32[]{:S(2)}, u32[]{:S(2)}) collective-permute-start(f32[52,1024]{1,0:T(8,128)S(1)} %fusion.68), channel_id=1, source_target_pairs={{0,2},{1,3},{2,0},{3,1},{4,6},{5,7},{6,4},{7,5},{8,10},{9,11},{10,... | collective-permute-start | bytes 638984 | tf_op jit(solution)/shard_map/ppermute | solution.py:107

commit v9 on v8

--- a/solution.py
+++ b/solution.py
@@ -150,12 +150,14 @@
     slots = capacity + page_cap
     all_requests = jnp.concatenate([requests, page_requests], axis=1)
     served = lax.all_to_all(all_requests, OWNER, split_axis=0, concat_axis=0, tiled=True)
-    returned = lax.all_to_all(
-        table[served.reshape(-1)].reshape(owners, slots, width),
+    nbr_rows = lax.all_to_all(
+        table[served[:, :capacity].reshape(-1)].reshape(owners, capacity, width),
         OWNER, split_axis=0, concat_axis=0, tiled=True,
-    )
-    nbr_rows = returned[:, :capacity].reshape(owners * capacity, width)
-    page_rows = returned[:, capacity:].reshape(owners * page_cap, width)
+    ).reshape(owners * capacity, width)
+    page_rows = lax.all_to_all(
+        table[served[:, capacity:].reshape(-1)].reshape(owners, page_cap, width),
+        OWNER, split_axis=0, concat_axis=0, tiled=True,
+    ).reshape(owners * page_cap, width)
     nbr_flat = (owner_of * capacity + slot_of).reshape(queries, fan_count)
     nbr_slots = jnp.arange(owners * capacity, dtype=jnp.int32)
     pool_weights = jnp.sum(

time: 352 us -> 351 us (level)
  waiting for transfers between devices: 221 us -> 208 us
  matrix products: 12.4 us -> 19.1 us
  starting transfers between devices: 18.6 us -> 25.1 us
    all_to_all x1 -> x2, waiting for transfers between devices: 163 us -> 149 us  [the longest x1 114 us: local(): lax.all_to_all(table[served[:, capacity:].reshape(-1)].reshape(owners, pa...]
    gather x1 -> x2, local copies, waits for them, and re-layouts: 20.8 us -> 27.1 us  [the longest x1 16.6 us: local(): table[served[:, capacity:].reshape(-1)].reshape(owners, page_cap, width)]
    slice x2 -> x1, local copies, waits for them, and re-layouts: 5.87 us -> 0.07 us  [local(): served[:, capacity:].reshape(-1)]
    all_to_all x1 -> x2, starting transfers between devices: 6.02 us -> 11.6 us  [the longest x1 6.01 us: local(): lax.all_to_all(table[served[:, capacity:].reshape(-1)].reshape(owners, pa...]
    unnamed x27 -> x25, local copies, waits for them, and re-layouts: 7.9 us -> 8.15 us
  transfers between devices with their start and end apart: 11 -> 12, of which waited for: 7 -> 8; matrix products, arithmetic and copies ran while one was open for 2% -> 8% of each run, Pallas kernels for 0% -> 0%
where the time goes in v9:
time: 351 us; the launch traced here: 350 us
  waiting for transfers between devices  208 us (59%)
  local copies, waits for them, and re-layouts  53.6 us (15%)
  blocking collectives  36.4 us (10%)
  starting transfers between devices  25.1 us (7%)
  matrix products  19.1 us (5%)
  other arithmetic  6.15 us (2%)
    all_to_all x1, waiting for transfers between devices, local(): lax.all_to_all(table[served[:, capacity:].reshape(-1)].reshape(owners, pa...  114 us
    all_to_all x1, waiting for transfers between devices, local(): lax.all_to_all(table[served[:, :capacity].reshape(-1)].reshape(owners, ca...  34.4 us
    ppermute x4, waiting for transfers between devices, ring_gather(): lax.ppermute(forward_part, axis, [(i, (i + 1) % size) for i in range(size)])  25.1 us
    all_to_all x1, blocking collectives, local(): lax.all_to_all(all_requests, OWNER, split_axis=0, concat_axis=0, tiled=True)  21.5 us
    gather x1, local copies, waits for them, and re-layouts, local(): table[served[:, capacity:].reshape(-1)].reshape(owners, page_cap, width)  16.6 us
    ppermute x2, waiting for transfers between devices, pair_sum(): lax.ppermute(values, 'neg', [(i, i ^ step) for i in range(groups)])  14.6 us
    all_gather x1, blocking collectives, weight_grads(): gathered = lax.all_gather(gathered, OWNER[1], axis=0)  12.9 us
    gather x1, local copies, waits for them, and re-layouts, local(): table[served[:, :capacity].reshape(-1)].reshape(owners, capacity, width)  10.5 us
  transfers between devices with their start and end apart: 12, of which 8 were waited for; matrix products, arithmetic and copies ran while one was open for 8% of the time, Pallas kernels for 0%

profile of v9, /device:TPU:6, one launch (start us, length us, event | category | flops | bytes accessed | tf_op | source)
XLA Modules:
  0.0 350.0 jit_solution(10349498051360644111)
XLA Ops:
  0.6 0.9 reshape.985
  4.7 2.0 fusion.3
  7.8 21.5 %all_to_all.27 = s32[64,1,56]{2,1,0:T(1,128)S(1)} all-to-all(s32[64,1,56]{2,1,0:T(1,128)S(1)} %bitcast.104), channel_id=1, replica_groups=mesh['oz'=8,'oy'=4,'oc'=2,'neg'=4] {'oz','oy','oc'}, dimensions={0} | all-to-all | bytes 28672 | tf_op jit(solution)/shard_map/all_to_all | solution.py:152
  29.4 10.5 %gather_fusion.1 = bf16[1024,1024]{1,0:T(8,128)(2,1)} fusion(bf16[4096,1024]{1,0:T(8,128)(2,1)} %param.17, s32[1024]{0:T(1024)S(1)} %broadcast_clamp_fusion), kind=kCustom, calls=%fused_computation.1 | custom fusion | bytes 4198400 | tf_op jit(solution)/shard_map/gather | solution.py:154
  39.9 5.6 %all-to-all-start.2 = ((bf16[64,16,1024]{2,1,0:T(8,128)(2,1)}), bf16[64,16,1024]{2,1,0:T(8,128)(2,1)}, u32[]{:S(2)}, u32[]{:S(2)}) async-start(bf16[64,16,1024]{2,1,0:T(8,128)(2,1)} %bitcast.91), calls=%async_computation.2 | async-start | bytes 4194304 | tf_op jit(solution)/shard_map/all_to_all | solution.py:153
  45.7 16.6 %gather_fusion = bf16[2560,1024]{1,0:T(8,128)(2,1)} fusion(bf16[4096,1024]{1,0:T(8,128)(2,1)} %param.17, s32[3072]{0:T(1024)S(1)} %pad_clamp_fusion), kind=kCustom, calls=%fused_computation | custom fusion | bytes 10496000 | tf_op jit(solution)/shard_map/gather | solution.py:158
  62.3 34.4 %all-to-all-done.2 = bf16[64,16,1024]{2,1,0:T(8,128)(2,1)} async-done(((bf16[64,16,1024]{2,1,0:T(8,128)(2,1)}), bf16[64,16,1024]{2,1,0:T(8,128)(2,1)}, u32[]{:S(2)}, u32[]{:S(2)}) %all-to-all-start.2) | async-done | bytes 2097184 | tf_op jit(solution)/shard_map/all_to_all | solution.py:153
  96.7 6.0 %all-to-all-start.1 = ((bf16[64,40,1024]{2,1,0:T(8,128)(2,1)}), bf16[64,40,1024]{2,1,0:T(8,128)(2,1)}, u32[]{:S(2)}, u32[]{:S(2)}) async-start(bf16[64,40,1024]{2,1,0:T(8,128)(2,1)} %bitcast.90), calls=%async_computation.1 | async-start | bytes 10485760 | tf_op jit(solution)/shard_map/all_to_all | solution.py:157
  103.7 2.5 convolution_convert_fusion.1
  106.8 114.5 %all-to-all-done.1 = bf16[64,40,1024]{2,1,0:T(8,128)(2,1)} async-done(((bf16[64,40,1024]{2,1,0:T(8,128)(2,1)}), bf16[64,40,1024]{2,1,0:T(8,128)(2,1)}, u32[]{:S(2)}, u32[]{:S(2)}) %all-to-all-start.1) | async-done | bytes 5242912 | tf_op jit(solution)/shard_map/all_to_all | solution.py:157
  221.3 3.5 convolution_convert_fusion
  226.0 4.0 %fusion.37 = f32[8,2560]{1,0:T(8,128)S(1)} fusion(bf16[2560,1024]{1,0:T(8,128)(2,1)} %bitcast.10, f32[8,1024]{1,0:T(8,128)S(1)} %get-tuple-element.25), kind=kOutput, calls=%fused_computation.108 | convolution fusion | flops 41951232 | bytes 5357568 | tf_op jit(solution)/shard_map/dot_general | solution.py:183
  230.0 6.7 %gather_fusion.2 = f32[1024]{0:T(1024)S(1)} fusion(f32[8,2560]{1,0:T(8,128)S(1)} %fusion.37, s32[1024]{0:T(1024)S(1)} %fusion.51), kind=kCustom, calls=%fused_computation.2 | custom fusion | bytes 16384 | tf_op jit(solution)/shard_map/jit(take_along_axis)/gather | solution.py:186
  237.5 2.0 select_reduce_fusion
  239.4 3.4 multiply_reduce_fusion
  244.3 1.9 all-gather.2
  246.2 12.9 %all-gather.1 = bf16[8,12,2048]{2,1,0:T(8,128)(2,1)S(1)} all-gather(bf16[2,12,2048]{2,1,0:T(8,128)(2,1)S(1)} %all-gather.2), channel_id=3, replica_groups=mesh['oz'=8,'oy'=4,'oc'=2,'neg'=4] {'oy'}, dimensions={0}, use_global_device_ids=true | all-gather | bytes 491520 | tf_op jit(solution)/shard_map/all_gather | solution.py:68
  259.2 2.0 collective-permute-start.3
  262.4 6.1 %all-to-all-start.3 = ((bf16[64,2,192]{2,1,0:T(2,128)(2,1)}), bf16[64,2,192]{2,1,0:T(2,128)(2,1)S(1)}, u32[]{:S(2)}, u32[]{:S(2)}) async-start(bf16[64,2,192]{2,1,0:T(2,128)(2,1)} %reshape.1041), calls=%async_computation.3 | async-start | bytes 131072 | tf_op jit(solution)/shard_map/all_to_all | solution.py:62
  269.3 9.1 %all-to-all-done.3 = bf16[64,2,192]{2,1,0:T(2,128)(2,1)S(1)} async-done(((bf16[64,2,192]{2,1,0:T(2,128)(2,1)}), bf16[64,2,192]{2,1,0:T(2,128)(2,1)S(1)}, u32[]{:S(2)}, u32[]{:S(2)}) %all-to-all-start.3) | async-done | bytes 49184 | tf_op jit(solution)/shard_map/all_to_all | solution.py:62
  279.5 1.6 collective-permute-start.4
  281.0 1.9 bitcast_dynamic-update-slice_fusion.6
  282.9 10.2 %collective-permute-done.1 = bf16[4,2,12,2048]{3,2,1,0:T(8,128)(2,1)S(1)} collective-permute-done((bf16[4,2,12,2048]{3,2,1,0:T(8,128)(2,1)}, bf16[4,2,12,2048]{3,2,1,0:T(8,128)(2,1)S(1)}, u32[]{:S(2)}, u32[]{:S(2)}) %collective-permute-start.1) | collective-permute-done | bytes 393248 | tf_op jit(solution)/shard_map/ppermute | solution.py:99
  293.2 1.7 collective-permute-start.2
  296.0 12.8 %collective-permute-done.5 = bf16[4,2,12,2048]{3,2,1,0:T(8,128)(2,1)S(1)} collective-permute-done((bf16[4,2,12,2048]{3,2,1,0:T(8,128)(2,1)S(1)}, bf16[4,2,12,2048]{3,2,1,0:T(8,128)(2,1)S(1)}, u32[]{:S(2)}, u32[]{:S(2)}) %collective-permute-start.5) | collective-permute-done | bytes 393248 | tf_op jit(solution)/shard_map/ppermute | solution.py:96
  309.7 12.3 %collective-permute-done.6 = bf16[4,2,12,2048]{3,2,1,0:T(8,128)(2,1)S(1)} collective-permute-done((bf16[4,2,12,2048]{3,2,1,0:T(8,128)(2,1)S(1)}, bf16[4,2,12,2048]{3,2,1,0:T(8,128)(2,1)S(1)}, u32[]{:S(2)}, u32[]{:S(2)}) %collective-permute-start.6) | collective-permute-done | bytes 393248 | tf_op jit(solution)/shard_map/ppermute | solution.py:96
  325.4 1.7 slice.133
  327.8 2.1 slice.137
  329.9 1.2 fusion.15
  331.9 0.9 collective-permute-start.7
  332.8 7.0 %collective-permute-done.7 = f32[52,1024]{1,0:T(8,128)S(1)} collective-permute-done((f32[52,1024]{1,0:T(8,128)S(1)}, f32[52,1024]{1,0:T(8,128)S(1)}, u32[]{:S(2)}, u32[]{:S(2)}) %collective-permute-start.7) | collective-permute-done | bytes 213024 | tf_op jit(solution)/shard_map/ppermute | solution.py:107
  340.0 7.5 %collective-permute-done.8 = f32[52,1024]{1,0:T(8,128)S(1)} collective-permute-done((f32[52,1024]{1,0:T(8,128)S(1)}, f32[52,1024]{1,0:T(8,128)S(1)}, u32[]{:S(2)}, u32[]{:S(2)}) %collective-permute-start.8) | collective-permute-done | bytes 213024 | tf_op jit(solution)/shard_map/ppermute | solution.py:107
  (102 shorter events, 21.1 us)
Async XLA Ops:
  0.6 105.7 %copy-start = (bf16[1024,1024]{1,0:T(8,128)(2,1)S(1)}, bf16[1024,1024]{1,0:T(8,128)(2,1)}, u32[]{:S(2)}) copy-start(bf16[1024,1024]{1,0:T(8,128)(2,1)} %param.18) | copy-start | bytes 6291460
  39.9 56.7 %all-to-all-start.2 = ((bf16[64,16,1024]{2,1,0:T(8,128)(2,1)}), bf16[64,16,1024]{2,1,0:T(8,128)(2,1)}, u32[]{:S(2)}, u32[]{:S(2)}) async-start(bf16[64,16,1024]{2,1,0:T(8,128)(2,1)} %bitcast.91), calls=%async_computation.2 | async-start | bytes 4194304 | tf_op jit(solution)/shard_map/all_to_all | solution.py:153
  96.7 6.1 %copy-start.4 = (s32[8,50]{1,0:T(8,128)S(1)}, s32[8,50]{1,0:T(8,128)}, u32[]{:S(2)}) copy-start(s32[8,50]{1,0:T(8,128)} %param.12) | copy-start | bytes 4804
  96.7 6.3 %copy-start.5 = (s32[8,50]{1,0:T(8,128)S(1)}, s32[8,50]{1,0:T(8,128)}, u32[]{:S(2)}) copy-start(s32[8,50]{1,0:T(8,128)} %param.13) | copy-start | bytes 4804
  96.7 9.7 %copy-start.6 = (f32[1024]{0:T(1024)S(1)}, f32[1024]{0:T(1024)}, u32[]{:S(2)}) copy-start(f32[1024]{0:T(1024)} %param.19) | copy-start | bytes 12292
  96.7 124.6 %all-to-all-start.1 = ((bf16[64,40,1024]{2,1,0:T(8,128)(2,1)}), bf16[64,40,1024]{2,1,0:T(8,128)(2,1)}, u32[]{:S(2)}, u32[]{:S(2)}) async-start(bf16[64,40,1024]{2,1,0:T(8,128)(2,1)} %bitcast.90), calls=%async_computation.1 | async-start | bytes 10485760 | tf_op jit(solution)/shard_map/all_to_all | solution.py:157
  106.4 118.4 %copy-start.7 = (f32[1024]{0:T(1024)S(1)}, f32[1024]{0:T(1024)}, u32[]{:S(2)}) copy-start(f32[1024]{0:T(1024)} %param.21) | copy-start | bytes 12292
  221.3 3.7 %copy-start.1 = (bf16[2048,1024]{1,0:T(8,128)(2,1)S(1)}, bf16[2048,1024]{1,0:T(8,128)(2,1)}, u32[]{:S(2)}) copy-start(bf16[2048,1024]{1,0:T(8,128)(2,1)} %param.20) | copy-start | bytes 12582916
  226.0 16.8 %copy-start.3 = (f32[8,1024]{1,0:T(8,128)}, f32[8,1024]{1,0:T(8,128)S(1)}, u32[]{:S(2)}) copy-start(f32[8,1024]{1,0:T(8,128)S(1)} %get-tuple-element.25) | copy-start | bytes 98308
  236.7 6.2 %copy-start.2 = (bf16[2048,1024]{1,0:T(8,128)(2,1)S(1)}, bf16[2048,1024]{1,0:T(8,128)(2,1)}, u32[]{:S(2)}) copy-start(bf16[2048,1024]{1,0:T(8,128)(2,1)} %param.20) | copy-start | bytes 12582916
  259.2 19.5 %collective-permute-start = (bf16[4,2,12,2048]{3,2,1,0:T(8,128)(2,1)S(1)}, bf16[4,2,12,2048]{3,2,1,0:T(8,128)(2,1)}, u32[]{:S(2)}, u32[]{:S(2)}) collective-permute-start(bf16[4,2,12,2048]{3,2,1,0:T(8,128)(2,1)S(1)} %bitcast.94), channel_id=1, source_target_pairs={{0,224},{32,0},{64,32},{96,64},{128,96},{160,128},{192,160},{224,1... | collective-permute-start | bytes 1179656 | tf_op jit(solution)/shard_map/ppermute | solution.py:99
  259.2 20.3 %collective-permute-start.3 = (bf16[4,2,12,2048]{3,2,1,0:T(8,128)(2,1)S(1)}, bf16[4,2,12,2048]{3,2,1,0:T(8,128)(2,1)S(1)}, u32[]{:S(2)}, u32[]{:S(2)}) collective-permute-start(bf16[4,2,12,2048]{3,2,1,0:T(8,128)(2,1)S(1)} %bitcast.95), channel_id=1, source_target_pairs={{0,32},{32,64},{64,96},{96,128},{128,160},{160,192},{192,224},{224... | collective-permute-start | bytes 1179656 | tf_op jit(solution)/shard_map/ppermute | solution.py:96
  262.4 16.1 %all-to-all-start.3 = ((bf16[64,2,192]{2,1,0:T(2,128)(2,1)}), bf16[64,2,192]{2,1,0:T(2,128)(2,1)S(1)}, u32[]{:S(2)}, u32[]{:S(2)}) async-start(bf16[64,2,192]{2,1,0:T(2,128)(2,1)} %reshape.1041), calls=%async_computation.3 | async-start | bytes 131072 | tf_op jit(solution)/shard_map/all_to_all | solution.py:62
  278.7 14.5 %collective-permute-start.1 = (bf16[4,2,12,2048]{3,2,1,0:T(8,128)(2,1)}, bf16[4,2,12,2048]{3,2,1,0:T(8,128)(2,1)S(1)}, u32[]{:S(2)}, u32[]{:S(2)}) collective-permute-start(bf16[4,2,12,2048]{3,2,1,0:T(8,128)(2,1)} %collective-permute-done), channel_id=1, source_target_pairs={{0,224},{32,0},{64,32},{96,64},{128,96},{160,128},{192,160},{224,1... | collective-permute-start | bytes 1179656 | tf_op jit(solution)/shard_map/ppermute | solution.py:99
  279.5 15.4 %collective-permute-start.4 = (bf16[4,2,12,2048]{3,2,1,0:T(8,128)(2,1)S(1)}, bf16[4,2,12,2048]{3,2,1,0:T(8,128)(2,1)S(1)}, u32[]{:S(2)}, u32[]{:S(2)}) collective-permute-start(bf16[4,2,12,2048]{3,2,1,0:T(8,128)(2,1)S(1)} %collective-permute-done.3), channel_id=1, source_target_pairs={{0,32},{32,64},{64,96},{96,128},{128,160},{160,192},{192,224},{224... | collective-permute-start | bytes 1179656 | tf_op jit(solution)/shard_map/ppermute | solution.py:96
  293.2 15.7 %collective-permute-start.2 = (bf16[4,2,12,2048]{3,2,1,0:T(8,128)(2,1)S(1)}, bf16[4,2,12,2048]{3,2,1,0:T(8,128)(2,1)S(1)}, u32[]{:S(2)}, u32[]{:S(2)}) collective-permute-start(bf16[4,2,12,2048]{3,2,1,0:T(8,128)(2,1)S(1)} %collective-permute-done.1), channel_id=1, source_target_pairs={{0,224},{32,0},{64,32},{96,64},{128,96},{160,128},{192,160},{224,1... | collective-permute-start | bytes 1179656 | tf_op jit(solution)/shard_map/ppermute | solution.py:99
  294.8 14.0 %collective-permute-start.5 = (bf16[4,2,12,2048]{3,2,1,0:T(8,128)(2,1)S(1)}, bf16[4,2,12,2048]{3,2,1,0:T(8,128)(2,1)S(1)}, u32[]{:S(2)}, u32[]{:S(2)}) collective-permute-start(bf16[4,2,12,2048]{3,2,1,0:T(8,128)(2,1)S(1)} %collective-permute-done.4), channel_id=1, source_target_pairs={{0,32},{32,64},{64,96},{96,128},{128,160},{160,192},{192,224},{224... | collective-permute-start | bytes 1179656 | tf_op jit(solution)/shard_map/ppermute | solution.py:96
  308.9 13.2 %collective-permute-start.6 = (bf16[4,2,12,2048]{3,2,1,0:T(8,128)(2,1)S(1)}, bf16[4,2,12,2048]{3,2,1,0:T(8,128)(2,1)S(1)}, u32[]{:S(2)}, u32[]{:S(2)}) collective-permute-start(bf16[4,2,12,2048]{3,2,1,0:T(8,128)(2,1)S(1)} %collective-permute-done.5), channel_id=1, source_target_pairs={{0,32},{32,64},{64,96},{96,128},{128,160},{160,192},{192,224},{224... | collective-permute-start | bytes 1179656 | tf_op jit(solution)/shard_map/ppermute | solution.py:96
  331.9 8.0 %collective-permute-start.7 = (f32[52,1024]{1,0:T(8,128)S(1)}, f32[52,1024]{1,0:T(8,128)S(1)}, u32[]{:S(2)}, u32[]{:S(2)}) collective-permute-start(f32[52,1024]{1,0:T(8,128)S(1)} %pad_maximum_fusion), channel_id=1, source_target_pairs={{0,1},{1,0},{2,3},{3,2},{4,5},{5,4},{6,7},{7,6},{8,9},{9,8},{10,11... | collective-permute-start | bytes 638984 | tf_op jit(solution)/shard_map/ppermute | solution.py:107
  339.9 7.6 %collective-permute-start.8 = (f32[52,1024]{1,0:T(8,128)S(1)}, f32[52,1024]{1,0:T(8,128)S(1)}, u32[]{:S(2)}, u32[]{:S(2)}) collective-permute-start(f32[52,1024]{1,0:T(8,128)S(1)} %fusion.68), channel_id=1, source_target_pairs={{0,2},{1,3},{2,0},{3,1},{4,6},{5,7},{6,4},{7,5},{8,10},{9,11},{10,... | collective-permute-start | bytes 638984 | tf_op jit(solution)/shard_map/ppermute | solution.py:107

commit v10 on v9

--- a/solution.py
+++ b/solution.py
@@ -183,12 +183,13 @@
     slot_scores = lax.dot_general(
         embed_b, page_rows, (((1,), (1,)), ((), ())), preferred_element_type=jnp.float32
     )
-    neg_scores = jnp.take_along_axis(slot_scores, neg_flat, axis=1)
+    neg_match = neg_flat[:, :, None] == page_slots[None, None, :]
+    neg_scores = jnp.sum(jnp.where(neg_match, slot_scores[:, None, :], 0.0), axis=2)
     pos_scores = jnp.einsum("qe,qe->q", embed_b, pos_rows, preferred_element_type=jnp.float32)
     loss_part, slope_b, slope_total = margin_terms(neg_scores, pos_scores, loss_scale)
     slope_slots = jnp.sum(
         jnp.where(
-            neg_flat[:, :, None] == page_slots[None, None, :],
+            neg_match,
             slope_b.astype(jnp.float32)[:, :, None],
             0.0,
         ),

time: 351 us -> 345 us (0.983)
  local copies, waits for them, and re-layouts: 53.6 us -> 46.9 us
    gather x1 -> x0, local copies, waits for them, and re-layouts: 6.73 us -> none  [local(): neg_scores = jnp.take_along_axis(slot_scores, neg_flat, axis=1)]
    unnamed x25 -> x23, local copies, waits for them, and re-layouts: 8.15 us -> 8.14 us
where the time goes in v10:
time: 345 us; the launch traced here: 344 us
  waiting for transfers between devices  208 us (60%)
  local copies, waits for them, and re-layouts  46.9 us (14%)
  blocking collectives  36.4 us (11%)
  starting transfers between devices  24.9 us (7%)
  matrix products  19.1 us (6%)
  other arithmetic  7.51 us (2%)
    all_to_all x1, waiting for transfers between devices, local(): lax.all_to_all(table[served[:, capacity:].reshape(-1)].reshape(owners, pa...  115 us
    all_to_all x1, waiting for transfers between devices, local(): lax.all_to_all(table[served[:, :capacity].reshape(-1)].reshape(owners, ca...  34.4 us
    ppermute x4, waiting for transfers between devices, ring_gather(): lax.ppermute(forward_part, axis, [(i, (i + 1) % size) for i in range(size)])  25.1 us
    all_to_all x1, blocking collectives, local(): lax.all_to_all(all_requests, OWNER, split_axis=0, concat_axis=0, tiled=True)  21.5 us
    gather x1, local copies, waits for them, and re-layouts, local(): table[served[:, capacity:].reshape(-1)].reshape(owners, page_cap, width)  16.6 us
    ppermute x2, waiting for transfers between devices, pair_sum(): lax.ppermute(values, 'neg', [(i, i ^ step) for i in range(groups)])  14.6 us
    all_gather x1, blocking collectives, weight_grads(): gathered = lax.all_gather(gathered, OWNER[1], axis=0)  12.9 us
    gather x1, local copies, waits for them, and re-layouts, local(): table[served[:, :capacity].reshape(-1)].reshape(owners, capacity, width)  10.5 us
  transfers between devices with their start and end apart: 12, of which 8 were waited for; matrix products, arithmetic and copies ran while one was open for 8% of the time, Pallas kernels for 0%

profile of v10, /device:TPU:6, one launch (start us, length us, event | category | flops | bytes accessed | tf_op | source)
XLA Modules:
  0.0 344.5 jit_solution(1972323021082677501)
XLA Ops:
  0.6 0.9 reshape.930
  4.7 2.0 fusion.3
  7.8 21.5 %all_to_all.27 = s32[64,1,56]{2,1,0:T(1,128)S(1)} all-to-all(s32[64,1,56]{2,1,0:T(1,128)S(1)} %bitcast.82), channel_id=1, replica_groups=mesh['oz'=8,'oy'=4,'oc'=2,'neg'=4] {'oz','oy','oc'}, dimensions={0} | all-to-all | bytes 28672 | tf_op jit(solution)/shard_map/all_to_all | solution.py:152
  29.4 10.5 %gather_fusion.1 = bf16[1024,1024]{1,0:T(8,128)(2,1)} fusion(bf16[4096,1024]{1,0:T(8,128)(2,1)} %param.17, s32[1024]{0:T(1024)S(1)} %broadcast_clamp_fusion), kind=kCustom, calls=%fused_computation.1 | custom fusion | bytes 4198400 | tf_op jit(solution)/shard_map/gather | solution.py:154
  39.9 5.6 %all-to-all-start.2 = ((bf16[64,16,1024]{2,1,0:T(8,128)(2,1)}), bf16[64,16,1024]{2,1,0:T(8,128)(2,1)}, u32[]{:S(2)}, u32[]{:S(2)}) async-start(bf16[64,16,1024]{2,1,0:T(8,128)(2,1)} %bitcast.69), calls=%async_computation.2 | async-start | bytes 4194304 | tf_op jit(solution)/shard_map/all_to_all | solution.py:153
  45.7 16.6 %gather_fusion = bf16[2560,1024]{1,0:T(8,128)(2,1)} fusion(bf16[4096,1024]{1,0:T(8,128)(2,1)} %param.17, s32[3072]{0:T(1024)S(1)} %pad_clamp_fusion), kind=kCustom, calls=%fused_computation | custom fusion | bytes 10496000 | tf_op jit(solution)/shard_map/gather | solution.py:158
  62.3 34.4 %all-to-all-done.2 = bf16[64,16,1024]{2,1,0:T(8,128)(2,1)} async-done(((bf16[64,16,1024]{2,1,0:T(8,128)(2,1)}), bf16[64,16,1024]{2,1,0:T(8,128)(2,1)}, u32[]{:S(2)}, u32[]{:S(2)}) %all-to-all-start.2) | async-done | bytes 2097184 | tf_op jit(solution)/shard_map/all_to_all | solution.py:153
  96.7 6.0 %all-to-all-start.1 = ((bf16[64,40,1024]{2,1,0:T(8,128)(2,1)}), bf16[64,40,1024]{2,1,0:T(8,128)(2,1)}, u32[]{:S(2)}, u32[]{:S(2)}) async-start(bf16[64,40,1024]{2,1,0:T(8,128)(2,1)} %bitcast.68), calls=%async_computation.1 | async-start | bytes 10485760 | tf_op jit(solution)/shard_map/all_to_all | solution.py:157
  103.6 2.5 convolution_convert_fusion.1
  106.7 114.5 %all-to-all-done.1 = bf16[64,40,1024]{2,1,0:T(8,128)(2,1)} async-done(((bf16[64,40,1024]{2,1,0:T(8,128)(2,1)}), bf16[64,40,1024]{2,1,0:T(8,128)(2,1)}, u32[]{:S(2)}, u32[]{:S(2)}) %all-to-all-start.1) | async-done | bytes 5242912 | tf_op jit(solution)/shard_map/all_to_all | solution.py:157
  221.3 3.5 %convolution_convert_fusion = bf16[2,8,1024]{2,1,0:T(8,128)(2,1)S(1)} fusion(bf16[2560,1024,1]{1,0,2:T(8,128)(2,1)} %bitcast.11, s32[2,8]{1,0:T(2,128)S(1)} %pad_add_fusion.1), kind=kOutput, calls=%fused_computation.23 | convolution fusion | flops 83943424 | bytes 5275712 | tf_op jit(solution)/shard_map/aqs,se->aqe/dot_general | solution.py:176
  226.0 4.0 %fusion.37 = f32[8,2560]{1,0:T(8,128)S(1)} fusion(bf16[2560,1024]{1,0:T(8,128)(2,1)} %bitcast.10, f32[8,1024]{1,0:T(8,128)S(1)} %get-tuple-element.25), kind=kOutput, calls=%fused_computation.106 | convolution fusion | flops 41951232 | bytes 5357568 | tf_op jit(solution)/shard_map/dot_general | solution.py:183
  230.0 1.5 select_reduce_fusion.1
  232.2 2.0 select_reduce_fusion
  234.1 3.4 multiply_reduce_fusion
  239.0 1.9 all-gather.2
  240.9 12.9 %all-gather.1 = bf16[8,12,2048]{2,1,0:T(8,128)(2,1)S(1)} all-gather(bf16[2,12,2048]{2,1,0:T(8,128)(2,1)S(1)} %all-gather.2), channel_id=3, replica_groups=mesh['oz'=8,'oy'=4,'oc'=2,'neg'=4] {'oy'}, dimensions={0}, use_global_device_ids=true | all-gather | bytes 491520 | tf_op jit(solution)/shard_map/all_gather | solution.py:68
  253.9 2.0 collective-permute-start.3
  257.1 6.1 %all-to-all-start.3 = ((bf16[64,2,192]{2,1,0:T(2,128)(2,1)}), bf16[64,2,192]{2,1,0:T(2,128)(2,1)S(1)}, u32[]{:S(2)}, u32[]{:S(2)}) async-start(bf16[64,2,192]{2,1,0:T(2,128)(2,1)} %reshape.979), calls=%async_computation.3 | async-start | bytes 131072 | tf_op jit(solution)/shard_map/all_to_all | solution.py:62
  264.0 9.1 %all-to-all-done.3 = bf16[64,2,192]{2,1,0:T(2,128)(2,1)S(1)} async-done(((bf16[64,2,192]{2,1,0:T(2,128)(2,1)}), bf16[64,2,192]{2,1,0:T(2,128)(2,1)S(1)}, u32[]{:S(2)}, u32[]{:S(2)}) %all-to-all-start.3) | async-done | bytes 49184 | tf_op jit(solution)/shard_map/all_to_all | solution.py:62
  273.9 1.6 collective-permute-start.4
  275.5 1.9 bitcast_dynamic-update-slice_fusion.6
  277.4 10.2 %collective-permute-done.1 = bf16[4,2,12,2048]{3,2,1,0:T(8,128)(2,1)S(1)} collective-permute-done((bf16[4,2,12,2048]{3,2,1,0:T(8,128)(2,1)}, bf16[4,2,12,2048]{3,2,1,0:T(8,128)(2,1)S(1)}, u32[]{:S(2)}, u32[]{:S(2)}) %collective-permute-start.1) | collective-permute-done | bytes 393248 | tf_op jit(solution)/shard_map/ppermute | solution.py:99
  287.6 1.7 collective-permute-start.2
  290.5 12.8 %collective-permute-done.5 = bf16[4,2,12,2048]{3,2,1,0:T(8,128)(2,1)S(1)} collective-permute-done((bf16[4,2,12,2048]{3,2,1,0:T(8,128)(2,1)S(1)}, bf16[4,2,12,2048]{3,2,1,0:T(8,128)(2,1)S(1)}, u32[]{:S(2)}, u32[]{:S(2)}) %collective-permute-start.5) | collective-permute-done | bytes 393248 | tf_op jit(solution)/shard_map/ppermute | solution.py:96
  304.2 12.3 %collective-permute-done.6 = bf16[4,2,12,2048]{3,2,1,0:T(8,128)(2,1)S(1)} collective-permute-done((bf16[4,2,12,2048]{3,2,1,0:T(8,128)(2,1)S(1)}, bf16[4,2,12,2048]{3,2,1,0:T(8,128)(2,1)S(1)}, u32[]{:S(2)}, u32[]{:S(2)}) %collective-permute-start.6) | collective-permute-done | bytes 393248 | tf_op jit(solution)/shard_map/ppermute | solution.py:96
  319.8 1.7 slice.131
  322.2 2.1 slice.135
  324.4 1.2 fusion.15
  326.4 0.9 collective-permute-start.7
  327.3 7.0 %collective-permute-done.7 = f32[52,1024]{1,0:T(8,128)S(1)} collective-permute-done((f32[52,1024]{1,0:T(8,128)S(1)}, f32[52,1024]{1,0:T(8,128)S(1)}, u32[]{:S(2)}, u32[]{:S(2)}) %collective-permute-start.7) | collective-permute-done | bytes 213024 | tf_op jit(solution)/shard_map/ppermute | solution.py:107
  334.5 7.5 %collective-permute-done.8 = f32[52,1024]{1,0:T(8,128)S(1)} collective-permute-done((f32[52,1024]{1,0:T(8,128)S(1)}, f32[52,1024]{1,0:T(8,128)S(1)}, u32[]{:S(2)}, u32[]{:S(2)}) %collective-permute-start.8) | collective-permute-done | bytes 213024 | tf_op jit(solution)/shard_map/ppermute | solution.py:107
  (99 shorter events, 20.8 us)
Async XLA Ops:
  0.6 105.7 %copy-start = (bf16[1024,1024]{1,0:T(8,128)(2,1)S(1)}, bf16[1024,1024]{1,0:T(8,128)(2,1)}, u32[]{:S(2)}) copy-start(bf16[1024,1024]{1,0:T(8,128)(2,1)} %param.18) | copy-start | bytes 6291460
  39.9 56.7 %all-to-all-start.2 = ((bf16[64,16,1024]{2,1,0:T(8,128)(2,1)}), bf16[64,16,1024]{2,1,0:T(8,128)(2,1)}, u32[]{:S(2)}, u32[]{:S(2)}) async-start(bf16[64,16,1024]{2,1,0:T(8,128)(2,1)} %bitcast.69), calls=%async_computation.2 | async-start | bytes 4194304 | tf_op jit(solution)/shard_map/all_to_all | solution.py:153
  96.7 6.1 %copy-start.3 = (s32[8,50]{1,0:T(8,128)S(1)}, s32[8,50]{1,0:T(8,128)}, u32[]{:S(2)}) copy-start(s32[8,50]{1,0:T(8,128)} %param.12) | copy-start | bytes 4804
  96.7 6.3 %copy-start.4 = (s32[8,50]{1,0:T(8,128)S(1)}, s32[8,50]{1,0:T(8,128)}, u32[]{:S(2)}) copy-start(s32[8,50]{1,0:T(8,128)} %param.13) | copy-start | bytes 4804
  96.7 9.6 %copy-start.5 = (f32[1024]{0:T(1024)S(1)}, f32[1024]{0:T(1024)}, u32[]{:S(2)}) copy-start(f32[1024]{0:T(1024)} %param.19) | copy-start | bytes 12292
  96.7 124.6 %all-to-all-start.1 = ((bf16[64,40,1024]{2,1,0:T(8,128)(2,1)}), bf16[64,40,1024]{2,1,0:T(8,128)(2,1)}, u32[]{:S(2)}, u32[]{:S(2)}) async-start(bf16[64,40,1024]{2,1,0:T(8,128)(2,1)} %bitcast.68), calls=%async_computation.1 | async-start | bytes 10485760 | tf_op jit(solution)/shard_map/all_to_all | solution.py:157
  106.3 118.4 %copy-start.6 = (f32[1024]{0:T(1024)S(1)}, f32[1024]{0:T(1024)}, u32[]{:S(2)}) copy-start(f32[1024]{0:T(1024)} %param.21) | copy-start | bytes 12292
  221.3 3.7 %copy-start.1 = (bf16[2048,1024]{1,0:T(8,128)(2,1)S(1)}, bf16[2048,1024]{1,0:T(8,128)(2,1)}, u32[]{:S(2)}) copy-start(bf16[2048,1024]{1,0:T(8,128)(2,1)} %param.20) | copy-start | bytes 12582916
  226.0 11.5 %copy-start.2 = (f32[8,1024]{1,0:T(8,128)}, f32[8,1024]{1,0:T(8,128)S(1)}, u32[]{:S(2)}) copy-start(f32[8,1024]{1,0:T(8,128)S(1)} %get-tuple-element.25) | copy-start | bytes 98308
  253.9 19.5 %collective-permute-start = (bf16[4,2,12,2048]{3,2,1,0:T(8,128)(2,1)S(1)}, bf16[4,2,12,2048]{3,2,1,0:T(8,128)(2,1)}, u32[]{:S(2)}, u32[]{:S(2)}) collective-permute-start(bf16[4,2,12,2048]{3,2,1,0:T(8,128)(2,1)S(1)} %bitcast.72), channel_id=1, source_target_pairs={{0,224},{32,0},{64,32},{96,64},{128,96},{160,128},{192,160},{224,1... | collective-permute-start | bytes 1179656 | tf_op jit(solution)/shard_map/ppermute | solution.py:99
  253.9 20.1 %collective-permute-start.3 = (bf16[4,2,12,2048]{3,2,1,0:T(8,128)(2,1)S(1)}, bf16[4,2,12,2048]{3,2,1,0:T(8,128)(2,1)S(1)}, u32[]{:S(2)}, u32[]{:S(2)}) collective-permute-start(bf16[4,2,12,2048]{3,2,1,0:T(8,128)(2,1)S(1)} %bitcast.73), channel_id=1, source_target_pairs={{0,32},{32,64},{64,96},{96,128},{128,160},{160,192},{192,224},{224... | collective-permute-start | bytes 1179656 | tf_op jit(solution)/shard_map/ppermute | solution.py:96
  257.1 16.1 %all-to-all-start.3 = ((bf16[64,2,192]{2,1,0:T(2,128)(2,1)}), bf16[64,2,192]{2,1,0:T(2,128)(2,1)S(1)}, u32[]{:S(2)}, u32[]{:S(2)}) async-start(bf16[64,2,192]{2,1,0:T(2,128)(2,1)} %reshape.979), calls=%async_computation.3 | async-start | bytes 131072 | tf_op jit(solution)/shard_map/all_to_all | solution.py:62
  273.4 14.2 %collective-permute-start.1 = (bf16[4,2,12,2048]{3,2,1,0:T(8,128)(2,1)}, bf16[4,2,12,2048]{3,2,1,0:T(8,128)(2,1)S(1)}, u32[]{:S(2)}, u32[]{:S(2)}) collective-permute-start(bf16[4,2,12,2048]{3,2,1,0:T(8,128)(2,1)} %collective-permute-done), channel_id=1, source_target_pairs={{0,224},{32,0},{64,32},{96,64},{128,96},{160,128},{192,160},{224,1... | collective-permute-start | bytes 1179656 | tf_op jit(solution)/shard_map/ppermute | solution.py:99
  273.9 15.4 %collective-permute-start.4 = (bf16[4,2,12,2048]{3,2,1,0:T(8,128)(2,1)S(1)}, bf16[4,2,12,2048]{3,2,1,0:T(8,128)(2,1)S(1)}, u32[]{:S(2)}, u32[]{:S(2)}) collective-permute-start(bf16[4,2,12,2048]{3,2,1,0:T(8,128)(2,1)S(1)} %collective-permute-done.3), channel_id=1, source_target_pairs={{0,32},{32,64},{64,96},{96,128},{128,160},{160,192},{192,224},{224... | collective-permute-start | bytes 1179656 | tf_op jit(solution)/shard_map/ppermute | solution.py:96
  287.6 15.7 %collective-permute-start.2 = (bf16[4,2,12,2048]{3,2,1,0:T(8,128)(2,1)S(1)}, bf16[4,2,12,2048]{3,2,1,0:T(8,128)(2,1)S(1)}, u32[]{:S(2)}, u32[]{:S(2)}) collective-permute-start(bf16[4,2,12,2048]{3,2,1,0:T(8,128)(2,1)S(1)} %collective-permute-done.1), channel_id=1, source_target_pairs={{0,224},{32,0},{64,32},{96,64},{128,96},{160,128},{192,160},{224,1... | collective-permute-start | bytes 1179656 | tf_op jit(solution)/shard_map/ppermute | solution.py:99
  289.3 14.0 %collective-permute-start.5 = (bf16[4,2,12,2048]{3,2,1,0:T(8,128)(2,1)S(1)}, bf16[4,2,12,2048]{3,2,1,0:T(8,128)(2,1)S(1)}, u32[]{:S(2)}, u32[]{:S(2)}) collective-permute-start(bf16[4,2,12,2048]{3,2,1,0:T(8,128)(2,1)S(1)} %collective-permute-done.4), channel_id=1, source_target_pairs={{0,32},{32,64},{64,96},{96,128},{128,160},{160,192},{192,224},{224... | collective-permute-start | bytes 1179656 | tf_op jit(solution)/shard_map/ppermute | solution.py:96
  303.3 13.2 %collective-permute-start.6 = (bf16[4,2,12,2048]{3,2,1,0:T(8,128)(2,1)S(1)}, bf16[4,2,12,2048]{3,2,1,0:T(8,128)(2,1)S(1)}, u32[]{:S(2)}, u32[]{:S(2)}) collective-permute-start(bf16[4,2,12,2048]{3,2,1,0:T(8,128)(2,1)S(1)} %collective-permute-done.5), channel_id=1, source_target_pairs={{0,32},{32,64},{64,96},{96,128},{128,160},{160,192},{192,224},{224... | collective-permute-start | bytes 1179656 | tf_op jit(solution)/shard_map/ppermute | solution.py:96
  326.4 8.0 %collective-permute-start.7 = (f32[52,1024]{1,0:T(8,128)S(1)}, f32[52,1024]{1,0:T(8,128)S(1)}, u32[]{:S(2)}, u32[]{:S(2)}) collective-permute-start(f32[52,1024]{1,0:T(8,128)S(1)} %pad_maximum_fusion), channel_id=1, source_target_pairs={{0,1},{1,0},{2,3},{3,2},{4,5},{5,4},{6,7},{7,6},{8,9},{9,8},{10,11... | collective-permute-start | bytes 638984 | tf_op jit(solution)/shard_map/ppermute | solution.py:107
  334.4 7.6 %collective-permute-start.8 = (f32[52,1024]{1,0:T(8,128)S(1)}, f32[52,1024]{1,0:T(8,128)S(1)}, u32[]{:S(2)}, u32[]{:S(2)}) collective-permute-start(f32[52,1024]{1,0:T(8,128)S(1)} %fusion.62), channel_id=1, source_target_pairs={{0,2},{1,3},{2,0},{3,1},{4,6},{5,7},{6,4},{7,5},{8,10},{9,11},{10,... | collective-permute-start | bytes 638984 | tf_op jit(solution)/shard_map/ppermute | solution.py:107

commit v11 on v10

--- a/solution.py
+++ b/solution.py
@@ -59,9 +59,19 @@
         ],
         axis=2,
     )
+    loss_value = stats[1, 0]
+    loss_hi = loss_value.astype(jnp.bfloat16)
+    loss_lo = (loss_value - loss_hi.astype(jnp.float32)).astype(jnp.bfloat16)
+    loss_chunk = jnp.zeros((owners, 1, left.shape[2]), jnp.bfloat16)
+    loss_chunk = loss_chunk.at[:, 0, 0].set(loss_hi).at[:, 0, 1].set(loss_lo)
+    left = jnp.concatenate([left, loss_chunk], axis=1)
     left = lax.all_to_all(left, OWNER, split_axis=0, concat_axis=0, tiled=True)
-    stats_hi = stats.astype(jnp.bfloat16)
-    stats_lo = (stats - stats_hi.astype(jnp.float32)).astype(jnp.bfloat16)
+    loss_parts = left[:, queries, :2].astype(jnp.float32)
+    loss_owner = jnp.sum(loss_parts[:, 0] + loss_parts[:, 1])
+    left = left[:, :queries]
+    bias_stats = stats[:1]
+    stats_hi = bias_stats.astype(jnp.bfloat16)
+    stats_lo = (bias_stats - stats_hi.astype(jnp.float32)).astype(jnp.bfloat16)
     payload = jnp.concatenate([d_conv_b, d_pool_b], axis=1)
     payload = jnp.concatenate([payload, stats_hi, stats_lo], axis=0)
     gathered = lax.all_gather(payload, OWNER[2], axis=0)
@@ -71,11 +81,13 @@
     left = jnp.roll(left.reshape((ring.shape[0], -1) + left.shape[1:]), -here, axis=0)
     left = left.reshape(owners * queries, conv_rows + pool_rows)
     right = ring[:, :, :, :queries].reshape(owners * queries, payload.shape[1])
-    stat_rows = stats.shape[0]
+    stat_rows = bias_stats.shape[0]
     stat_parts = jnp.roll(ring[:, :, :, queries:], here, axis=0).astype(jnp.float32)
     stats_sum = jnp.sum(
         stat_parts[:, :, :, :stat_rows] + stat_parts[:, :, :, stat_rows:], axis=(0, 1, 2)
     )
+    loss_line = jnp.zeros((1, stats.shape[1]), jnp.float32).at[0, 0].set(loss_owner)
+    stats_sum = jnp.concatenate([stats_sum, loss_line], axis=0)
     contract_rows = (((0,), (0,)), ((), ()))
     conv_width = d_conv_b.shape[1]
     conv_part = lax.dot_general(

time: 345 us -> 348 us (level)
    unnamed x23 -> x24, local copies, waits for them, and re-layouts: 8.14 us -> 8.41 us
where the time goes in v11:
time: 348 us
  waiting for transfers between devices  207 us (59%)
  local copies, waits for them, and re-layouts  48.6 us (14%)
  blocking collectives  36.4 us (10%)
  starting transfers between devices  24.9 us (7%)
  matrix products  19.1 us (5%)
  other arithmetic  8.72 us (3%)
    all_to_all x1, waiting for transfers between devices, local(): lax.all_to_all(table[served[:, capacity:].reshape(-1)].reshape(owners, pa...  113 us
    all_to_all x1, waiting for transfers between devices, local(): lax.all_to_all(table[served[:, :capacity].reshape(-1)].reshape(owners, ca...  34.4 us
    ppermute x4, waiting for transfers between devices, ring_gather(): lax.ppermute(forward_part, axis, [(i, (i + 1) % size) for i in range(size)])  25.1 us
    all_to_all x1, blocking collectives, local(): lax.all_to_all(all_requests, OWNER, split_axis=0, concat_axis=0, tiled=True)  21.5 us
    gather x1, local copies, waits for them, and re-layouts, local(): table[served[:, capacity:].reshape(-1)].reshape(owners, page_cap, width)  16.6 us
    ppermute x2, waiting for transfers between devices, pair_sum(): lax.ppermute(values, 'neg', [(i, i ^ step) for i in range(groups)])  14.6 us
    all_gather x1, blocking collectives, weight_grads(): gathered = lax.all_gather(gathered, OWNER[1], axis=0)  12.9 us
    gather x1, local copies, waits for them, and re-layouts, local(): table[served[:, :capacity].reshape(-1)].reshape(owners, capacity, width)  10.5 us
  transfers between devices with their start and end apart: 12, of which 8 were waited for; matrix products, arithmetic and copies ran while one was open for 8% of the time, Pallas kernels for 0%

profile of v11, /device:TPU:6, one launch (start us, length us, event | category | flops | bytes accessed | tf_op | source)
XLA Modules:
  0.0 347.5 jit_solution(13382494069556231974)
XLA Ops:
  0.6 0.9 reshape.1098
  4.7 2.0 fusion.3
  7.8 21.5 %all_to_all.27 = s32[64,1,56]{2,1,0:T(1,128)S(1)} all-to-all(s32[64,1,56]{2,1,0:T(1,128)S(1)} %bitcast.89), channel_id=1, replica_groups=mesh['oz'=8,'oy'=4,'oc'=2,'neg'=4] {'oz','oy','oc'}, dimensions={0} | all-to-all | bytes 28672 | tf_op jit(solution)/shard_map/all_to_all | solution.py:164
  29.4 10.5 %gather_fusion.1 = bf16[1024,1024]{1,0:T(8,128)(2,1)} fusion(bf16[4096,1024]{1,0:T(8,128)(2,1)} %param.23, s32[1024]{0:T(1024)S(1)} %broadcast_clamp_fusion), kind=kCustom, calls=%fused_computation.1 | custom fusion | bytes 4198400 | tf_op jit(solution)/shard_map/gather | solution.py:166
  39.9 5.6 %all-to-all-start.2 = ((bf16[64,16,1024]{2,1,0:T(8,128)(2,1)}), bf16[64,16,1024]{2,1,0:T(8,128)(2,1)}, u32[]{:S(2)}, u32[]{:S(2)}) async-start(bf16[64,16,1024]{2,1,0:T(8,128)(2,1)} %bitcast.76), calls=%async_computation.2 | async-start | bytes 4194304 | tf_op jit(solution)/shard_map/all_to_all | solution.py:165
  45.7 16.6 %gather_fusion = bf16[2560,1024]{1,0:T(8,128)(2,1)} fusion(bf16[4096,1024]{1,0:T(8,128)(2,1)} %param.23, s32[3072]{0:T(1024)S(1)} %pad_clamp_fusion), kind=kCustom, calls=%fused_computation | custom fusion | bytes 10496000 | tf_op jit(solution)/shard_map/gather | solution.py:170
  62.3 34.4 %all-to-all-done.2 = bf16[64,16,1024]{2,1,0:T(8,128)(2,1)} async-done(((bf16[64,16,1024]{2,1,0:T(8,128)(2,1)}), bf16[64,16,1024]{2,1,0:T(8,128)(2,1)}, u32[]{:S(2)}, u32[]{:S(2)}) %all-to-all-start.2) | async-done | bytes 2097184 | tf_op jit(solution)/shard_map/all_to_all | solution.py:165
  96.7 6.0 %all-to-all-start.1 = ((bf16[64,40,1024]{2,1,0:T(8,128)(2,1)}), bf16[64,40,1024]{2,1,0:T(8,128)(2,1)}, u32[]{:S(2)}, u32[]{:S(2)}) async-start(bf16[64,40,1024]{2,1,0:T(8,128)(2,1)} %bitcast.75), calls=%async_computation.1 | async-start | bytes 10485760 | tf_op jit(solution)/shard_map/all_to_all | solution.py:169
  104.8 2.5 convolution_convert_fusion.1
  108.0 113.3 %all-to-all-done.1 = bf16[64,40,1024]{2,1,0:T(8,128)(2,1)} async-done(((bf16[64,40,1024]{2,1,0:T(8,128)(2,1)}), bf16[64,40,1024]{2,1,0:T(8,128)(2,1)}, u32[]{:S(2)}, u32[]{:S(2)}) %all-to-all-start.1) | async-done | bytes 5242912 | tf_op jit(solution)/shard_map/all_to_all | solution.py:169
  221.3 3.5 convolution_convert_fusion
  226.0 4.0 %fusion.37 = f32[8,2560]{1,0:T(8,128)S(1)} fusion(bf16[2560,1024]{1,0:T(8,128)(2,1)} %bitcast.10, f32[8,1024]{1,0:T(8,128)S(1)} %get-tuple-element.59), kind=kOutput, calls=%fused_computation.106 | convolution fusion | flops 41951232 | bytes 5357568 | tf_op jit(solution)/shard_map/dot_general | solution.py:195
  230.0 1.5 select_reduce_fusion.1
  232.2 2.0 select_reduce_fusion
  234.1 3.4 multiply_reduce_fusion
  238.4 1.9 all-gather.2
  240.3 12.9 %all-gather.1 = bf16[8,10,2048]{2,1,0:T(8,128)(2,1)S(1)} all-gather(bf16[2,10,2048]{2,1,0:T(8,128)(2,1)S(1)} %all-gather.2), channel_id=3, replica_groups=mesh['oz'=8,'oy'=4,'oc'=2,'neg'=4] {'oy'}, dimensions={0}, use_global_device_ids=true | all-gather | bytes 409600 | tf_op jit(solution)/shard_map/all_gather | solution.py:78
  253.2 2.0 collective-permute-start.3
  258.0 6.1 %all-to-all-start.3 = ((bf16[64,2,216]{2,1,0:T(2,128)(2,1)}), bf16[64,2,216]{2,1,0:T(2,128)(2,1)S(1)}, u32[]{:S(2)}, u32[]{:S(2)}) async-start(bf16[64,2,216]{2,1,0:T(2,128)(2,1)} %reshape.1151), calls=%async_computation.3 | async-start | bytes 131072 | tf_op jit(solution)/shard_map/all_to_all | solution.py:68
  264.9 9.2 %all-to-all-done.3 = bf16[64,2,216]{2,1,0:T(2,128)(2,1)S(1)} async-done(((bf16[64,2,216]{2,1,0:T(2,128)(2,1)}), bf16[64,2,216]{2,1,0:T(2,128)(2,1)S(1)}, u32[]{:S(2)}, u32[]{:S(2)}) %all-to-all-start.3) | async-done | bytes 55328 | tf_op jit(solution)/shard_map/all_to_all | solution.py:68
  277.0 1.6 collective-permute-start.4
  278.7 1.9 bitcast_dynamic-update-slice_fusion.6
  280.6 10.2 %collective-permute-done.1 = bf16[4,2,10,2048]{3,2,1,0:T(8,128)(2,1)S(1)} collective-permute-done((bf16[4,2,10,2048]{3,2,1,0:T(8,128)(2,1)}, bf16[4,2,10,2048]{3,2,1,0:T(8,128)(2,1)S(1)}, u32[]{:S(2)}, u32[]{:S(2)}) %collective-permute-start.1) | collective-permute-done | bytes 327712 | tf_op jit(solution)/shard_map/ppermute | solution.py:111
  290.8 1.6 collective-permute-start.2
  293.7 12.7 %collective-permute-done.5 = bf16[4,2,10,2048]{3,2,1,0:T(8,128)(2,1)S(1)} collective-permute-done((bf16[4,2,10,2048]{3,2,1,0:T(8,128)(2,1)S(1)}, bf16[4,2,10,2048]{3,2,1,0:T(8,128)(2,1)S(1)}, u32[]{:S(2)}, u32[]{:S(2)}) %collective-permute-start.5) | collective-permute-done | bytes 327712 | tf_op jit(solution)/shard_map/ppermute | solution.py:108
  307.3 12.3 %collective-permute-done.6 = bf16[4,2,10,2048]{3,2,1,0:T(8,128)(2,1)S(1)} collective-permute-done((bf16[4,2,10,2048]{3,2,1,0:T(8,128)(2,1)S(1)}, bf16[4,2,10,2048]{3,2,1,0:T(8,128)(2,1)S(1)}, u32[]{:S(2)}, u32[]{:S(2)}) %collective-permute-start.6) | collective-permute-done | bytes 327712 | tf_op jit(solution)/shard_map/ppermute | solution.py:108
  323.0 1.7 slice.209
  325.4 2.1 slice.213
  327.5 1.2 fusion.20
  329.4 0.9 collective-permute-start.7
  330.4 7.0 %collective-permute-done.7 = f32[52,1024]{1,0:T(8,128)S(1)} collective-permute-done((f32[52,1024]{1,0:T(8,128)S(1)}, f32[52,1024]{1,0:T(8,128)S(1)}, u32[]{:S(2)}, u32[]{:S(2)}) %collective-permute-start.7) | collective-permute-done | bytes 213024 | tf_op jit(solution)/shard_map/ppermute | solution.py:119
  337.5 7.5 %collective-permute-done.8 = f32[52,1024]{1,0:T(8,128)S(1)} collective-permute-done((f32[52,1024]{1,0:T(8,128)S(1)}, f32[52,1024]{1,0:T(8,128)S(1)}, u32[]{:S(2)}, u32[]{:S(2)}) %collective-permute-start.8) | collective-permute-done | bytes 213024 | tf_op jit(solution)/shard_map/ppermute | solution.py:119
  (112 shorter events, 23.7 us)
Async XLA Ops:
  0.6 106.9 %copy-start = (bf16[1024,1024]{1,0:T(8,128)(2,1)S(1)}, bf16[1024,1024]{1,0:T(8,128)(2,1)}, u32[]{:S(2)}) copy-start(bf16[1024,1024]{1,0:T(8,128)(2,1)} %param.24) | copy-start | bytes 6291460
  39.9 56.7 %all-to-all-start.2 = ((bf16[64,16,1024]{2,1,0:T(8,128)(2,1)}), bf16[64,16,1024]{2,1,0:T(8,128)(2,1)}, u32[]{:S(2)}, u32[]{:S(2)}) async-start(bf16[64,16,1024]{2,1,0:T(8,128)(2,1)} %bitcast.76), calls=%async_computation.2 | async-start | bytes 4194304 | tf_op jit(solution)/shard_map/all_to_all | solution.py:165
  96.7 6.1 %copy-start.3 = (s32[8,50]{1,0:T(8,128)S(1)}, s32[8,50]{1,0:T(8,128)}, u32[]{:S(2)}) copy-start(s32[8,50]{1,0:T(8,128)} %param.18) | copy-start | bytes 4804
  96.7 6.3 %copy-start.4 = (s32[8,50]{1,0:T(8,128)S(1)}, s32[8,50]{1,0:T(8,128)}, u32[]{:S(2)}) copy-start(s32[8,50]{1,0:T(8,128)} %param.19) | copy-start | bytes 4804
  96.7 10.9 %copy-start.5 = (f32[1024]{0:T(1024)S(1)}, f32[1024]{0:T(1024)}, u32[]{:S(2)}) copy-start(f32[1024]{0:T(1024)} %param.25) | copy-start | bytes 12292
  96.7 124.6 %all-to-all-start.1 = ((bf16[64,40,1024]{2,1,0:T(8,128)(2,1)}), bf16[64,40,1024]{2,1,0:T(8,128)(2,1)}, u32[]{:S(2)}, u32[]{:S(2)}) async-start(bf16[64,40,1024]{2,1,0:T(8,128)(2,1)} %bitcast.75), calls=%async_computation.1 | async-start | bytes 10485760 | tf_op jit(solution)/shard_map/all_to_all | solution.py:169
  107.5 117.2 %copy-start.6 = (f32[1024]{0:T(1024)S(1)}, f32[1024]{0:T(1024)}, u32[]{:S(2)}) copy-start(f32[1024]{0:T(1024)} %param.27) | copy-start | bytes 12292
  221.3 3.7 %copy-start.1 = (bf16[2048,1024]{1,0:T(8,128)(2,1)S(1)}, bf16[2048,1024]{1,0:T(8,128)(2,1)}, u32[]{:S(2)}) copy-start(bf16[2048,1024]{1,0:T(8,128)(2,1)} %param.26) | copy-start | bytes 12582916
  226.0 11.5 %copy-start.2 = (f32[8,1024]{1,0:T(8,128)}, f32[8,1024]{1,0:T(8,128)S(1)}, u32[]{:S(2)}) copy-start(f32[8,1024]{1,0:T(8,128)S(1)} %get-tuple-element.59) | copy-start | bytes 98308
  253.2 23.3 %collective-permute-start = (bf16[4,2,10,2048]{3,2,1,0:T(8,128)(2,1)S(1)}, bf16[4,2,10,2048]{3,2,1,0:T(8,128)(2,1)}, u32[]{:S(2)}, u32[]{:S(2)}) collective-permute-start(bf16[4,2,10,2048]{3,2,1,0:T(8,128)(2,1)S(1)} %bitcast.79), channel_id=1, source_target_pairs={{0,224},{32,0},{64,32},{96,64},{128,96},{160,128},{192,160},{224,1... | collective-permute-start | bytes 983048 | tf_op jit(solution)/shard_map/ppermute | solution.py:111
  253.2 23.8 %collective-permute-start.3 = (bf16[4,2,10,2048]{3,2,1,0:T(8,128)(2,1)S(1)}, bf16[4,2,10,2048]{3,2,1,0:T(8,128)(2,1)S(1)}, u32[]{:S(2)}, u32[]{:S(2)}) collective-permute-start(bf16[4,2,10,2048]{3,2,1,0:T(8,128)(2,1)S(1)} %bitcast.80), channel_id=1, source_target_pairs={{0,32},{32,64},{64,96},{96,128},{128,160},{160,192},{192,224},{224... | collective-permute-start | bytes 983048 | tf_op jit(solution)/shard_map/ppermute | solution.py:108
  258.0 16.2 %all-to-all-start.3 = ((bf16[64,2,216]{2,1,0:T(2,128)(2,1)}), bf16[64,2,216]{2,1,0:T(2,128)(2,1)S(1)}, u32[]{:S(2)}, u32[]{:S(2)}) async-start(bf16[64,2,216]{2,1,0:T(2,128)(2,1)} %reshape.1151), calls=%async_computation.3 | async-start | bytes 131072 | tf_op jit(solution)/shard_map/all_to_all | solution.py:68
  276.6 14.2 %collective-permute-start.1 = (bf16[4,2,10,2048]{3,2,1,0:T(8,128)(2,1)}, bf16[4,2,10,2048]{3,2,1,0:T(8,128)(2,1)S(1)}, u32[]{:S(2)}, u32[]{:S(2)}) collective-permute-start(bf16[4,2,10,2048]{3,2,1,0:T(8,128)(2,1)} %collective-permute-done), channel_id=1, source_target_pairs={{0,224},{32,0},{64,32},{96,64},{128,96},{160,128},{192,160},{224,1... | collective-permute-start | bytes 983048 | tf_op jit(solution)/shard_map/ppermute | solution.py:111
  277.0 15.4 %collective-permute-start.4 = (bf16[4,2,10,2048]{3,2,1,0:T(8,128)(2,1)S(1)}, bf16[4,2,10,2048]{3,2,1,0:T(8,128)(2,1)S(1)}, u32[]{:S(2)}, u32[]{:S(2)}) collective-permute-start(bf16[4,2,10,2048]{3,2,1,0:T(8,128)(2,1)S(1)} %collective-permute-done.3), channel_id=1, source_target_pairs={{0,32},{32,64},{64,96},{96,128},{128,160},{160,192},{192,224},{224... | collective-permute-start | bytes 983048 | tf_op jit(solution)/shard_map/ppermute | solution.py:108
  290.8 15.6 %collective-permute-start.2 = (bf16[4,2,10,2048]{3,2,1,0:T(8,128)(2,1)S(1)}, bf16[4,2,10,2048]{3,2,1,0:T(8,128)(2,1)S(1)}, u32[]{:S(2)}, u32[]{:S(2)}) collective-permute-start(bf16[4,2,10,2048]{3,2,1,0:T(8,128)(2,1)S(1)} %collective-permute-done.1), channel_id=1, source_target_pairs={{0,224},{32,0},{64,32},{96,64},{128,96},{160,128},{192,160},{224,1... | collective-permute-start | bytes 983048 | tf_op jit(solution)/shard_map/ppermute | solution.py:111
  292.4 14.0 %collective-permute-start.5 = (bf16[4,2,10,2048]{3,2,1,0:T(8,128)(2,1)S(1)}, bf16[4,2,10,2048]{3,2,1,0:T(8,128)(2,1)S(1)}, u32[]{:S(2)}, u32[]{:S(2)}) collective-permute-start(bf16[4,2,10,2048]{3,2,1,0:T(8,128)(2,1)S(1)} %collective-permute-done.4), channel_id=1, source_target_pairs={{0,32},{32,64},{64,96},{96,128},{128,160},{160,192},{192,224},{224... | collective-permute-start | bytes 983048 | tf_op jit(solution)/shard_map/ppermute | solution.py:108
  306.4 13.2 %collective-permute-start.6 = (bf16[4,2,10,2048]{3,2,1,0:T(8,128)(2,1)S(1)}, bf16[4,2,10,2048]{3,2,1,0:T(8,128)(2,1)S(1)}, u32[]{:S(2)}, u32[]{:S(2)}) collective-permute-start(bf16[4,2,10,2048]{3,2,1,0:T(8,128)(2,1)S(1)} %collective-permute-done.5), channel_id=1, source_target_pairs={{0,32},{32,64},{64,96},{96,128},{128,160},{160,192},{192,224},{224... | collective-permute-start | bytes 983048 | tf_op jit(solution)/shard_map/ppermute | solution.py:108
  329.4 8.0 %collective-permute-start.7 = (f32[52,1024]{1,0:T(8,128)S(1)}, f32[52,1024]{1,0:T(8,128)S(1)}, u32[]{:S(2)}, u32[]{:S(2)}) collective-permute-start(f32[52,1024]{1,0:T(8,128)S(1)} %pad_maximum_fusion), channel_id=1, source_target_pairs={{0,1},{1,0},{2,3},{3,2},{4,5},{5,4},{6,7},{7,6},{8,9},{9,8},{10,11... | collective-permute-start | bytes 638984 | tf_op jit(solution)/shard_map/ppermute | solution.py:119
  337.4 7.6 %collective-permute-start.8 = (f32[52,1024]{1,0:T(8,128)S(1)}, f32[52,1024]{1,0:T(8,128)S(1)}, u32[]{:S(2)}, u32[]{:S(2)}) collective-permute-start(f32[52,1024]{1,0:T(8,128)S(1)} %fusion.62), channel_id=1, source_target_pairs={{0,2},{1,3},{2,0},{3,1},{4,6},{5,7},{6,4},{7,5},{8,10},{9,11},{10,... | collective-permute-start | bytes 638984 | tf_op jit(solution)/shard_map/ppermute | solution.py:119

commit v12 on v10

--- a/solution.py
+++ b/solution.py
@@ -68,24 +68,31 @@
     gathered = lax.all_gather(gathered, OWNER[1], axis=0)
     ring = ring_gather(gathered, OWNER[0], lax.axis_size(OWNER[0]))
     here = lax.axis_index(OWNER[0])
-    left = jnp.roll(left.reshape((ring.shape[0], -1) + left.shape[1:]), -here, axis=0)
-    left = left.reshape(owners * queries, conv_rows + pool_rows)
-    right = ring[:, :, :, :queries].reshape(owners * queries, payload.shape[1])
+    ring_size = len(ring)
+    left = left.reshape((ring_size, -1) + left.shape[1:])
     stat_rows = stats.shape[0]
-    stat_parts = jnp.roll(ring[:, :, :, queries:], here, axis=0).astype(jnp.float32)
+    stat_parts = jnp.roll(
+        jnp.stack([part[:, :, queries:] for part in ring]), here, axis=0
+    ).astype(jnp.float32)
     stats_sum = jnp.sum(
         stat_parts[:, :, :, :stat_rows] + stat_parts[:, :, :, stat_rows:], axis=(0, 1, 2)
     )
     contract_rows = (((0,), (0,)), ((), ()))
     conv_width = d_conv_b.shape[1]
-    conv_part = lax.dot_general(
-        left[:, :conv_rows], right[:, :conv_width], contract_rows,
-        preferred_element_type=jnp.float32,
-    )
-    pool_part = lax.dot_general(
-        left[:, conv_rows:], right[:, conv_width:], contract_rows,
-        preferred_element_type=jnp.float32,
-    )
+    conv_part = 0.0
+    pool_part = 0.0
+    for step, part in enumerate(ring):
+        block_left = lax.dynamic_index_in_dim(left, (here + step) % ring_size, 0, keepdims=False)
+        block_left = block_left.reshape(-1, conv_rows + pool_rows)
+        block_right = part[:, :, :queries].reshape(-1, payload.shape[1])
+        conv_part = conv_part + lax.dot_general(
+            block_left[:, :conv_rows], block_right[:, :conv_width], contract_rows,
+            preferred_element_type=jnp.float32,
+        )
+        pool_part = pool_part + lax.dot_general(
+            block_left[:, conv_rows:], block_right[:, conv_width:], contract_rows,
+            preferred_element_type=jnp.float32,
+        )
     return pool_part, conv_part, stats_sum
 
 
@@ -98,7 +105,7 @@
         if 2 * step < size:
             backward_part = lax.ppermute(backward_part, axis, [(i, (i - 1) % size) for i in range(size)])
             ahead.append(backward_part)
-    return jnp.stack([block] + ahead + behind[::-1])
+    return [block] + ahead + behind[::-1]
 
 
 def pair_sum(values, groups):

time: 345 us -> 346 us (level)
  local copies, waits for them, and re-layouts: 46.9 us -> 40.9 us
    ppermute x4, waiting for transfers between devices: 25.1 us -> 41.4 us  [ring_gather(): lax.ppermute(forward_part, axis, [(i, (i + 1) % size) for i in range(size)])]
    ppermute x3, waiting for transfers between devices: 10.2 us -> 0.01 us  [ring_gather(): lax.ppermute(backward_part, axis, [(i, (i - 1) % size) for i in range(siz...]
    unnamed x23 -> x43, local copies, waits for them, and re-layouts: 8.14 us -> 5.64 us
  transfers between devices with their start and end apart: 12 -> 12, of which waited for: 8 -> 9; matrix products, arithmetic and copies ran while one was open for 8% -> 7% of each run, Pallas kernels for 0% -> 0%
where the time goes in v12:
time: 346 us; the launch traced here: 345 us
  waiting for transfers between devices  211 us (61%)
  local copies, waits for them, and re-layouts  40.9 us (12%)
  blocking collectives  36.4 us (11%)
  starting transfers between devices  26 us (8%)
  matrix products  22.1 us (6%)
  other arithmetic  6.42 us (2%)
    all_to_all x1, waiting for transfers between devices, local(): lax.all_to_all(table[served[:, capacity:].reshape(-1)].reshape(owners, pa...  114 us
    ppermute x4, waiting for transfers between devices, ring_gather(): lax.ppermute(forward_part, axis, [(i, (i + 1) % size) for i in range(size)])  41.4 us
    all_to_all x1, waiting for transfers between devices, local(): lax.all_to_all(table[served[:, :capacity].reshape(-1)].reshape(owners, ca...  34.4 us
    all_to_all x1, blocking collectives, local(): lax.all_to_all(all_requests, OWNER, split_axis=0, concat_axis=0, tiled=True)  21.5 us
    gather x1, local copies, waits for them, and re-layouts, local(): table[served[:, capacity:].reshape(-1)].reshape(owners, page_cap, width)  16.6 us
    ppermute x2, waiting for transfers between devices, pair_sum(): lax.ppermute(values, 'neg', [(i, i ^ step) for i in range(groups)])  14.9 us
    all_gather x1, blocking collectives, weight_grads(): gathered = lax.all_gather(gathered, OWNER[1], axis=0)  12.9 us
    gather x1, local copies, waits for them, and re-layouts, local(): table[served[:, :capacity].reshape(-1)].reshape(owners, capacity, width)  10.5 us
  transfers between devices with their start and end apart: 12, of which 9 were waited for; matrix products, arithmetic and copies ran while one was open for 7% of the time, Pallas kernels for 0%

profile of v12, /device:TPU:6, one launch (start us, length us, event | category | flops | bytes accessed | tf_op | source)
XLA Modules:
  0.0 345.1 jit_solution(212437680542658945)
XLA Ops:
  0.6 0.9 reshape.980
  4.7 2.0 fusion.3
  7.8 21.5 %all_to_all.27 = s32[64,1,56]{2,1,0:T(1,128)S(1)} all-to-all(s32[64,1,56]{2,1,0:T(1,128)S(1)} %bitcast.151), channel_id=1, replica_groups=mesh['oz'=8,'oy'=4,'oc'=2,'neg'=4] {'oz','oy','oc'}, dimensions={0} | all-to-all | bytes 28672 | tf_op jit(solution)/shard_map/all_to_all | solution.py:159
  29.4 10.5 %gather_fusion.1 = bf16[1024,1024]{1,0:T(8,128)(2,1)} fusion(bf16[4096,1024]{1,0:T(8,128)(2,1)} %param.17, s32[1024]{0:T(1024)S(1)} %broadcast_clamp_fusion), kind=kCustom, calls=%fused_computation.1 | custom fusion | bytes 4198400 | tf_op jit(solution)/shard_map/gather | solution.py:161
  39.9 5.6 %all-to-all-start.2 = ((bf16[64,16,1024]{2,1,0:T(8,128)(2,1)}), bf16[64,16,1024]{2,1,0:T(8,128)(2,1)}, u32[]{:S(2)}, u32[]{:S(2)}) async-start(bf16[64,16,1024]{2,1,0:T(8,128)(2,1)} %bitcast.124), calls=%async_computation.2 | async-start | bytes 4194304 | tf_op jit(solution)/shard_map/all_to_all | solution.py:160
  45.7 16.6 %gather_fusion = bf16[2560,1024]{1,0:T(8,128)(2,1)} fusion(bf16[4096,1024]{1,0:T(8,128)(2,1)} %param.17, s32[3072]{0:T(1024)S(1)} %pad_clamp_fusion), kind=kCustom, calls=%fused_computation | custom fusion | bytes 10496000 | tf_op jit(solution)/shard_map/gather | solution.py:165
  62.3 34.4 %all-to-all-done.2 = bf16[64,16,1024]{2,1,0:T(8,128)(2,1)} async-done(((bf16[64,16,1024]{2,1,0:T(8,128)(2,1)}), bf16[64,16,1024]{2,1,0:T(8,128)(2,1)}, u32[]{:S(2)}, u32[]{:S(2)}) %all-to-all-start.2) | async-done | bytes 2097184 | tf_op jit(solution)/shard_map/all_to_all | solution.py:160
  96.7 6.0 %all-to-all-start.1 = ((bf16[64,40,1024]{2,1,0:T(8,128)(2,1)}), bf16[64,40,1024]{2,1,0:T(8,128)(2,1)}, u32[]{:S(2)}, u32[]{:S(2)}) async-start(bf16[64,40,1024]{2,1,0:T(8,128)(2,1)} %bitcast.123), calls=%async_computation.1 | async-start | bytes 10485760 | tf_op jit(solution)/shard_map/all_to_all | solution.py:164
  103.7 2.5 convolution_convert_fusion.1
  106.8 114.5 %all-to-all-done.1 = bf16[64,40,1024]{2,1,0:T(8,128)(2,1)} async-done(((bf16[64,40,1024]{2,1,0:T(8,128)(2,1)}), bf16[64,40,1024]{2,1,0:T(8,128)(2,1)}, u32[]{:S(2)}, u32[]{:S(2)}) %all-to-all-start.1) | async-done | bytes 5242912 | tf_op jit(solution)/shard_map/all_to_all | solution.py:164
  221.3 3.5 %convolution_convert_fusion = bf16[2,8,1024]{2,1,0:T(8,128)(2,1)S(1)} fusion(bf16[2560,1024,1]{1,0,2:T(8,128)(2,1)} %bitcast.11, s32[2,8]{1,0:T(2,128)S(1)} %pad_add_fusion.1), kind=kOutput, calls=%fused_computation.35 | convolution fusion | flops 83943424 | bytes 5275712 | tf_op jit(solution)/shard_map/aqs,se->aqe/dot_general | solution.py:183
  226.0 4.0 %fusion.90 = f32[8,2560]{1,0:T(8,128)S(1)} fusion(bf16[2560,1024]{1,0:T(8,128)(2,1)} %bitcast.10, f32[8,1024]{1,0:T(8,128)S(1)} %get-tuple-element.25), kind=kOutput, calls=%fused_computation.172 | convolution fusion | flops 41951232 | bytes 5357568 | tf_op jit(solution)/shard_map/dot_general | solution.py:190
  230.0 1.5 select_reduce_fusion.1
  232.2 2.0 select_reduce_fusion
  234.8 3.5 %multiply_reduce_fusion = (f32[8]{0:T(128)S(1)}, f32[8,1024]{1,0:T(8,128)S(1)}) fusion(f32[8,1024]{1,0:T(8,128)S(1)} %get-tuple-element.25, bf16[2,8,1024]{2,1,0:T(8,128)(2,1)S(1)} %convolution_convert_fusion, f32[8]{0:T(128)S(1)} %get-tuple-element.22, bf16[8,2560]{1,0:T(8,128)(2,1)S(1)} %select_reduce_fusion, bf16[2560,1024]{1,0:T(8,128)(2,1)} %bitcast.10), kind=kOutput, calls=%fused_computation.114 | convolution fusion | flops 41983992 | bytes 5365824 | tf_op jit(solution)/shard_map/dot_general | solution.py:205
  239.3 1.9 all-gather.2
  241.2 12.9 %all-gather.1 = bf16[8,12,2048]{2,1,0:T(8,128)(2,1)S(1)} all-gather(bf16[2,12,2048]{2,1,0:T(8,128)(2,1)S(1)} %all-gather.2), channel_id=3, replica_groups=mesh['oz'=8,'oy'=4,'oc'=2,'neg'=4] {'oy'}, dimensions={0}, use_global_device_ids=true | all-gather | bytes 491520 | tf_op jit(solution)/shard_map/all_gather | solution.py:68
  255.3 5.9 %all-to-all-start.3 = ((bf16[64,2,192]{2,1,0:T(2,128)(2,1)}), bf16[64,2,192]{2,1,0:T(2,128)(2,1)}, u32[]{:S(2)}, u32[]{:S(2)}) async-start(bf16[64,2,192]{2,1,0:T(2,128)(2,1)} %reshape.1042), calls=%async_computation.3 | async-start | bytes 131072 | tf_op jit(solution)/shard_map/all_to_all | solution.py:62
  261.9 3.0 collective-permute-start
  264.9 6.2 %all-to-all-done.3 = bf16[64,2,192]{2,1,0:T(2,128)(2,1)} async-done(((bf16[64,2,192]{2,1,0:T(2,128)(2,1)}), bf16[64,2,192]{2,1,0:T(2,128)(2,1)}, u32[]{:S(2)}, u32[]{:S(2)}) %all-to-all-start.3) | async-done | bytes 49184 | tf_op jit(solution)/shard_map/all_to_all | solution.py:62
  271.1 1.0 reshape.1043
  272.6 7.2 %collective-permute-done.3 = bf16[4,2,12,2048]{3,2,1,0:T(8,128)(2,1)S(1)} collective-permute-done((bf16[4,2,12,2048]{3,2,1,0:T(8,128)(2,1)S(1)}, bf16[4,2,12,2048]{3,2,1,0:T(8,128)(2,1)S(1)}, u32[]{:S(2)}, u32[]{:S(2)}) %collective-permute-start.3) | collective-permute-done | bytes 393248 | tf_op jit(solution)/shard_map/ppermute | solution.py:103
  280.2 1.0 slice.302
  282.0 1.7 collective-permute-start.4
  283.7 1.0 fusion.52
  284.7 11.3 %collective-permute-done.4 = bf16[4,2,12,2048]{3,2,1,0:T(8,128)(2,1)S(1)} collective-permute-done((bf16[4,2,12,2048]{3,2,1,0:T(8,128)(2,1)S(1)}, bf16[4,2,12,2048]{3,2,1,0:T(8,128)(2,1)S(1)}, u32[]{:S(2)}, u32[]{:S(2)}) %collective-permute-start.4) | collective-permute-done | bytes 393248 | tf_op jit(solution)/shard_map/ppermute | solution.py:103
  297.0 2.0 collective-permute-start.5
  299.0 11.1 %collective-permute-done.5 = bf16[4,2,12,2048]{3,2,1,0:T(8,128)(2,1)S(1)} collective-permute-done((bf16[4,2,12,2048]{3,2,1,0:T(8,128)(2,1)S(1)}, bf16[4,2,12,2048]{3,2,1,0:T(8,128)(2,1)S(1)}, u32[]{:S(2)}, u32[]{:S(2)}) %collective-permute-start.5) | collective-permute-done | bytes 393248 | tf_op jit(solution)/shard_map/ppermute | solution.py:103
  311.6 11.8 %collective-permute-done.6 = bf16[4,2,12,2048]{3,2,1,0:T(8,128)(2,1)S(1)} collective-permute-done((bf16[4,2,12,2048]{3,2,1,0:T(8,128)(2,1)S(1)}, bf16[4,2,12,2048]{3,2,1,0:T(8,128)(2,1)S(1)}, u32[]{:S(2)}, u32[]{:S(2)}) %collective-permute-start.6) | collective-permute-done | bytes 393248 | tf_op jit(solution)/shard_map/ppermute | solution.py:103
  323.7 1.0 fusion.53
  327.6 7.4 %collective-permute-done.7 = f32[52,1024]{1,0:T(8,128)S(1)} collective-permute-done((f32[52,1024]{1,0:T(8,128)S(1)}, f32[52,1024]{1,0:T(8,128)S(1)}, u32[]{:S(2)}, u32[]{:S(2)}) %collective-permute-start.7) | collective-permute-done | bytes 213024 | tf_op jit(solution)/shard_map/ppermute | solution.py:114
  335.1 7.5 %collective-permute-done.8 = f32[52,1024]{1,0:T(8,128)S(1)} collective-permute-done((f32[52,1024]{1,0:T(8,128)S(1)}, f32[52,1024]{1,0:T(8,128)S(1)}, u32[]{:S(2)}, u32[]{:S(2)}) %collective-permute-start.8) | collective-permute-done | bytes 213024 | tf_op jit(solution)/shard_map/ppermute | solution.py:114
  (139 shorter events, 20.3 us)
Async XLA Ops:
  0.6 105.8 %copy-start = (bf16[1024,1024]{1,0:T(8,128)(2,1)S(1)}, bf16[1024,1024]{1,0:T(8,128)(2,1)}, u32[]{:S(2)}) copy-start(bf16[1024,1024]{1,0:T(8,128)(2,1)} %param.18) | copy-start | bytes 6291460
  39.9 56.7 %all-to-all-start.2 = ((bf16[64,16,1024]{2,1,0:T(8,128)(2,1)}), bf16[64,16,1024]{2,1,0:T(8,128)(2,1)}, u32[]{:S(2)}, u32[]{:S(2)}) async-start(bf16[64,16,1024]{2,1,0:T(8,128)(2,1)} %bitcast.124), calls=%async_computation.2 | async-start | bytes 4194304 | tf_op jit(solution)/shard_map/all_to_all | solution.py:160
  96.7 6.1 %copy-start.10 = (s32[8,50]{1,0:T(8,128)S(1)}, s32[8,50]{1,0:T(8,128)}, u32[]{:S(2)}) copy-start(s32[8,50]{1,0:T(8,128)} %param.13) | copy-start | bytes 4804
  96.7 6.5 %copy-start.9 = (s32[8,50]{1,0:T(8,128)S(1)}, s32[8,50]{1,0:T(8,128)}, u32[]{:S(2)}) copy-start(s32[8,50]{1,0:T(8,128)} %param.12) | copy-start | bytes 4804
  96.7 124.6 %all-to-all-start.1 = ((bf16[64,40,1024]{2,1,0:T(8,128)(2,1)}), bf16[64,40,1024]{2,1,0:T(8,128)(2,1)}, u32[]{:S(2)}, u32[]{:S(2)}) async-start(bf16[64,40,1024]{2,1,0:T(8,128)(2,1)} %bitcast.123), calls=%async_computation.1 | async-start | bytes 10485760 | tf_op jit(solution)/shard_map/all_to_all | solution.py:164
  102.7 3.7 %copy-start.11 = (f32[1024]{0:T(1024)S(1)}, f32[1024]{0:T(1024)}, u32[]{:S(2)}) copy-start(f32[1024]{0:T(1024)} %param.19) | copy-start | bytes 12292
  221.3 3.7 %copy-start.1 = (bf16[2048,1024]{1,0:T(8,128)(2,1)S(1)}, bf16[2048,1024]{1,0:T(8,128)(2,1)}, u32[]{:S(2)}) copy-start(bf16[2048,1024]{1,0:T(8,128)(2,1)} %param.20) | copy-start | bytes 12582916
  221.3 3.7 %copy-start.12 = (f32[1024]{0:T(1024)S(1)}, f32[1024]{0:T(1024)}, u32[]{:S(2)}) copy-start(f32[1024]{0:T(1024)} %param.21) | copy-start | bytes 12292
  226.0 12.3 %copy-start.4 = (f32[8,1024]{1,0:T(8,128)}, f32[8,1024]{1,0:T(8,128)S(1)}, u32[]{:S(2)}) copy-start(f32[8,1024]{1,0:T(8,128)S(1)} %get-tuple-element.25) | copy-start | bytes 98308
  234.8 3.7 %copy-start.2 = (bf16[2048,1024]{1,0:T(8,128)(2,1)S(1)}, bf16[2048,1024]{1,0:T(8,128)(2,1)}, u32[]{:S(2)}) copy-start(bf16[2048,1024]{1,0:T(8,128)(2,1)} %param.20) | copy-start | bytes 12582916
  255.3 15.8 %all-to-all-start.3 = ((bf16[64,2,192]{2,1,0:T(2,128)(2,1)}), bf16[64,2,192]{2,1,0:T(2,128)(2,1)}, u32[]{:S(2)}, u32[]{:S(2)}) async-start(bf16[64,2,192]{2,1,0:T(2,128)(2,1)} %reshape.1042), calls=%async_computation.3 | async-start | bytes 131072 | tf_op jit(solution)/shard_map/all_to_all | solution.py:62
  261.9 18.3 %collective-permute-start = (bf16[4,2,12,2048]{3,2,1,0:T(8,128)(2,1)S(1)}, bf16[4,2,12,2048]{3,2,1,0:T(8,128)(2,1)}, u32[]{:S(2)}, u32[]{:S(2)}) collective-permute-start(bf16[4,2,12,2048]{3,2,1,0:T(8,128)(2,1)S(1)} %bitcast.126), channel_id=1, source_target_pairs={{0,224},{32,0},{64,32},{96,64},{128,96},{160,128},{192,160},{224,1... | collective-permute-start | bytes 1179656 | tf_op jit(solution)/shard_map/ppermute | solution.py:106
  264.9 14.9 %collective-permute-start.3 = (bf16[4,2,12,2048]{3,2,1,0:T(8,128)(2,1)S(1)}, bf16[4,2,12,2048]{3,2,1,0:T(8,128)(2,1)S(1)}, u32[]{:S(2)}, u32[]{:S(2)}) collective-permute-start(bf16[4,2,12,2048]{3,2,1,0:T(8,128)(2,1)S(1)} %bitcast.127), channel_id=1, source_target_pairs={{0,32},{32,64},{64,96},{96,128},{128,160},{160,192},{192,224},{224... | collective-permute-start | bytes 1179656 | tf_op jit(solution)/shard_map/ppermute | solution.py:103
  272.1 11.6 %copy-start.3 = (bf16[16,4,2,4,2048]{4,3,2,1,0:T(4,128)(2,1)S(1)}, bf16[16,4,2,4,2048]{4,3,2,1,0:T(4,128)(2,1)}, u32[]{:S(2)}) copy-start(bf16[16,4,2,4,2048]{4,3,2,1,0:T(4,128)(2,1)} %fusion.50) | copy-start | bytes 6291460
  279.8 16.2 %copy-start.5 = (bf16[4,2,12,2048]{3,2,1,0:T(8,128)(2,1)}, bf16[4,2,12,2048]{3,2,1,0:T(8,128)(2,1)S(1)}, u32[]{:S(2)}) copy-start(bf16[4,2,12,2048]{3,2,1,0:T(8,128)(2,1)S(1)} %collective-permute-done.3) | copy-start | bytes 1179652
  281.7 14.8 %collective-permute-start.1 = (bf16[4,2,12,2048]{3,2,1,0:T(8,128)(2,1)}, bf16[4,2,12,2048]{3,2,1,0:T(8,128)(2,1)S(1)}, u32[]{:S(2)}, u32[]{:S(2)}) collective-permute-start(bf16[4,2,12,2048]{3,2,1,0:T(8,128)(2,1)} %collective-permute-done), channel_id=1, source_target_pairs={{0,224},{32,0},{64,32},{96,64},{128,96},{160,128},{192,160},{224,1... | collective-permute-start | bytes 1179656 | tf_op jit(solution)/shard_map/ppermute | solution.py:106
  282.0 14.0 %collective-permute-start.4 = (bf16[4,2,12,2048]{3,2,1,0:T(8,128)(2,1)S(1)}, bf16[4,2,12,2048]{3,2,1,0:T(8,128)(2,1)S(1)}, u32[]{:S(2)}, u32[]{:S(2)}) collective-permute-start(bf16[4,2,12,2048]{3,2,1,0:T(8,128)(2,1)S(1)} %collective-permute-done.3), channel_id=1, source_target_pairs={{0,32},{32,64},{64,96},{96,128},{128,160},{160,192},{192,224},{224... | collective-permute-start | bytes 1179656 | tf_op jit(solution)/shard_map/ppermute | solution.py:103
  296.5 27.1 %copy-start.6 = (bf16[4,2,12,2048]{3,2,1,0:T(8,128)(2,1)S(1)}, bf16[4,2,12,2048]{3,2,1,0:T(8,128)(2,1)}, u32[]{:S(2)}) copy-start(bf16[4,2,12,2048]{3,2,1,0:T(8,128)(2,1)} %copy-done.5) | copy-start | bytes 1179652
  296.9 13.7 %collective-permute-start.2 = (bf16[4,2,12,2048]{3,2,1,0:T(8,128)(2,1)S(1)}, bf16[4,2,12,2048]{3,2,1,0:T(8,128)(2,1)S(1)}, u32[]{:S(2)}, u32[]{:S(2)}) collective-permute-start(bf16[4,2,12,2048]{3,2,1,0:T(8,128)(2,1)S(1)} %collective-permute-done.1), channel_id=1, source_target_pairs={{0,224},{32,0},{64,32},{96,64},{128,96},{160,128},{192,160},{224,1... | collective-permute-start | bytes 1179656 | tf_op jit(solution)/shard_map/ppermute | solution.py:106
  297.0 13.2 %collective-permute-start.5 = (bf16[4,2,12,2048]{3,2,1,0:T(8,128)(2,1)S(1)}, bf16[4,2,12,2048]{3,2,1,0:T(8,128)(2,1)S(1)}, u32[]{:S(2)}, u32[]{:S(2)}) collective-permute-start(bf16[4,2,12,2048]{3,2,1,0:T(8,128)(2,1)S(1)} %collective-permute-done.4), channel_id=1, source_target_pairs={{0,32},{32,64},{64,96},{96,128},{128,160},{160,192},{192,224},{224... | collective-permute-start | bytes 1179656 | tf_op jit(solution)/shard_map/ppermute | solution.py:103
  311.1 12.3 %collective-permute-start.6 = (bf16[4,2,12,2048]{3,2,1,0:T(8,128)(2,1)S(1)}, bf16[4,2,12,2048]{3,2,1,0:T(8,128)(2,1)S(1)}, u32[]{:S(2)}, u32[]{:S(2)}) collective-permute-start(bf16[4,2,12,2048]{3,2,1,0:T(8,128)(2,1)S(1)} %collective-permute-done.5), channel_id=1, source_target_pairs={{0,32},{32,64},{64,96},{96,128},{128,160},{160,192},{192,224},{224... | collective-permute-start | bytes 1179656 | tf_op jit(solution)/shard_map/ppermute | solution.py:103
  323.4 1.7 copy-start.7
  325.2 1.0 copy-start.8
  326.7 8.3 %collective-permute-start.7 = (f32[52,1024]{1,0:T(8,128)S(1)}, f32[52,1024]{1,0:T(8,128)S(1)}, u32[]{:S(2)}, u32[]{:S(2)}) collective-permute-start(f32[52,1024]{1,0:T(8,128)S(1)} %pad_maximum_fusion), channel_id=1, source_target_pairs={{0,1},{1,0},{2,3},{3,2},{4,5},{5,4},{6,7},{7,6},{8,9},{9,8},{10,11... | collective-permute-start | bytes 638984 | tf_op jit(solution)/shard_map/ppermute | solution.py:114
  335.0 7.6 %collective-permute-start.8 = (f32[52,1024]{1,0:T(8,128)S(1)}, f32[52,1024]{1,0:T(8,128)S(1)}, u32[]{:S(2)}, u32[]{:S(2)}) collective-permute-start(f32[52,1024]{1,0:T(8,128)S(1)} %fusion.115), channel_id=1, source_target_pairs={{0,2},{1,3},{2,0},{3,1},{4,6},{5,7},{6,4},{7,5},{8,10},{9,11},{10,... | collective-permute-start | bytes 638984 | tf_op jit(solution)/shard_map/ppermute | solution.py:114
